TPU v7x, 1024 devices: a whole 8x8x8 slice. The times are simulated.
1024 devices in a mesh: seq: 16 (over z, x_lo), head: 64 (over y, x_hi, core).
Axes of the slice: x: 8 (x_hi: 4, x_lo: 2; x = x_hi * 2 + x_lo), y: 8, z: 8, core: 2. Of those that a mesh axis runs over, the one named last changes fastest.
Arguments:
- queries: bfloat16 [4096, 8192], P('seq', 'head'), may hold values from -41 to 41
- keys: bfloat16 [16, 1600, 8, 128], P('seq', 'head'), may hold values from -4 to 4
- values: bfloat16 [16, 1600, 8, 128], P('seq', 'head'), may hold values from -6 to 6
- cotangent: bfloat16 [4096, 8192], P('seq', 'head'), may hold values from -6 to 6
- mask: int32 [4096, 2], P('seq'), may hold values from 0 to 1, as said below
Outputs:
- attended: bfloat16 [4096, 8192], P('seq', 'head')
- grad_query: bfloat16 [4096, 8192], P('seq', 'head')
- grad_keys: bfloat16 [16, 1600, 8, 128], P('seq', 'head')
- grad_values: bfloat16 [16, 1600, 8, 128], P('seq', 'head')
Inputs may be any that keep to these rules, and one draw needn't show every extreme that they name: mask[t, 0] is 1 where token t attends to the image of its own block of 256 tokens, mask[t, 1] where it attends to the image of the block before. Within each block the ones of column 0 form a suffix that covers at least the block's second half, the ones of column 1 a prefix that holds the block's first token and at most its first 128 tokens, exactly that many in block 1; column 1 is all 0 on the first block.
All inputs are finite; a program needn't handle non-finite values.
Results may differ from a plain program's by a relative error of at most 0.038.
Values may be sent and summed in bfloat16 or wider, within the bound.
No kernel may reach another device: no remote copies, remote signals or barrier semaphores. Data moves between devices by JAX's collectives and lax.ppermute only.
A program may use at most 32 MiB of HBM per device.

v0:
```python
import jax
import jax.numpy as jnp
from jax import lax
from jax.sharding import PartitionSpec as P

KVH = 8
HD = 128


NEGATIVE = -1e30


def passed_along(value, axis, by):
    length = lax.axis_size(axis)
    pairs = [(i, i + by) for i in range(length) if 0 <= i + by < length]
    return lax.ppermute(value, axis, pairs)


def spread_heads(shard, copies):
    return jnp.repeat(jnp.transpose(shard, (1, 0, 2)), copies, axis=0)


def block_forward(query_rows, key_rows, value_rows, keep_mask):
    scores = jnp.einsum(
        "rd,kd->rk", query_rows, key_rows, preferred_element_type=jnp.float32
    ) * HD ** (-0.5)
    scores = jnp.where(keep_mask[:, None] > 0, scores, NEGATIVE)
    highest = jnp.max(scores, axis=1)
    powered = jnp.exp(scores - highest[:, None])
    totals = jnp.sum(powered, axis=1)
    partial_value = jnp.dot(
        powered.astype(jnp.bfloat16), value_rows, preferred_element_type=jnp.float32
    )
    return (scores, highest, totals, partial_value)


def finish_backward(weights, grad_rows, row_delta, query_rows, key_rows, value_rows):
    grad_weights = jnp.einsum(
        "rd,kd->rk", grad_rows, value_rows, preferred_element_type=jnp.float32
    )
    grad_scores = (weights * (grad_weights - row_delta[:, None]) * HD ** (-0.5)).astype(
        jnp.bfloat16
    )
    query_grad = jnp.dot(grad_scores, key_rows, preferred_element_type=jnp.float32)
    key_part = jnp.einsum(
        "rk,rd->kd", grad_scores, query_rows, preferred_element_type=jnp.float32
    ).astype(jnp.bfloat16)
    value_part = jnp.einsum(
        "rk,rd->kd", weights.astype(jnp.bfloat16), grad_rows, preferred_element_type=jnp.float32
    ).astype(jnp.bfloat16)
    return (query_grad, key_part, value_part)


def block_backward(
    scores, highest, totals, live_rows, grad_rows, row_delta, query_rows, key_rows, value_rows
):
    weights = live_rows[:, None] * jnp.exp(scores - highest[:, None]) / totals[:, None]
    return finish_backward(weights, grad_rows, row_delta, query_rows, key_rows, value_rows)


def group_sum(received, groups):
    slot_count, row_count, feature = received.shape
    summed = (
        received.astype(jnp.float32)
        .reshape(groups, slot_count // groups, row_count, feature)
        .sum(axis=1)
    )
    return jnp.transpose(summed, (1, 0, 2))


def per_device(queries, keys, values, cotangent, mask):
    head_devices = lax.axis_size("head")
    copies = head_devices // KVH
    head_count = queries.shape[1] // HD
    vision_rows = keys.shape[1]
    keep_own = jnp.repeat(mask[:, 0], head_count)
    keep_prev = jnp.repeat(mask[:, 1], head_count)
    live_rows = (keep_own + keep_prev > 0).astype(jnp.float32)
    key_own, value_own = (
        lax.all_to_all(
            spread_heads(keys[0], copies), "head", split_axis=0, concat_axis=1, tiled=True
        ),
        lax.all_to_all(
            spread_heads(values[0], copies), "head", split_axis=0, concat_axis=1, tiled=True
        ),
    )
    key_own = key_own[0]
    value_own = value_own[0]
    key_prev, value_prev = passed_along((key_own, value_own), "seq", 1)
    score_own, peak_own, total_own, partial_own = block_forward(
        queries, key_own, value_own, keep_own
    )
    score_prev, peak_prev, total_prev, partial_prev = block_forward(
        queries, key_prev, value_prev, keep_prev
    )
    highest = jnp.maximum(peak_own, peak_prev)
    scale_own = jnp.exp(peak_own - highest)
    scale_prev = jnp.exp(peak_prev - highest)
    totals = scale_own * total_own + scale_prev * total_prev
    attended = (
        live_rows[:, None]
        * (scale_own[:, None] * partial_own + scale_prev[:, None] * partial_prev)
        / totals[:, None]
    ).astype(jnp.bfloat16)
    row_delta = jnp.sum(cotangent.astype(jnp.float32) * attended.astype(jnp.float32), axis=1)
    gq_own, gk_own, gv_own = block_backward(
        score_own, highest, totals, live_rows, cotangent, row_delta, queries, key_own, value_own
    )
    gq_prev, gk_prev, gv_prev = block_backward(
        score_prev, highest, totals, live_rows, cotangent, row_delta, queries, key_prev, value_prev
    )
    grad_query = (gq_own + gq_prev).astype(jnp.bfloat16)
    second_key, second_value = passed_along((gk_prev, gv_prev), "seq", -1)
    returned = (
        lax.all_to_all(
            gk_own.reshape(head_devices, vision_rows, HD),
            "head",
            split_axis=0,
            concat_axis=0,
            tiled=True,
        ),
        lax.all_to_all(
            gv_own.reshape(head_devices, vision_rows, HD),
            "head",
            split_axis=0,
            concat_axis=0,
            tiled=True,
        ),
        lax.all_to_all(
            second_key.reshape(head_devices, vision_rows, HD),
            "head",
            split_axis=0,
            concat_axis=0,
            tiled=True,
        ),
        lax.all_to_all(
            second_value.reshape(head_devices, vision_rows, HD),
            "head",
            split_axis=0,
            concat_axis=0,
            tiled=True,
        ),
    )
    key_sum = group_sum(returned[0], KVH)
    value_sum = group_sum(returned[1], KVH)
    second_key_sum = group_sum(returned[2], KVH)
    second_value_sum = group_sum(returned[3], KVH)
    grad_keys = key_sum + second_key_sum
    grad_values = value_sum + second_value_sum
    return (
        attended,
        grad_query,
        grad_keys.astype(jnp.bfloat16)[None],
        grad_values.astype(jnp.bfloat16)[None],
    )


def solution(mesh):
    return jax.shard_map(
        per_device,
        mesh=mesh,
        in_specs=(
            P("seq", "head"),
            P("seq", "head", None, None),
            P("seq", "head", None, None),
            P("seq", "head"),
            P("seq", None),
        ),
        out_specs=(
            P("seq", "head"),
            P("seq", "head"),
            P("seq", "head", None, None),
            P("seq", "head", None, None),
        ),
        check_vma=False,
    )
```

profile of v0, /device:TPU:386, one launch (start us, length us, event | category | flops | bytes accessed | tf_op | source)
XLA Modules:
  0.0 215.2 jit_solution(15781640073644150134)
XLA Ops:
  0.7 0.9 copy.18
  1.5 0.9 broadcast_in_dim.54
  2.4 12.6 %all-to-all-start.1 = ((bf16[64,25,128]{2,1,0:T(8,128)(2,1)}), bf16[64,25,128]{2,1,0:T(8,128)(2,1)S(1)}, u32[]{:S(2)}, u32[]{:S(2)}) async-start(bf16[64,25,128]{2,1,0:T(8,128)(2,1)} %bitcast.6), calls=%async_computation.1 | async-start | bytes 1048576 | tf_op jit(solution)/shard_map/all_to_all | solution.py:83
  15.0 18.7 %all-to-all-done.1 = bf16[64,25,128]{2,1,0:T(8,128)(2,1)S(1)} async-done(((bf16[64,25,128]{2,1,0:T(8,128)(2,1)}), bf16[64,25,128]{2,1,0:T(8,128)(2,1)S(1)}, u32[]{:S(2)}, u32[]{:S(2)}) %all-to-all-start.1) | async-done | bytes 409632 | tf_op jit(solution)/shard_map/all_to_all | solution.py:83
  33.7 0.9 broadcast_in_dim.50
  34.6 6.7 %all-to-all-start = ((bf16[64,25,128]{2,1,0:T(8,128)(2,1)}), bf16[64,25,128]{2,1,0:T(8,128)(2,1)S(1)}, u32[]{:S(2)}, u32[]{:S(2)}) async-start(bf16[64,25,128]{2,1,0:T(8,128)(2,1)} %bitcast.3), calls=%async_computation | async-start | bytes 1048576 | tf_op jit(solution)/shard_map/all_to_all | solution.py:80
  41.4 0.1 copy.19
  41.5 0.9 squeeze.15
  42.4 8.2 %collective-permute-start.1 = (bf16[1600,128]{1,0:T(8,128)(2,1)}, bf16[1600,128]{1,0:T(8,128)(2,1)}, u32[]{:S(2)}, u32[]{:S(2)}) collective-permute-start(bf16[1600,128]{1,0:T(8,128)(2,1)} %squeeze.15), channel_id=1, source_target_pairs={{0,64},{64,128},{128,192},{192,256},{256,320},{320,384},{384,448},... | collective-permute-start | bytes 1228808 | tf_op jit(solution)/shard_map/ppermute | solution.py:16
  50.6 9.0 %all-to-all-done = bf16[64,25,128]{2,1,0:T(8,128)(2,1)S(1)} async-done(((bf16[64,25,128]{2,1,0:T(8,128)(2,1)}), bf16[64,25,128]{2,1,0:T(8,128)(2,1)S(1)}, u32[]{:S(2)}, u32[]{:S(2)}) %all-to-all-start) | async-done | bytes 409632 | tf_op jit(solution)/shard_map/all_to_all | solution.py:80
  59.7 0.1 squeeze.13
  59.8 10.0 %collective-permute-start = (bf16[1600,128]{1,0:T(8,128)(2,1)S(1)}, bf16[1600,128]{1,0:T(8,128)(2,1)S(1)}, u32[]{:S(2)}, u32[]{:S(2)}) collective-permute-start(bf16[1600,128]{1,0:T(8,128)(2,1)S(1)} %squeeze.13), channel_id=1, source_target_pairs={{0,64},{64,128},{128,192},{192,256},{256,320},{320,384},{384,448},... | collective-permute-start | bytes 1228808 | tf_op jit(solution)/shard_map/ppermute | solution.py:16
  69.9 0.4 fusion.23
  70.4 0.3 fusion.8
  70.7 8.3 %collective-permute-done = bf16[1600,128]{1,0:T(8,128)(2,1)S(1)} collective-permute-done((bf16[1600,128]{1,0:T(8,128)(2,1)S(1)}, bf16[1600,128]{1,0:T(8,128)(2,1)S(1)}, u32[]{:S(2)}, u32[]{:S(2)}) %collective-permute-start) | collective-permute-done | bytes 409632 | tf_op jit(solution)/shard_map/ppermute | solution.py:16
  79.0 0.4 fusion.22
  79.4 0.3 fusion.10
  79.8 1.4 convolution_multiply_fusion.2
  81.2 1.5 multiply_reduce_fusion
  82.7 1.6 fusion.6
  84.3 0.9 copy-done.3
  85.2 1.1 convolution_convert_fusion.3
  86.4 1.9 reshape.91
  88.3 5.5 %all-to-all-start.2 = ((bf16[64,25,128]{2,1,0:T(8,128)(2,1)}), bf16[64,25,128]{2,1,0:T(8,128)(2,1)}, u32[]{:S(2)}, u32[]{:S(2)}) async-start(bf16[64,25,128]{2,1,0:T(8,128)(2,1)} %reshape.91), calls=%async_computation.2 | async-start | bytes 1048576 | tf_op jit(solution)/shard_map/all_to_all | solution.py:115
  93.8 1.2 convolution_convert_fusion.1
  95.0 2.0 reshape.97
  97.0 17.4 %all-to-all-done.2 = bf16[64,25,128]{2,1,0:T(8,128)(2,1)} async-done(((bf16[64,25,128]{2,1,0:T(8,128)(2,1)}), bf16[64,25,128]{2,1,0:T(8,128)(2,1)}, u32[]{:S(2)}, u32[]{:S(2)}) %all-to-all-start.2) | async-done | bytes 409632 | tf_op jit(solution)/shard_map/all_to_all | solution.py:115
  114.3 5.0 %all-to-all-start.4 = ((bf16[64,25,128]{2,1,0:T(8,128)(2,1)}), bf16[64,25,128]{2,1,0:T(8,128)(2,1)S(1)}, u32[]{:S(2)}, u32[]{:S(2)}) async-start(bf16[64,25,128]{2,1,0:T(8,128)(2,1)} %reshape.97), calls=%async_computation.4 | async-start | bytes 1048576 | tf_op jit(solution)/shard_map/all_to_all | solution.py:122
  119.3 1.6 fusion.7
  120.9 0.4 convolution_convert_fusion.2
  121.3 1.9 collective-permute-start.2
  123.2 21.2 %collective-permute-done.2 = bf16[1600,128]{1,0:T(8,128)(2,1)S(1)} collective-permute-done((bf16[1600,128]{1,0:T(8,128)(2,1)S(1)}, bf16[1600,128]{1,0:T(8,128)(2,1)S(1)}, u32[]{:S(2)}, u32[]{:S(2)}) %collective-permute-start.2) | collective-permute-done | bytes 409632 | tf_op jit(solution)/shard_map/ppermute | solution.py:16
  144.4 0.9 reshape.94
  145.4 0.8 copy-done.7
  146.2 13.0 %all-to-all-start.3 = ((bf16[64,25,128]{2,1,0:T(8,128)(2,1)}), bf16[64,25,128]{2,1,0:T(8,128)(2,1)}, u32[]{:S(2)}, u32[]{:S(2)}) async-start(bf16[64,25,128]{2,1,0:T(8,128)(2,1)} %reshape.94), calls=%async_computation.3 | async-start | bytes 1048576 | tf_op jit(solution)/shard_map/all_to_all | solution.py:129
  159.2 2.1 convolution_convert_fusion
  161.4 1.9 collective-permute-start.3
  163.3 0.7 copy.20
  164.0 0.4 fusion.24
  164.5 16.1 %collective-permute-done.3 = bf16[1600,128]{1,0:T(8,128)(2,1)S(1)} collective-permute-done((bf16[1600,128]{1,0:T(8,128)(2,1)}, bf16[1600,128]{1,0:T(8,128)(2,1)S(1)}, u32[]{:S(2)}, u32[]{:S(2)}) %collective-permute-start.3) | collective-permute-done | bytes 409632 | tf_op jit(solution)/shard_map/ppermute | solution.py:16
  180.6 0.9 reshape.100
  181.6 12.6 %all-to-all-start.5 = ((bf16[64,25,128]{2,1,0:T(8,128)(2,1)}), bf16[64,25,128]{2,1,0:T(8,128)(2,1)S(1)}, u32[]{:S(2)}, u32[]{:S(2)}) async-start(bf16[64,25,128]{2,1,0:T(8,128)(2,1)} %reshape.100), calls=%async_computation.5 | async-start | bytes 1048576 | tf_op jit(solution)/shard_map/all_to_all | solution.py:136
  194.2 1.1 fusion.12
  195.3 1.1 convert_reduce_fusion.3
  196.5 1.1 convert_reduce_fusion.2
  197.7 0.6 copy.21
  198.3 16.2 %all-to-all-done.5 = bf16[64,25,128]{2,1,0:T(8,128)(2,1)S(1)} async-done(((bf16[64,25,128]{2,1,0:T(8,128)(2,1)}), bf16[64,25,128]{2,1,0:T(8,128)(2,1)S(1)}, u32[]{:S(2)}, u32[]{:S(2)}) %all-to-all-start.5) | async-done | bytes 409632 | tf_op jit(solution)/shard_map/all_to_all | solution.py:136
  214.6 0.6 copy.22
  (40 shorter events, 0.3 us)
Async XLA Ops:
  0.6 69.3 %copy-start = (bf16[256,128]{1,0:T(8,128)(2,1)S(1)}, bf16[256,128]{1,0:T(8,128)(2,1)}, u32[]{:S(2)}) copy-start(bf16[256,128]{1,0:T(8,128)(2,1)} %param.5) | copy-start | bytes 196612
  0.6 14.4 %copy-start.14 = (bf16[1,25,8,128]{3,2,1,0:T(8,128)(2,1)S(1)}, bf16[1,25,8,128]{3,2,1,0:T(8,128)(2,1)}, u32[]{:S(2)}) copy-start(bf16[1,25,8,128]{3,2,1,0:T(8,128)(2,1)} %param.6) | copy-start | bytes 153604
  1.5 39.8 %copy-start.11 = (bf16[256,128]{1,0:T(8,128)(2,1)S(1)}, bf16[256,128]{1,0:T(8,128)(2,1)}, u32[]{:S(2)}) copy-start(bf16[256,128]{1,0:T(8,128)(2,1)} %param.8) | copy-start | bytes 196612
  1.5 39.9 %copy-start.15 = (s32[256,2]{0,1:T(2,128)S(1)}, s32[256,2]{0,1:T(2,128)}, u32[]{:S(2)}) copy-start(s32[256,2]{0,1:T(2,128)} %param.9) | copy-start | bytes 6148
  2.4 31.3 %all-to-all-start.1 = ((bf16[64,25,128]{2,1,0:T(8,128)(2,1)}), bf16[64,25,128]{2,1,0:T(8,128)(2,1)S(1)}, u32[]{:S(2)}, u32[]{:S(2)}) async-start(bf16[64,25,128]{2,1,0:T(8,128)(2,1)} %bitcast.6), calls=%async_computation.1 | async-start | bytes 1048576 | tf_op jit(solution)/shard_map/all_to_all | solution.py:83
  34.6 25.1 %all-to-all-start = ((bf16[64,25,128]{2,1,0:T(8,128)(2,1)}), bf16[64,25,128]{2,1,0:T(8,128)(2,1)S(1)}, u32[]{:S(2)}, u32[]{:S(2)}) async-start(bf16[64,25,128]{2,1,0:T(8,128)(2,1)} %bitcast.3), calls=%async_computation | async-start | bytes 1048576 | tf_op jit(solution)/shard_map/all_to_all | solution.py:80
  42.4 38.8 %collective-permute-start.1 = (bf16[1600,128]{1,0:T(8,128)(2,1)}, bf16[1600,128]{1,0:T(8,128)(2,1)}, u32[]{:S(2)}, u32[]{:S(2)}) collective-permute-start(bf16[1600,128]{1,0:T(8,128)(2,1)} %squeeze.15), channel_id=1, source_target_pairs={{0,64},{64,128},{128,192},{192,256},{256,320},{320,384},{384,448},... | collective-permute-start | bytes 1228808 | tf_op jit(solution)/shard_map/ppermute | solution.py:16
  59.8 10.8 %copy-start.1 = (bf16[1600,128]{1,0:T(8,128)(2,1)}, bf16[1600,128]{1,0:T(8,128)(2,1)S(1)}, u32[]{:S(2)}) copy-start(bf16[1600,128]{1,0:T(8,128)(2,1)S(1)} %squeeze.13) | copy-start | bytes 1228804
  59.8 19.1 %collective-permute-start = (bf16[1600,128]{1,0:T(8,128)(2,1)S(1)}, bf16[1600,128]{1,0:T(8,128)(2,1)S(1)}, u32[]{:S(2)}, u32[]{:S(2)}) collective-permute-start(bf16[1600,128]{1,0:T(8,128)(2,1)S(1)} %squeeze.13), channel_id=1, source_target_pairs={{0,64},{64,128},{128,192},{192,256},{256,320},{320,384},{384,448},... | collective-permute-start | bytes 1228808 | tf_op jit(solution)/shard_map/ppermute | solution.py:16
  79.0 0.8 copy-start.9
  81.2 1.5 copy-start.12
  84.3 0.9 copy-start.3
  85.2 8.6 %copy-start.13 = (bf16[256,128]{1,0:T(8,128)(2,1)S(1)}, bf16[256,128]{1,0:T(8,128)(2,1)}, u32[]{:S(2)}) copy-start(bf16[256,128]{1,0:T(8,128)(2,1)} %param.8) | copy-start | bytes 196612
  88.3 26.0 %all-to-all-start.2 = ((bf16[64,25,128]{2,1,0:T(8,128)(2,1)}), bf16[64,25,128]{2,1,0:T(8,128)(2,1)}, u32[]{:S(2)}, u32[]{:S(2)}) async-start(bf16[64,25,128]{2,1,0:T(8,128)(2,1)} %reshape.91), calls=%async_computation.2 | async-start | bytes 1048576 | tf_op jit(solution)/shard_map/all_to_all | solution.py:115
  114.3 31.1 %all-to-all-start.4 = ((bf16[64,25,128]{2,1,0:T(8,128)(2,1)}), bf16[64,25,128]{2,1,0:T(8,128)(2,1)S(1)}, u32[]{:S(2)}, u32[]{:S(2)}) async-start(bf16[64,25,128]{2,1,0:T(8,128)(2,1)} %reshape.97), calls=%async_computation.4 | async-start | bytes 1048576 | tf_op jit(solution)/shard_map/all_to_all | solution.py:122
  120.9 24.5 %copy-start.5 = (bf16[256,1600]{0,1:T(8,128)(2,1)}, bf16[256,1600]{0,1:T(8,128)(2,1)S(1)}, u32[]{:S(2)}) copy-start(bf16[256,1600]{0,1:T(8,128)(2,1)S(1)} %fusion.7) | copy-start | bytes 2457604
  121.3 23.1 %collective-permute-start.2 = (bf16[1600,128]{1,0:T(8,128)(2,1)S(1)}, bf16[1600,128]{1,0:T(8,128)(2,1)S(1)}, u32[]{:S(2)}, u32[]{:S(2)}) collective-permute-start(bf16[1600,128]{1,0:T(8,128)(2,1)S(1)} %convolution_convert_fusion.2), channel_id=1, source_target_pairs={{64,0},{128,64},{192,128},{256,192},{320,256},{384,320},{448,384},... | collective-permute-start | bytes 1228808 | tf_op jit(solution)/shard_map/ppermute | solution.py:16
  145.4 0.8 copy-start.7
  146.2 35.4 %all-to-all-start.3 = ((bf16[64,25,128]{2,1,0:T(8,128)(2,1)}), bf16[64,25,128]{2,1,0:T(8,128)(2,1)}, u32[]{:S(2)}, u32[]{:S(2)}) async-start(bf16[64,25,128]{2,1,0:T(8,128)(2,1)} %reshape.94), calls=%async_computation.3 | async-start | bytes 1048576 | tf_op jit(solution)/shard_map/all_to_all | solution.py:129
  159.2 4.8 %copy-start.2 = (bf16[1600,128]{1,0:T(8,128)(2,1)S(1)}, bf16[1600,128]{1,0:T(8,128)(2,1)}, u32[]{:S(2)}) copy-start(bf16[1600,128]{1,0:T(8,128)(2,1)} %copy-done.1) | copy-start | bytes 1228804
  159.2 4.8 %copy-start.4 = (bf16[256,1600]{0,1:T(8,128)(2,1)S(1)}, bf16[256,1600]{0,1:T(8,128)(2,1)}, u32[]{:S(2)}) copy-start(bf16[256,1600]{0,1:T(8,128)(2,1)} %copy-done.3) | copy-start | bytes 2457604
  161.4 19.2 %collective-permute-start.3 = (bf16[1600,128]{1,0:T(8,128)(2,1)}, bf16[1600,128]{1,0:T(8,128)(2,1)S(1)}, u32[]{:S(2)}, u32[]{:S(2)}) collective-permute-start(bf16[1600,128]{1,0:T(8,128)(2,1)} %convolution_convert_fusion), channel_id=1, source_target_pairs={{64,0},{128,64},{192,128},{256,192},{320,256},{384,320},{448,384},... | collective-permute-start | bytes 1228808 | tf_op jit(solution)/shard_map/ppermute | solution.py:16
  164.0 30.1 %copy-start.6 = (bf16[256,1600]{0,1:T(8,128)(2,1)S(1)}, bf16[256,1600]{0,1:T(8,128)(2,1)}, u32[]{:S(2)}) copy-start(bf16[256,1600]{0,1:T(8,128)(2,1)} %copy-done.5) | copy-start | bytes 2457604
  164.0 30.1 %copy-start.10 = (bf16[1600,128]{1,0:T(8,128)(2,1)S(1)}, bf16[1600,128]{1,0:T(8,128)(2,1)}, u32[]{:S(2)}) copy-start(bf16[1600,128]{1,0:T(8,128)(2,1)} %copy-done.9) | copy-start | bytes 1228804
  181.6 14.8 %copy-start.8 = (bf16[64,25,128]{2,1,0:T(8,128)(2,1)S(1)}, bf16[64,25,128]{2,1,0:T(8,128)(2,1)}, u32[]{:S(2)}) copy-start(bf16[64,25,128]{2,1,0:T(8,128)(2,1)} %copy-done.7) | copy-start | bytes 1228804
  181.6 32.9 %all-to-all-start.5 = ((bf16[64,25,128]{2,1,0:T(8,128)(2,1)}), bf16[64,25,128]{2,1,0:T(8,128)(2,1)S(1)}, u32[]{:S(2)}, u32[]{:S(2)}) async-start(bf16[64,25,128]{2,1,0:T(8,128)(2,1)} %reshape.100), calls=%async_computation.5 | async-start | bytes 1048576 | tf_op jit(solution)/shard_map/all_to_all | solution.py:136
where the time goes:
time: 216 us; the launch traced here: 215 us
  waiting for transfers between devices  107 us (50%)
  starting transfers between devices  77.5 us (36%)
  local copies, waits for them, and re-layouts  13.4 us (6%)
  matrix products  13.3 us (6%)
  other arithmetic  3.1 us (1%)
    ppermute x4, waiting for transfers between devices, passed_along(): return lax.ppermute(value, axis, pairs)  45.7 us
    ppermute x4, starting transfers between devices, passed_along(): return lax.ppermute(value, axis, pairs)  22.1 us
    all_to_all x1, waiting for transfers between devices, per_device(): lax.all_to_all(spread_heads(values[0], copies), 'head', split_axis=0, con...  18.7 us
    all_to_all x1, waiting for transfers between devices, per_device(): lax.all_to_all(gk_own.reshape(head_devices, vision_rows, HD), 'head', spl...  17.4 us
    all_to_all x1, waiting for transfers between devices, per_device(): lax.all_to_all(second_value.reshape(head_devices, vision_rows, HD), 'head...  16.2 us
    all_to_all x1, starting transfers between devices, per_device(): lax.all_to_all(second_key.reshape(head_devices, vision_rows, HD), 'head',...  13 us
    all_to_all x1, starting transfers between devices, per_device(): lax.all_to_all(second_value.reshape(head_devices, vision_rows, HD), 'head...  12.6 us
    all_to_all x1, starting transfers between devices, per_device(): lax.all_to_all(spread_heads(values[0], copies), 'head', split_axis=0, con...  12.6 us
  transfers between devices with their start and end apart: 10, of which 7 were waited for; matrix products, arithmetic and copies ran while one was open for 9% of the time, Pallas kernels for 0%

commit v1 on v0

v1 whole, which is shorter than its diff:
```python
import jax
import jax.numpy as jnp
from jax import lax
from jax.sharding import Mesh
from jax.sharding import PartitionSpec as P

HD = 128

NEGATIVE = -1e30


def passed_along(value, axis, by):
    length = lax.axis_size(axis)
    pairs = [(i, i + by) for i in range(length) if 0 <= i + by < length]
    return lax.ppermute(value, axis, pairs)


def block_forward(query_rows, key_rows, value_rows, keep_mask):
    scores = jnp.einsum(
        "rd,kd->rk", query_rows, key_rows, preferred_element_type=jnp.float32
    ) * HD ** (-0.5)
    scores = jnp.where(keep_mask[:, None] > 0, scores, NEGATIVE)
    highest = jnp.max(scores, axis=1)
    powered = jnp.exp(scores - highest[:, None])
    totals = jnp.sum(powered, axis=1)
    partial_value = jnp.dot(
        powered.astype(jnp.bfloat16), value_rows, preferred_element_type=jnp.float32
    )
    return (scores, highest, totals, partial_value)


def block_backward(
    scores, highest, totals, live_rows, grad_rows, row_delta, query_rows, key_rows, value_rows
):
    weights = live_rows[:, None] * jnp.exp(scores - highest[:, None]) / totals[:, None]
    grad_weights = jnp.einsum(
        "rd,kd->rk", grad_rows, value_rows, preferred_element_type=jnp.float32
    )
    grad_scores = (weights * (grad_weights - row_delta[:, None]) * HD ** (-0.5)).astype(
        jnp.bfloat16
    )
    query_grad = jnp.dot(grad_scores, key_rows, preferred_element_type=jnp.float32)
    key_part = jnp.einsum(
        "rk,rd->kd", grad_scores, query_rows, preferred_element_type=jnp.float32
    ).astype(jnp.bfloat16)
    value_part = jnp.einsum(
        "rk,rd->kd", weights.astype(jnp.bfloat16), grad_rows, preferred_element_type=jnp.float32
    ).astype(jnp.bfloat16)
    return (query_grad, key_part, value_part)


def per_device(queries, keys, values, cotangent, mask):
    groups = lax.axis_size("y")
    copies = lax.axis_size("r")
    rows = keys.shape[1]
    own_kv = jnp.stack([keys[0], values[0]])
    prev_kv = passed_along(own_kv, "seq", 1)
    both = jnp.concatenate([own_kv, prev_kv])
    both = jnp.transpose(both, (2, 0, 1, 3))
    by_group = lax.all_to_all(both, "y", split_axis=0, concat_axis=0, tiled=True)
    gathered = lax.all_gather(by_group, "r", axis=0, tiled=True)
    key_own, value_own, key_prev, value_prev = (
        gathered[:, i].reshape(copies * groups * rows, HD) for i in range(4)
    )

    head_count = queries.shape[1] // HD
    keep_own = jnp.repeat(mask[:, 0], head_count)
    keep_prev = jnp.repeat(mask[:, 1], head_count)
    live_rows = (keep_own + keep_prev > 0).astype(jnp.float32)
    score_own, peak_own, total_own, partial_own = block_forward(
        queries, key_own, value_own, keep_own
    )
    score_prev, peak_prev, total_prev, partial_prev = block_forward(
        queries, key_prev, value_prev, keep_prev
    )
    highest = jnp.maximum(peak_own, peak_prev)
    scale_own = jnp.exp(peak_own - highest)
    scale_prev = jnp.exp(peak_prev - highest)
    totals = scale_own * total_own + scale_prev * total_prev
    attended = (
        live_rows[:, None]
        * (scale_own[:, None] * partial_own + scale_prev[:, None] * partial_prev)
        / totals[:, None]
    ).astype(jnp.bfloat16)
    row_delta = jnp.sum(cotangent.astype(jnp.float32) * attended.astype(jnp.float32), axis=1)
    gq_own, gk_own, gv_own = block_backward(
        score_own, highest, totals, live_rows, cotangent, row_delta, queries, key_own, value_own
    )
    gq_prev, gk_prev, gv_prev = block_backward(
        score_prev, highest, totals, live_rows, cotangent, row_delta, queries, key_prev, value_prev
    )
    grad_query = (gq_own + gq_prev).astype(jnp.bfloat16)

    parts = jnp.stack(
        [p.reshape(copies * groups, rows, HD) for p in (gk_own, gv_own, gk_prev, gv_prev)],
        axis=1,
    )
    summed = lax.psum_scatter(parts.reshape(copies * groups, -1), "r", scatter_dimension=0, tiled=True).reshape(groups, 4, rows, HD)
    returned = lax.all_to_all(summed, "y", split_axis=0, concat_axis=0, tiled=True)
    second = passed_along(returned[:, 2:], "seq", -1)
    total = returned[:, :2].astype(jnp.float32) + second.astype(jnp.float32)
    total = jnp.transpose(total, (1, 2, 0, 3)).astype(jnp.bfloat16)
    return (attended, grad_query, total[0][None], total[1][None])


def solution(mesh):
    seq_devices, head_devices = mesh.devices.shape
    groups = 8
    split = Mesh(
        mesh.devices.reshape(seq_devices, groups, head_devices // groups), ("seq", "y", "r")
    )
    heads = ("y", "r")
    return jax.shard_map(
        per_device,
        mesh=split,
        in_specs=(
            P("seq", heads),
            P("seq", heads, None, None),
            P("seq", heads, None, None),
            P("seq", heads),
            P("seq", None),
        ),
        out_specs=(
            P("seq", heads),
            P("seq", heads),
            P("seq", heads, None, None),
            P("seq", heads, None, None),
        ),
        check_vma=False,
    )
```

time: 216 us -> 185 us (0.86)
  the two profiles are of different devices: /device:TPU:386 before, /device:TPU:2 now
where the time goes in v1:
time: 185 us
  waiting for transfers between devices  110 us (59%)
  local copies, waits for them, and re-layouts  24.3 us (13%)
  starting transfers between devices  14.3 us (8%)
  between operations  14.3 us (8%)
  blocking collectives  12.9 us (7%)
  matrix products  7.63 us (4%)
    reduce_scatter x1, waiting for transfers between devices, per_device(): lax.psum_scatter(parts.reshape(copies * groups, -1), 'r', scatter_dimensi...  47.1 us
    all_gather x1, waiting for transfers between devices, per_device(): gathered = lax.all_gather(by_group, 'r', axis=0, tiled=True)  37.8 us
    ppermute x2, waiting for transfers between devices, passed_along(): return lax.ppermute(value, axis, pairs)  15.3 us
    all_to_all x1, blocking collectives, per_device(): lax.all_to_all(both, 'y', split_axis=0, concat_axis=0, tiled=True)  12.9 us
    slice x1, local copies, waits for them, and re-layouts, per_device(): gathered[:, i].reshape(copies * groups * rows, HD)  12.7 us
    all_to_all x1, waiting for transfers between devices, per_device(): lax.all_to_all(summed, 'y', split_axis=0, concat_axis=0, tiled=True)  9.42 us
    ppermute x2, starting transfers between devices, passed_along(): return lax.ppermute(value, axis, pairs)  7.46 us
    all_to_all x1, starting transfers between devices, per_device(): lax.all_to_all(summed, 'y', split_axis=0, concat_axis=0, tiled=True)  6.75 us
  transfers between devices with their start and end apart: 5, of which 5 were waited for; matrix products, arithmetic and copies ran while one was open for 1% of the time, Pallas kernels for 0%

profile of v1, /device:TPU:2, one launch (start us, length us, event | category | flops | bytes accessed | tf_op | source)
XLA Modules:
  0.0 184.6 jit_solution(805615334668839639)
XLA Ops:
  7.2 0.9 copy.30
  8.1 0.9 copy.31
  9.0 0.2 pad_maximum_fusion.1
  9.3 5.2 %collective-permute-start = (bf16[2,25,8,128]{3,0,1,2:T(2,128)(2,1)S(1)}, bf16[2,25,8,128]{3,0,1,2:T(2,128)(2,1)S(1)}, u32[]{:S(2)}, u32[]{:S(2)}) collective-permute-start(bf16[2,25,8,128]{3,0,1,2:T(2,128)(2,1)S(1)} %pad_maximum_fusion.1), channel_id=1, source_target_pairs={{0,64},{64,128},{128,192},{192,256},{256,320},{320,384},{384,448},... | collective-permute-start | bytes 307208 | tf_op jit(solution)/shard_map/ppermute | solution.py:15
  14.5 11.9 %collective-permute-done = bf16[2,25,8,128]{3,0,1,2:T(2,128)(2,1)S(1)} collective-permute-done((bf16[2,25,8,128]{3,0,1,2:T(2,128)(2,1)S(1)}, bf16[2,25,8,128]{3,0,1,2:T(2,128)(2,1)S(1)}, u32[]{:S(2)}, u32[]{:S(2)}) %collective-permute-start) | collective-permute-done | bytes 102432 | tf_op jit(solution)/shard_map/ppermute | solution.py:15
  26.4 0.3 maximum_bitcast_fusion
  26.7 12.9 %all_to_all.10 = bf16[8,4,25,128]{3,1,2,0:T(4,128)(2,1)} all-to-all(bf16[8,4,25,128]{3,1,2,0:T(4,128)(2,1)S(1)} %maximum_bitcast_fusion), channel_id=1, replica_groups=mesh['seq'=16,'y'=8,'r'=8] {'y'}, dimensions={0} | all-to-all | bytes 409600 | tf_op jit(solution)/shard_map/all_to_all | solution.py:60
  39.7 0.0 reduce-scatter.2.cloned.1.call-start
  39.7 0.1 copy.32
  39.9 37.8 %all-gather.2.cloned.1.call-done = bf16[64,4,25,128]{3,1,2,0:T(4,128)(2,1)} async-done(((bf16[8,4,25,128]{3,1,2,0:T(4,128)(2,1)}), bf16[64,4,25,128]{3,1,2,0:T(4,128)(2,1)}) %all-gather.2.cloned.1.call-update) | async-done | bytes 1638416 | tf_op jit(solution)/shard_map/all_gather | solution.py:61
  77.6 12.7 %slice_reduce_fusion = (bf16[64,25,128]{2,1,0:T(8,128)(2,1)S(1)}, bf16[64,25,128]{2,1,0:T(8,128)(2,1)S(1)}, bf16[64,25,128]{2,1,0:T(8,128)(2,1)S(1)}, bf16[64,25,128]{2,1,0:T(8,128)(2,1)S(1)}) fusion(bf16[64,4,25,128]{3,1,2,0:T(4,128)(2,1)} %all-gather.2.cloned.1.call-done), kind=kLoop, calls=%fused_computation.33 | loop fusion | bytes 3276800 | tf_op jit(solution)/shard_map/slice | solution.py:63
  90.4 0.1 reshape_squeeze.15
  90.5 0.1 reshape_squeeze.14
  90.7 0.1 reshape_squeeze.13
  90.8 0.1 reshape_squeeze.12
  91.0 0.4 fusion.25
  91.5 0.4 fusion.26
  91.9 0.5 fusion.8
  92.4 0.4 convolution_multiply_fusion.3
  92.8 0.4 convolution_convert_fusion
  93.3 0.5 multiply_reduce_fusion
  93.8 0.6 fusion.7
  94.3 0.2 copy-done.6
  94.6 0.6 fusion.6
  95.2 1.2 convolution_convert_fusion.2
  96.4 0.1 stack_reshape.15
  96.6 0.4 convolution_convert_fusion.1
  96.9 1.1 convolution_convert_fusion.3
  98.1 1.1 stack_reshape.12
  99.2 0.1 stack_reshape.14
  99.4 1.1 stack_reshape.13
  100.5 0.3 pad_maximum_fusion
  100.9 0.6 copy.33
  101.5 1.7 reshape.45
  103.2 47.1 %reduce-scatter.2.cloned.1.call-done = bf16[8,12800]{1,0:T(8,128)(2,1)} async-done(((bf16[64,12800]{1,0:T(8,128)(2,1)}), bf16[8,12800]{1,0:T(8,128)(2,1)}) %reduce-scatter.2.cloned.1.call-update) | async-done | bytes 204816 | tf_op jit(solution)/shard_map/reduce_scatter | solution.py:98
  150.4 1.7 copy.34
  152.1 6.8 %all-to-all-start.1 = ((bf16[8,4,25,128]{3,1,2,0:T(4,128)(2,1)}), bf16[8,4,25,128]{3,1,2,0:T(4,128)(2,1)S(1)}, u32[]{:S(2)}, u32[]{:S(2)}) async-start(bf16[8,4,25,128]{3,1,2,0:T(4,128)(2,1)} %copy.34), calls=%async_computation.2 | async-start | bytes 409600 | tf_op jit(solution)/shard_map/all_to_all | solution.py:99
  158.8 0.4 fusion.27
  159.3 9.4 %all-to-all-done.1 = bf16[8,4,25,128]{3,1,2,0:T(4,128)(2,1)S(1)} async-done(((bf16[8,4,25,128]{3,1,2,0:T(4,128)(2,1)}), bf16[8,4,25,128]{3,1,2,0:T(4,128)(2,1)S(1)}, u32[]{:S(2)}, u32[]{:S(2)}) %all-to-all-start.1) | async-done | bytes 204832 | tf_op jit(solution)/shard_map/all_to_all | solution.py:99
  168.7 0.1 slice.45
  168.8 2.3 %collective-permute-start.1 = (bf16[8,2,25,128]{3,1,2,0:T(2,128)(2,1)S(1)}, bf16[8,2,25,128]{3,1,2,0:T(2,128)(2,1)S(1)}, u32[]{:S(2)}, u32[]{:S(2)}) collective-permute-start(bf16[8,2,25,128]{3,1,2,0:T(2,128)(2,1)S(1)} %slice.45), channel_id=1, source_target_pairs={{64,0},{128,64},{192,128},{256,192},{320,256},{384,320},{448,384},... | collective-permute-start | bytes 307208 | tf_op jit(solution)/shard_map/ppermute | solution.py:15
  171.1 1.1 fusion.16
  172.2 0.7 copy.35
  172.9 3.3 %collective-permute-done.1 = bf16[8,2,25,128]{3,1,2,0:T(2,128)(2,1)S(1)} collective-permute-done((bf16[8,2,25,128]{3,1,2,0:T(2,128)(2,1)S(1)}, bf16[8,2,25,128]{3,1,2,0:T(2,128)(2,1)S(1)}, u32[]{:S(2)}, u32[]{:S(2)}) %collective-permute-start.1) | collective-permute-done | bytes 102432 | tf_op jit(solution)/shard_map/ppermute | solution.py:15
  176.2 0.1 fusion.23
  176.4 0.1 fusion.24
  176.5 0.6 copy.37
  177.1 0.6 copy.36
  (20 shorter events, 0.1 us)
Async XLA Ops:
  7.2 83.8 %copy-start = (bf16[256,128]{1,0:T(8,128)(2,1)S(1)}, bf16[256,128]{1,0:T(8,128)(2,1)}, u32[]{:S(2)}) copy-start(bf16[256,128]{1,0:T(8,128)(2,1)} %param.5) | copy-start | bytes 196612
  7.2 32.6 %copy-start.5 = (bf16[256,128]{1,0:T(8,128)(2,1)S(1)}, bf16[256,128]{1,0:T(8,128)(2,1)}, u32[]{:S(2)}) copy-start(bf16[256,128]{1,0:T(8,128)(2,1)} %param.8) | copy-start | bytes 196612
  7.2 32.7 %copy-start.7 = (s32[256,2]{0,1:T(2,128)S(1)}, s32[256,2]{0,1:T(2,128)}, u32[]{:S(2)}) copy-start(s32[256,2]{0,1:T(2,128)} %param.9) | copy-start | bytes 6148
  7.2 70.4 %all-gather.2.cloned.1.call-start = ((), (), s32[]{:S(2)}) async-start(), calls=%async_computation.3 | async-start | bytes 1843200 | tf_op jit(solution)/shard_map/all_gather | solution.py:61
  9.3 17.1 %collective-permute-start = (bf16[2,25,8,128]{3,0,1,2:T(2,128)(2,1)S(1)}, bf16[2,25,8,128]{3,0,1,2:T(2,128)(2,1)S(1)}, u32[]{:S(2)}, u32[]{:S(2)}) collective-permute-start(bf16[2,25,8,128]{3,0,1,2:T(2,128)(2,1)S(1)} %pad_maximum_fusion.1), channel_id=1, source_target_pairs={{0,64},{64,128},{128,192},{192,256},{256,320},{320,384},{384,448},... | collective-permute-start | bytes 307208 | tf_op jit(solution)/shard_map/ppermute | solution.py:15
  39.7 110.7 %reduce-scatter.2.cloned.1.call-start = ((), (), s32[]{:S(2)}) async-start(), calls=%async_computation.4 | async-start | bytes 1843200 | tf_op jit(solution)/shard_map/reduce_scatter | solution.py:98
  93.7 0.8 copy-start.6
  94.6 2.0 %copy-start.1 = (bf16[1600,256]{1,0:T(8,128)(2,1)}, bf16[1600,256]{1,0:T(8,128)(2,1)S(1)}, u32[]{:S(2)}) copy-start(bf16[1600,256]{1,0:T(8,128)(2,1)S(1)} %fusion.7) | copy-start | bytes 2457604
  95.2 1.7 copy-start.3
  103.2 55.6 %copy-start.4 = (bf16[1600,256]{1,0:T(8,128)(2,1)S(1)}, bf16[1600,256]{1,0:T(8,128)(2,1)}, u32[]{:S(2)}) copy-start(bf16[1600,256]{1,0:T(8,128)(2,1)} %copy-done.3) | copy-start | bytes 2457604
  103.2 67.9 %copy-start.2 = (bf16[1600,256]{1,0:T(8,128)(2,1)S(1)}, bf16[1600,256]{1,0:T(8,128)(2,1)}, u32[]{:S(2)}) copy-start(bf16[1600,256]{1,0:T(8,128)(2,1)} %copy-done.1) | copy-start | bytes 2457604
  152.1 16.6 %all-to-all-start.1 = ((bf16[8,4,25,128]{3,1,2,0:T(4,128)(2,1)}), bf16[8,4,25,128]{3,1,2,0:T(4,128)(2,1)S(1)}, u32[]{:S(2)}, u32[]{:S(2)}) async-start(bf16[8,4,25,128]{3,1,2,0:T(4,128)(2,1)} %copy.34), calls=%async_computation.2 | async-start | bytes 409600 | tf_op jit(solution)/shard_map/all_to_all | solution.py:99
  168.8 7.5 %collective-permute-start.1 = (bf16[8,2,25,128]{3,1,2,0:T(2,128)(2,1)S(1)}, bf16[8,2,25,128]{3,1,2,0:T(2,128)(2,1)S(1)}, u32[]{:S(2)}, u32[]{:S(2)}) collective-permute-start(bf16[8,2,25,128]{3,1,2,0:T(2,128)(2,1)S(1)} %slice.45), channel_id=1, source_target_pairs={{64,0},{128,64},{192,128},{256,192},{320,256},{384,320},{448,384},... | collective-permute-start | bytes 307208 | tf_op jit(solution)/shard_map/ppermute | solution.py:15
Sparse Core Ops, SparseCore 0:
  39.8 37.7 all-gather.1
  103.4 46.9 reduce-scatter.1

commit v2 on v1

--- a/solution.py
+++ b/solution.py
@@ -5,6 +5,7 @@
 from jax.sharding import PartitionSpec as P
 
 HD = 128
+KVH = 8
 
 NEGATIVE = -1e30
 
@@ -13,6 +14,12 @@
     length = lax.axis_size(axis)
     pairs = [(i, i + by) for i in range(length) if 0 <= i + by < length]
     return lax.ppermute(value, axis, pairs)
+
+
+def swapped(value):
+    n = lax.axis_size("r")
+    pairs = [(a * n + b, b * n + a) for a in range(n) for b in range(n)]
+    return lax.ppermute(value, ("y", "r"), pairs)
 
 
 def block_forward(query_rows, key_rows, value_rows, keep_mask):
@@ -52,16 +59,20 @@
 def per_device(queries, keys, values, cotangent, mask):
     groups = lax.axis_size("y")
     copies = lax.axis_size("r")
+    blocks = groups * copies
     rows = keys.shape[1]
+    inputs = swapped(jnp.stack([queries, cotangent]))
+    queries, cotangent = inputs[0], inputs[1]
+
     own_kv = jnp.stack([keys[0], values[0]])
     prev_kv = passed_along(own_kv, "seq", 1)
-    both = jnp.concatenate([own_kv, prev_kv])
-    both = jnp.transpose(both, (2, 0, 1, 3))
-    by_group = lax.all_to_all(both, "y", split_axis=0, concat_axis=0, tiled=True)
-    gathered = lax.all_gather(by_group, "r", axis=0, tiled=True)
-    key_own, value_own, key_prev, value_prev = (
-        gathered[:, i].reshape(copies * groups * rows, HD) for i in range(4)
-    )
+    both = jnp.transpose(jnp.concatenate([own_kv, prev_kv]), (0, 2, 1, 3))
+    by_copy = lax.all_to_all(both, "r", split_axis=1, concat_axis=1, tiled=True)
+    by_copy = by_copy.reshape(4, copies, rows * HD)
+    gathered = lax.all_gather(by_copy, "y", axis=1, tiled=True)
+    gathered = jnp.transpose(gathered.reshape(4, blocks, rows, HD), (0, 2, 1, 3))
+    gathered = gathered.reshape(4, rows * blocks, HD)
+    key_own, value_own, key_prev, value_prev = (gathered[i] for i in range(4))
 
     head_count = queries.shape[1] // HD
     keep_own = jnp.repeat(mask[:, 0], head_count)
@@ -90,24 +101,23 @@
         score_prev, highest, totals, live_rows, cotangent, row_delta, queries, key_prev, value_prev
     )
     grad_query = (gq_own + gq_prev).astype(jnp.bfloat16)
+    outputs = swapped(jnp.stack([attended, grad_query]))
 
-    parts = jnp.stack(
-        [p.reshape(copies * groups, rows, HD) for p in (gk_own, gv_own, gk_prev, gv_prev)],
-        axis=1,
-    )
-    summed = lax.psum_scatter(parts.reshape(copies * groups, -1), "r", scatter_dimension=0, tiled=True).reshape(groups, 4, rows, HD)
-    returned = lax.all_to_all(summed, "y", split_axis=0, concat_axis=0, tiled=True)
+    parts = jnp.stack([gk_own, gv_own, gk_prev, gv_prev]).reshape(4, rows, blocks, HD)
+    parts = jnp.transpose(parts, (2, 0, 1, 3)).reshape(blocks, -1)
+    summed = lax.psum_scatter(parts, "y", scatter_dimension=0, tiled=True)
+    summed = summed.reshape(copies, 4, rows, HD)
+    returned = lax.all_to_all(summed, "r", split_axis=0, concat_axis=0, tiled=True)
     second = passed_along(returned[:, 2:], "seq", -1)
     total = returned[:, :2].astype(jnp.float32) + second.astype(jnp.float32)
     total = jnp.transpose(total, (1, 2, 0, 3)).astype(jnp.bfloat16)
-    return (attended, grad_query, total[0][None], total[1][None])
+    return (outputs[0], outputs[1], total[0][None], total[1][None])
 
 
 def solution(mesh):
     seq_devices, head_devices = mesh.devices.shape
-    groups = 8
     split = Mesh(
-        mesh.devices.reshape(seq_devices, groups, head_devices // groups), ("seq", "y", "r")
+        mesh.devices.reshape(seq_devices, KVH, head_devices // KVH), ("seq", "y", "r")
     )
     heads = ("y", "r")
     return jax.shard_map(

time: 185 us -> 186 us (level)
  the two profiles are of different devices: /device:TPU:2 before, /device:TPU:12 now
where the time goes in v2:
time: 186 us; the launch traced here: 185 us
  waiting for transfers between devices  111 us (60%)
  blocking collectives  22 us (12%)
  starting transfers between devices  15.8 us (8%)
  local copies, waits for them, and re-layouts  15.6 us (8%)
  between operations  14.4 us (8%)
  matrix products  5.19 us (3%)
    all_gather x1, waiting for transfers between devices, per_device(): gathered = lax.all_gather(by_copy, 'y', axis=1, tiled=True)  47.5 us
    reduce_scatter x1, waiting for transfers between devices, per_device(): summed = lax.psum_scatter(parts, 'y', scatter_dimension=0, tiled=True)  44.9 us
    all_to_all x1, blocking collectives, per_device(): by_copy = lax.all_to_all(both, 'r', split_axis=1, concat_axis=1, tiled=True)  22 us
    ppermute x2, waiting for transfers between devices, swapped(): return lax.ppermute(value, ('y', 'r'), pairs)  12.5 us
    all_to_all x1, starting transfers between devices, per_device(): lax.all_to_all(summed, 'r', split_axis=0, concat_axis=0, tiled=True)  7.21 us
    unnamed x22, local copies, waits for them, and re-layouts  6.36 us
    ppermute x2, starting transfers between devices, swapped(): return lax.ppermute(value, ('y', 'r'), pairs)  4.74 us
    ppermute x2, starting transfers between devices, passed_along(): return lax.ppermute(value, axis, pairs)  3.79 us
  transfers between devices with their start and end apart: 7, of which 5 were waited for; matrix products, arithmetic and copies ran while one was open for 3% of the time, Pallas kernels for 0%

profile of v2, /device:TPU:12, one launch (start us, length us, event | category | flops | bytes accessed | tf_op | source)
XLA Modules:
  0.0 185.4 jit_solution(17050480821973689574)
XLA Ops:
  7.2 0.9 copy.77
  8.1 0.9 copy.78
  9.0 0.2 pad_maximum_fusion.2
  9.3 2.5 %collective-permute-start.1 = (bf16[2,25,8,128]{3,0,1,2:T(2,128)(2,1)S(1)}, bf16[2,25,8,128]{3,0,1,2:T(2,128)(2,1)S(1)}, u32[]{:S(2)}, u32[]{:S(2)}) collective-permute-start(bf16[2,25,8,128]{3,0,1,2:T(2,128)(2,1)S(1)} %pad_maximum_fusion.2), channel_id=1, source_target_pairs={{0,64},{64,128},{128,192},{192,256},{256,320},{320,384},{384,448},... | collective-permute-start | bytes 307208 | tf_op jit(solution)/shard_map/ppermute | solution.py:16
  11.8 2.2 %collective-permute-done.1 = bf16[2,25,8,128]{3,0,1,2:T(2,128)(2,1)S(1)} collective-permute-done((bf16[2,25,8,128]{3,0,1,2:T(2,128)(2,1)S(1)}, bf16[2,25,8,128]{3,0,1,2:T(2,128)(2,1)S(1)}, u32[]{:S(2)}, u32[]{:S(2)}) %collective-permute-start.1) | collective-permute-done | bytes 102432 | tf_op jit(solution)/shard_map/ppermute | solution.py:16
  14.0 0.3 maximum_bitcast_fusion.1
  14.4 22.0 %all_to_all.10 = bf16[4,8,25,128]{3,0,2,1:T(4,128)(2,1)S(1)} all-to-all(bf16[4,8,25,128]{3,0,2,1:T(4,128)(2,1)S(1)} %maximum_bitcast_fusion.1), channel_id=1, replica_groups=mesh['seq'=16,'y'=8,'r'=8] {'r'}, dimensions={1} | all-to-all | bytes 409600 | tf_op jit(solution)/shard_map/all_to_all | solution.py:70
  36.3 0.7 copy.98
  37.4 1.9 %collective-permute-start = (bf16[2,256,128]{1,2,0:T(8,128)(2,1)S(1)}, bf16[2,256,128]{1,2,0:T(8,128)(2,1)S(1)}, u32[]{:S(2)}, u32[]{:S(2)}) collective-permute-start(bf16[2,256,128]{1,2,0:T(8,128)(2,1)S(1)} %pad_maximum_fusion), channel_id=1, source_target_pairs={{0,0},{1,8},{2,16},{3,24},{4,32},{5,40},{6,48},{7,56},{8,1},{9,9},... | collective-permute-start | bytes 393224 | tf_op jit(solution)/shard_map/ppermute | solution.py:22
  39.4 47.5 %all-gather.2.cloned.1.call-done = bf16[4,64,3200]{2,1,0:T(8,128)(2,1)} async-done(((bf16[4,8,3200]{2,1,0:T(8,128)(2,1)}), bf16[4,64,3200]{2,1,0:T(8,128)(2,1)}) %all-gather.2.cloned.1.call-update) | async-done | bytes 1638416 | tf_op jit(solution)/shard_map/all_gather | solution.py:72
  86.9 2.7 %reshape.70 = bf16[4,64,25,128]{3,2,1,0:T(8,128)(2,1)S(1)} reshape(bf16[4,64,3200]{2,1,0:T(8,128)(2,1)} %all-gather.2.cloned.1.call-done) | data formatting | bytes 3276800 | tf_op jit(solution)/shard_map/reshape | solution.py:73
  89.6 0.4 fusion.25
  90.0 0.2 copy.83
  90.2 0.2 copy.82
  90.4 0.2 copy.81
  90.5 0.2 copy.80
  90.7 0.4 fusion.27
  91.1 0.4 fusion.28
  91.6 0.5 fusion.8
  92.0 0.4 convolution_convert_fusion
  92.5 0.3 copy.89
  92.8 0.4 convolution_convert_fusion.2
  93.2 0.3 copy.87
  93.5 0.4 convolution_multiply_fusion.3
  94.0 0.5 multiply_reduce_fusion
  94.4 0.6 fusion.7
  95.0 0.4 convolution_convert_fusion.1
  95.4 0.3 copy.88
  95.7 0.6 fusion.6
  96.3 0.4 convolution_convert_fusion.3
  96.6 0.5 copy-done.2
  97.2 0.3 copy.86
  97.4 0.3 maximum_bitcast_fusion
  97.7 1.7 reshape.71
  99.5 1.1 copy-done.3
  100.6 0.3 fusion.29
  100.9 44.9 %reduce-scatter.2.cloned.1.call-done = bf16[8,12800]{1,0:T(8,128)(2,1)} async-done(((bf16[64,12800]{1,0:T(8,128)(2,1)}), bf16[8,12800]{1,0:T(8,128)(2,1)}) %reduce-scatter.2.cloned.1.call-update) | async-done | bytes 204816 | tf_op jit(solution)/shard_map/reduce_scatter | solution.py:108
  145.8 1.7 copy.90
  147.5 7.2 %all-to-all-start.1 = ((bf16[8,4,25,128]{3,1,2,0:T(4,128)(2,1)}), bf16[8,4,25,128]{3,1,2,0:T(4,128)(2,1)S(1)}, u32[]{:S(2)}, u32[]{:S(2)}) async-start(bf16[8,4,25,128]{3,1,2,0:T(4,128)(2,1)} %copy.90), calls=%async_computation.2 | async-start | bytes 409600 | tf_op jit(solution)/shard_map/all_to_all | solution.py:110
  154.7 0.3 fusion.17
  155.1 2.8 %collective-permute-start.2 = (bf16[2,256,128]{1,2,0:T(8,128)(2,1)S(1)}, bf16[2,256,128]{1,2,0:T(8,128)(2,1)S(1)}, u32[]{:S(2)}, u32[]{:S(2)}) collective-permute-start(bf16[2,256,128]{1,2,0:T(8,128)(2,1)S(1)} %pad_maximum_fusion.1), channel_id=1, source_target_pairs={{0,0},{1,8},{2,16},{3,24},{4,32},{5,40},{6,48},{7,56},{8,1},{9,9},... | collective-permute-start | bytes 393224 | tf_op jit(solution)/shard_map/ppermute | solution.py:22
  157.9 3.6 %all-to-all-done.1 = bf16[8,4,25,128]{3,1,2,0:T(4,128)(2,1)S(1)} async-done(((bf16[8,4,25,128]{3,1,2,0:T(4,128)(2,1)}), bf16[8,4,25,128]{3,1,2,0:T(4,128)(2,1)S(1)}, u32[]{:S(2)}, u32[]{:S(2)}) %all-to-all-start.1) | async-done | bytes 204832 | tf_op jit(solution)/shard_map/all_to_all | solution.py:110
  161.7 1.3 collective-permute-start.3
  163.0 12.5 %collective-permute-done.2 = bf16[2,256,128]{1,2,0:T(8,128)(2,1)S(1)} collective-permute-done((bf16[2,256,128]{1,2,0:T(8,128)(2,1)S(1)}, bf16[2,256,128]{1,2,0:T(8,128)(2,1)S(1)}, u32[]{:S(2)}, u32[]{:S(2)}) %collective-permute-start.2) | collective-permute-done | bytes 131104 | tf_op jit(solution)/shard_map/ppermute | solution.py:22
  175.5 0.7 copy.92
  176.2 0.7 copy.91
  177.3 0.6 copy.94
  177.9 0.6 copy.93
  (28 shorter events, 0.8 us)
Async XLA Ops:
  7.2 30.0 %copy-start.4 = (bf16[256,128]{1,0:T(8,128)(2,1)S(1)}, bf16[256,128]{1,0:T(8,128)(2,1)}, u32[]{:S(2)}) copy-start(bf16[256,128]{1,0:T(8,128)(2,1)} %param.5) | copy-start | bytes 196612
  7.2 30.1 %copy-start.5 = (bf16[256,128]{1,0:T(8,128)(2,1)S(1)}, bf16[256,128]{1,0:T(8,128)(2,1)}, u32[]{:S(2)}) copy-start(bf16[256,128]{1,0:T(8,128)(2,1)} %param.8) | copy-start | bytes 196612
  7.2 32.2 %copy-start.6 = (s32[256,2]{0,1:T(2,128)S(1)}, s32[256,2]{0,1:T(2,128)}, u32[]{:S(2)}) copy-start(s32[256,2]{0,1:T(2,128)} %param.9) | copy-start | bytes 6148
  7.2 79.7 %all-gather.2.cloned.1.call-start = ((), (), s32[]{:S(2)}) async-start(), calls=%async_computation.3 | async-start | bytes 1843200 | tf_op jit(solution)/shard_map/all_gather | solution.py:72
  9.3 4.7 %collective-permute-start.1 = (bf16[2,25,8,128]{3,0,1,2:T(2,128)(2,1)S(1)}, bf16[2,25,8,128]{3,0,1,2:T(2,128)(2,1)S(1)}, u32[]{:S(2)}, u32[]{:S(2)}) collective-permute-start(bf16[2,25,8,128]{3,0,1,2:T(2,128)(2,1)S(1)} %pad_maximum_fusion.2), channel_id=1, source_target_pairs={{0,64},{64,128},{128,192},{192,256},{256,320},{320,384},{384,448},... | collective-permute-start | bytes 307208 | tf_op jit(solution)/shard_map/ppermute | solution.py:16
  37.1 108.7 %reduce-scatter.2.cloned.1.call-start = ((), (), s32[]{:S(2)}) async-start(), calls=%async_computation.4 | async-start | bytes 1843200 | tf_op jit(solution)/shard_map/reduce_scatter | solution.py:108
  37.4 53.3 %collective-permute-start = (bf16[2,256,128]{1,2,0:T(8,128)(2,1)S(1)}, bf16[2,256,128]{1,2,0:T(8,128)(2,1)S(1)}, u32[]{:S(2)}, u32[]{:S(2)}) collective-permute-start(bf16[2,256,128]{1,2,0:T(8,128)(2,1)S(1)} %pad_maximum_fusion), channel_id=1, source_target_pairs={{0,0},{1,8},{2,16},{3,24},{4,32},{5,40},{6,48},{7,56},{8,1},{9,9},... | collective-permute-start | bytes 393224 | tf_op jit(solution)/shard_map/ppermute | solution.py:22
  95.0 1.2 copy-start
  96.3 0.9 copy-start.2
  99.5 1.1 copy-start.3
  99.5 55.3 %copy-start.1 = (bf16[256,1600]{0,1:T(8,128)(2,1)S(1)}, bf16[256,1600]{0,1:T(8,128)(2,1)}, u32[]{:S(2)}) copy-start(bf16[256,1600]{0,1:T(8,128)(2,1)} %copy-done) | copy-start | bytes 2457604
  147.5 14.1 %all-to-all-start.1 = ((bf16[8,4,25,128]{3,1,2,0:T(4,128)(2,1)}), bf16[8,4,25,128]{3,1,2,0:T(4,128)(2,1)S(1)}, u32[]{:S(2)}, u32[]{:S(2)}) async-start(bf16[8,4,25,128]{3,1,2,0:T(4,128)(2,1)} %copy.90), calls=%async_computation.2 | async-start | bytes 409600 | tf_op jit(solution)/shard_map/all_to_all | solution.py:110
  155.1 20.4 %collective-permute-start.2 = (bf16[2,256,128]{1,2,0:T(8,128)(2,1)S(1)}, bf16[2,256,128]{1,2,0:T(8,128)(2,1)S(1)}, u32[]{:S(2)}, u32[]{:S(2)}) collective-permute-start(bf16[2,256,128]{1,2,0:T(8,128)(2,1)S(1)} %pad_maximum_fusion.1), channel_id=1, source_target_pairs={{0,0},{1,8},{2,16},{3,24},{4,32},{5,40},{6,48},{7,56},{8,1},{9,9},... | collective-permute-start | bytes 393224 | tf_op jit(solution)/shard_map/ppermute | solution.py:22
  161.7 15.3 %collective-permute-start.3 = (bf16[8,2,25,128]{3,1,2,0:T(2,128)(2,1)S(1)}, bf16[8,2,25,128]{3,1,2,0:T(2,128)(2,1)S(1)}, u32[]{:S(2)}, u32[]{:S(2)}) collective-permute-start(bf16[8,2,25,128]{3,1,2,0:T(2,128)(2,1)S(1)} %slice.69), channel_id=1, source_target_pairs={{64,0},{128,64},{192,128},{256,192},{320,256},{384,320},{448,384},... | collective-permute-start | bytes 307208 | tf_op jit(solution)/shard_map/ppermute | solution.py:16
Sparse Core Ops, SparseCore 0:
  37.2 49.6 all-gather.1
  99.6 46.1 reduce-scatter.1

commit v3 on v1

v3 whole, which is shorter than its diff:
```python
import jax
import jax.numpy as jnp
from jax import lax
from jax.sharding import Mesh
from jax.sharding import PartitionSpec as P

HD = 128
KVH = 8

NEGATIVE = -1e30


def passed_along(value, axis, by):
    length = lax.axis_size(axis)
    pairs = [(i, i + by) for i in range(length) if 0 <= i + by < length]
    return lax.ppermute(value, axis, pairs)


def block_forward(query_rows, key_rows, value_rows, keep_mask):
    scores = jnp.einsum(
        "rd,kd->rk", query_rows, key_rows, preferred_element_type=jnp.float32
    ) * HD ** (-0.5)
    scores = jnp.where(keep_mask[:, None] > 0, scores, NEGATIVE)
    highest = jnp.max(scores, axis=1)
    powered = jnp.exp(scores - highest[:, None])
    totals = jnp.sum(powered, axis=1)
    partial_value = jnp.dot(
        powered.astype(jnp.bfloat16), value_rows, preferred_element_type=jnp.float32
    )
    return (scores, highest, totals, partial_value)


def finish_backward(weights, grad_rows, row_delta, query_rows, key_rows, value_rows):
    grad_weights = jnp.einsum(
        "rd,kd->rk", grad_rows, value_rows, preferred_element_type=jnp.float32
    )
    grad_scores = (weights * (grad_weights - row_delta[:, None]) * HD ** (-0.5)).astype(
        jnp.bfloat16
    )
    query_grad = jnp.dot(grad_scores, key_rows, preferred_element_type=jnp.float32)
    key_part = jnp.einsum(
        "rk,rd->kd", grad_scores, query_rows, preferred_element_type=jnp.float32
    ).astype(jnp.bfloat16)
    value_part = jnp.einsum(
        "rk,rd->kd", weights.astype(jnp.bfloat16), grad_rows, preferred_element_type=jnp.float32
    ).astype(jnp.bfloat16)
    return (query_grad, key_part, value_part)


def per_device(queries, keys, values, cotangent, mask):
    groups = lax.axis_size("y")
    copies = lax.axis_size("r")
    blocks = groups * copies
    rows = keys.shape[1]
    tokens = queries.shape[0]
    half = tokens // 2

    served = passed_along(jnp.stack([queries[:half], cotangent[:half]]), "seq", -1)
    query_next, grad_next = served[0], served[1]

    own_kv = jnp.stack([keys[0], values[0]])
    own_kv = jnp.transpose(own_kv, (0, 2, 1, 3)).reshape(2, KVH, rows * HD)
    by_group = lax.all_to_all(own_kv, "y", split_axis=1, concat_axis=1, tiled=True)
    gathered = lax.all_gather(by_group, "r", axis=1, tiled=True)
    gathered = jnp.transpose(gathered.reshape(2, blocks, rows, HD), (0, 2, 1, 3))
    gathered = gathered.reshape(2, rows * blocks, HD)
    key_own, value_own = gathered[0], gathered[1]

    keep_own = mask[:, 0]
    keep_prev = mask[:, 1]
    live_rows = (keep_own + keep_prev > 0).astype(jnp.float32)
    score_own, peak_own, total_own, partial_own = block_forward(
        queries, key_own, value_own, keep_own
    )

    score_next = jnp.einsum(
        "rd,kd->rk", query_next, key_own, preferred_element_type=jnp.float32
    ) * HD ** (-0.5)
    peak_next = jnp.max(score_next, axis=1)
    total_next = jnp.sum(jnp.exp(score_next - peak_next[:, None]), axis=1)
    partial_next = jnp.dot(
        jnp.exp(score_next - peak_next[:, None]).astype(jnp.bfloat16),
        value_own,
        preferred_element_type=jnp.float32,
    )
    stats = jnp.concatenate(
        [partial_next, peak_next.reshape(-1, HD), total_next.reshape(-1, HD)]
    )
    stats = passed_along(stats, "seq", 1)
    seen = keep_prev[:half] > 0
    got_peak = stats[half : half + half // HD].reshape(half)
    got_total = stats[half + half // HD :].reshape(half)
    rest = tokens - half
    peak_prev = jnp.concatenate(
        [jnp.where(seen, got_peak, NEGATIVE), jnp.full((rest,), NEGATIVE, jnp.float32)]
    )
    total_prev = jnp.concatenate(
        [jnp.where(seen, got_total, 0.0), jnp.zeros((rest,), jnp.float32)]
    )
    partial_prev = jnp.concatenate(
        [jnp.where(seen[:, None], stats[:half], 0.0), jnp.zeros((rest, HD), jnp.float32)]
    )

    highest = jnp.maximum(peak_own, peak_prev)
    scale_own = jnp.exp(peak_own - highest)
    scale_prev = jnp.exp(peak_prev - highest)
    totals = scale_own * total_own + scale_prev * total_prev
    attended = (
        live_rows[:, None]
        * (scale_own[:, None] * partial_own + scale_prev[:, None] * partial_prev)
        / totals[:, None]
    ).astype(jnp.bfloat16)
    row_delta = jnp.sum(cotangent.astype(jnp.float32) * attended.astype(jnp.float32), axis=1)

    control = jnp.stack(
        [
            jnp.where(seen, highest[:half], got_peak),
            jnp.where(seen, 1.0 / totals[:half], 0.0),
            row_delta[:half],
        ]
    )
    control = passed_along(control, "seq", -1)

    weights_own = live_rows[:, None] * jnp.exp(score_own - highest[:, None]) / totals[:, None]
    gq_own, gk_own, gv_own = finish_backward(
        weights_own, cotangent, row_delta, queries, key_own, value_own
    )
    weights_next = jnp.exp(score_next - control[0][:, None]) * control[1][:, None]
    gq_next, gk_next, gv_next = finish_backward(
        weights_next, grad_next, control[2], query_next, key_own, value_own
    )
    gq_prev = passed_along(gq_next, "seq", 1)
    grad_query = (
        gq_own + jnp.concatenate([gq_prev, jnp.zeros((rest, HD), jnp.float32)])
    ).astype(jnp.bfloat16)

    parts = jnp.stack(
        [
            gk_own.astype(jnp.float32) + gk_next.astype(jnp.float32),
            gv_own.astype(jnp.float32) + gv_next.astype(jnp.float32),
        ]
    ).astype(jnp.bfloat16)
    parts = jnp.transpose(parts.reshape(2, rows, copies, groups, HD), (2, 0, 1, 3, 4))
    parts = parts.reshape(blocks, -1)
    summed = lax.psum_scatter(parts, "r", scatter_dimension=0, tiled=True)
    summed = summed.reshape(2, rows, groups, HD)
    returned = lax.all_to_all(summed, "y", split_axis=2, concat_axis=2, tiled=True)
    return (attended, grad_query, returned[0][None], returned[1][None])


def solution(mesh):
    seq_devices, head_devices = mesh.devices.shape
    split = Mesh(
        mesh.devices.reshape(seq_devices, KVH, head_devices // KVH), ("seq", "y", "r")
    )
    heads = ("y", "r")
    return jax.shard_map(
        per_device,
        mesh=split,
        in_specs=(
            P("seq", heads),
            P("seq", heads, None, None),
            P("seq", heads, None, None),
            P("seq", heads),
            P("seq", None),
        ),
        out_specs=(
            P("seq", heads),
            P("seq", heads),
            P("seq", heads, None, None),
            P("seq", heads, None, None),
        ),
        check_vma=False,
    )
```

time: 185 us -> 137 us (0.74)
  the two profiles are of different devices: /device:TPU:2 before, /device:TPU:5 now
where the time goes in v3:
time: 137 us
  waiting for transfers between devices  59.6 us (44%)
  blocking collectives  24.4 us (18%)
  starting transfers between devices  21.4 us (16%)
  between operations  14.3 us (10%)
  local copies, waits for them, and re-layouts  7.97 us (6%)
  matrix products  5.92 us (4%)
  other arithmetic  3.14 us (2%)
    reduce_scatter x1, waiting for transfers between devices, per_device(): summed = lax.psum_scatter(parts, 'r', scatter_dimension=0, tiled=True)  44.3 us
    all_gather x1, blocking collectives, per_device(): gathered = lax.all_gather(by_group, 'r', axis=1, tiled=True)  24.4 us
    ppermute x4, starting transfers between devices, passed_along(): return lax.ppermute(value, axis, pairs)  8.13 us
    all_to_all x1, starting transfers between devices, per_device(): lax.all_to_all(own_kv, 'y', split_axis=1, concat_axis=1, tiled=True)  7.28 us
    all_to_all x1, waiting for transfers between devices, per_device(): lax.all_to_all(summed, 'y', split_axis=2, concat_axis=2, tiled=True)  6.54 us
    all_to_all x1, starting transfers between devices, per_device(): lax.all_to_all(summed, 'y', split_axis=2, concat_axis=2, tiled=True)  5.96 us
    ppermute x4, waiting for transfers between devices, passed_along(): return lax.ppermute(value, axis, pairs)  4.72 us
    all_to_all x1, waiting for transfers between devices, per_device(): lax.all_to_all(own_kv, 'y', split_axis=1, concat_axis=1, tiled=True)  4.02 us
  transfers between devices with their start and end apart: 7, of which 5 were waited for; matrix products, arithmetic and copies ran while one was open for 5% of the time, Pallas kernels for 0%

profile of v3, /device:TPU:5, one launch (start us, length us, event | category | flops | bytes accessed | tf_op | source)
XLA Modules:
  0.0 136.7 jit_solution(5620748098246440404)
XLA Ops:
  7.2 0.8 maximum_bitcast_fusion
  8.0 0.7 copy.35
  8.7 7.3 %all-to-all-start = ((bf16[2,8,3200]{2,0,1:T(2,128)(2,1)}), bf16[2,8,3200]{2,0,1:T(2,128)(2,1)S(1)}, u32[]{:S(2)}, u32[]{:S(2)}) async-start(bf16[2,8,3200]{2,0,1:T(2,128)(2,1)} %copy.35), calls=%async_computation | async-start | bytes 204800 | tf_op jit(solution)/shard_map/all_to_all | solution.py:63
  16.0 0.0 reduce-scatter.2.cloned.1.call-start
  16.1 0.8 slice_bitcast_fusion.2
  16.8 1.3 collective-permute-start
  18.1 0.8 compare_convert_fusion
  18.9 0.7 compare_bitcast_fusion
  19.6 4.0 %all-to-all-done = bf16[2,8,3200]{2,0,1:T(2,128)(2,1)S(1)} async-done(((bf16[2,8,3200]{2,0,1:T(2,128)(2,1)}), bf16[2,8,3200]{2,0,1:T(2,128)(2,1)S(1)}, u32[]{:S(2)}, u32[]{:S(2)}) %all-to-all-start) | async-done | bytes 102432 | tf_op jit(solution)/shard_map/all_to_all | solution.py:63
  23.6 24.4 %all_gather.3 = bf16[2,64,3200]{2,0,1:T(2,128)(2,1)S(1)} all-gather(bf16[2,8,3200]{2,0,1:T(2,128)(2,1)S(1)} %all-to-all-done), channel_id=1, replica_groups=mesh['seq'=16,'y'=8,'r'=8] {'r'}, dimensions={1}, use_global_device_ids=true | all-gather | bytes 921600 | tf_op jit(solution)/shard_map/all_gather | solution.py:64
  48.0 0.1 copy.36
  48.1 0.4 reshape.58
  48.5 0.0 copy-start
  48.5 0.1 fusion.36
  48.6 0.2 copy.37
  48.8 0.6 copy-done
  49.3 0.4 fusion.39
  49.8 0.2 copy.38
  50.0 0.4 fusion.38
  50.4 0.2 fusion.20
  50.6 0.3 fusion.24
  51.0 1.3 collective-permute-start.1
  52.3 0.3 fusion.15
  52.6 1.3 collective-permute-done.1
  54.0 0.1 slice_select_fusion
  54.1 1.1 multiply_reduce_fusion
  55.2 0.6 fusion.3
  55.8 0.4 fusion.10
  56.3 1.3 collective-permute-start.2
  57.6 0.4 fusion.14
  57.9 3.4 %collective-permute-done.2 = f32[3,128]{1,0:T(4,128)S(1)} collective-permute-done((f32[3,128]{1,0:T(4,128)S(1)}, f32[3,128]{1,0:T(4,128)S(1)}, u32[]{:S(2)}, u32[]{:S(2)}) %collective-permute-start.2) | collective-permute-done | bytes 1568 | tf_op jit(solution)/shard_map/ppermute | solution.py:16
  61.3 0.3 fusion.6
  61.7 0.3 fusion.9
  61.9 0.3 fusion.13
  62.2 0.1 copy_bitcast_fusion
  62.3 1.8 %reshape.63 = bf16[64,6400]{1,0:T(8,128)(2,1)} reshape(bf16[8,2,25,8,128]{4,3,2,1,0:T(8,128)(2,1)S(1)} %copy_bitcast_fusion) | data formatting | bytes 1638400 | tf_op jit(solution)/shard_map/reshape | solution.py:144
  64.1 0.0 reduce-scatter.2.cloned.1.call-update
  64.2 0.3 fusion.40
  64.5 4.3 %collective-permute-start.3 = (f32[128,128]{1,0:T(8,128)S(1)}, f32[128,128]{1,0:T(8,128)S(1)}, u32[]{:S(2)}, u32[]{:S(2)}) collective-permute-start(f32[128,128]{1,0:T(8,128)S(1)} %fusion.40), channel_id=1, source_target_pairs={{0,64},{64,128},{128,192},{192,256},{256,320},{320,384},{384,448},... | collective-permute-start | bytes 196616 | tf_op jit(solution)/shard_map/ppermute | solution.py:16
  68.7 44.3 %reduce-scatter.2.cloned.1.call-done = bf16[8,6400]{1,0:T(8,128)(2,1)} async-done(((bf16[64,6400]{1,0:T(8,128)(2,1)}), bf16[8,6400]{1,0:T(8,128)(2,1)}) %reduce-scatter.2.cloned.1.call-update) | async-done | bytes 102416 | tf_op jit(solution)/shard_map/reduce_scatter | solution.py:145
  113.1 1.1 reshape.64
  114.1 0.7 copy.42
  114.9 6.0 %all-to-all-start.1 = ((bf16[2,25,8,128]{3,0,1,2:T(2,128)(2,1)}), bf16[2,25,8,128]{3,0,1,2:T(2,128)(2,1)S(1)}, u32[]{:S(2)}, u32[]{:S(2)}) async-start(bf16[2,25,8,128]{3,0,1,2:T(2,128)(2,1)} %copy.42), calls=%async_computation.2 | async-start | bytes 204800 | tf_op jit(solution)/shard_map/all_to_all | solution.py:147
  120.8 1.1 add_convert_fusion
  121.9 6.5 %all-to-all-done.1 = bf16[2,25,8,128]{3,0,1,2:T(2,128)(2,1)S(1)} async-done(((bf16[2,25,8,128]{3,0,1,2:T(2,128)(2,1)}), bf16[2,25,8,128]{3,0,1,2:T(2,128)(2,1)S(1)}, u32[]{:S(2)}, u32[]{:S(2)}) %all-to-all-start.1) | async-done | bytes 102432 | tf_op jit(solution)/shard_map/all_to_all | solution.py:147
  128.4 0.1 fusion.37
  128.6 0.6 copy.43
  129.2 0.6 copy.44
  (16 shorter events, 0.1 us)
Async XLA Ops:
  8.7 14.9 %all-to-all-start = ((bf16[2,8,3200]{2,0,1:T(2,128)(2,1)}), bf16[2,8,3200]{2,0,1:T(2,128)(2,1)S(1)}, u32[]{:S(2)}, u32[]{:S(2)}) async-start(bf16[2,8,3200]{2,0,1:T(2,128)(2,1)} %copy.35), calls=%async_computation | async-start | bytes 204800 | tf_op jit(solution)/shard_map/all_to_all | solution.py:63
  16.0 97.1 %reduce-scatter.2.cloned.1.call-start = ((), (), s32[]{:S(2)}) async-start(), calls=%async_computation.3 | async-start | bytes 921600 | tf_op jit(solution)/shard_map/reduce_scatter | solution.py:145
  16.8 33.1 %collective-permute-start = (bf16[2,128,128]{2,1,0:T(8,128)(2,1)S(1)}, bf16[2,128,128]{2,1,0:T(8,128)(2,1)S(1)}, u32[]{:S(2)}, u32[]{:S(2)}) collective-permute-start(bf16[2,128,128]{2,1,0:T(8,128)(2,1)S(1)} %pad_maximum_fusion.2), channel_id=1, source_target_pairs={{64,0},{128,64},{192,128},{256,192},{320,256},{384,320},{448,384},... | collective-permute-start | bytes 196616 | tf_op jit(solution)/shard_map/ppermute | solution.py:16
  48.5 0.8 copy-start
  50.6 3.3 %copy-start.2 = (s32[256,2]{0,1:T(2,128)S(1)}, s32[256,2]{0,1:T(2,128)}, u32[]{:S(2)}) copy-start(s32[256,2]{0,1:T(2,128)} %param.9) | copy-start | bytes 6148
  50.6 3.5 %copy-start.1 = (bf16[256,128]{1,0:T(8,128)(2,1)S(1)}, bf16[256,128]{1,0:T(8,128)(2,1)}, u32[]{:S(2)}) copy-start(bf16[256,128]{1,0:T(8,128)(2,1)} %param.8) | copy-start | bytes 196612
  51.0 2.9 %collective-permute-start.1 = (f32[130,128]{1,0:T(8,128)S(1)}, f32[130,128]{1,0:T(8,128)S(1)}, u32[]{:S(2)}, u32[]{:S(2)}) collective-permute-start(f32[130,128]{1,0:T(8,128)S(1)} %pad_maximum_fusion.1), channel_id=1, source_target_pairs={{0,64},{64,128},{128,192},{192,256},{256,320},{320,384},{384,448},... | collective-permute-start | bytes 199688 | tf_op jit(solution)/shard_map/ppermute | solution.py:16
  56.3 5.0 %collective-permute-start.2 = (f32[3,128]{1,0:T(4,128)S(1)}, f32[3,128]{1,0:T(4,128)S(1)}, u32[]{:S(2)}, u32[]{:S(2)}) collective-permute-start(f32[3,128]{1,0:T(4,128)S(1)} %pad_maximum_fusion.3), channel_id=1, source_target_pairs={{64,0},{128,64},{192,128},{256,192},{320,256},{384,320},{448,384},... | collective-permute-start | bytes 4616 | tf_op jit(solution)/shard_map/ppermute | solution.py:16
  64.5 56.3 %collective-permute-start.3 = (f32[128,128]{1,0:T(8,128)S(1)}, f32[128,128]{1,0:T(8,128)S(1)}, u32[]{:S(2)}, u32[]{:S(2)}) collective-permute-start(f32[128,128]{1,0:T(8,128)S(1)} %fusion.40), channel_id=1, source_target_pairs={{0,64},{64,128},{128,192},{192,256},{256,320},{320,384},{384,448},... | collective-permute-start | bytes 196616 | tf_op jit(solution)/shard_map/ppermute | solution.py:16
  114.9 13.6 %all-to-all-start.1 = ((bf16[2,25,8,128]{3,0,1,2:T(2,128)(2,1)}), bf16[2,25,8,128]{3,0,1,2:T(2,128)(2,1)S(1)}, u32[]{:S(2)}, u32[]{:S(2)}) async-start(bf16[2,25,8,128]{3,0,1,2:T(2,128)(2,1)} %copy.42), calls=%async_computation.2 | async-start | bytes 204800 | tf_op jit(solution)/shard_map/all_to_all | solution.py:147
Sparse Core Ops, SparseCore 0:
  64.3 48.7 reduce-scatter.1

commit v4 on v3

--- a/solution.py
+++ b/solution.py
@@ -141,9 +141,8 @@
         ]
     ).astype(jnp.bfloat16)
     parts = jnp.transpose(parts.reshape(2, rows, copies, groups, HD), (2, 0, 1, 3, 4))
-    parts = parts.reshape(blocks, -1)
-    summed = lax.psum_scatter(parts, "r", scatter_dimension=0, tiled=True)
-    summed = summed.reshape(2, rows, groups, HD)
+    parts = lax.all_to_all(parts, "r", split_axis=0, concat_axis=0, tiled=True)
+    summed = jnp.sum(parts.astype(jnp.float32), axis=0).astype(jnp.bfloat16)
     returned = lax.all_to_all(summed, "y", split_axis=2, concat_axis=2, tiled=True)
     return (attended, grad_query, returned[0][None], returned[1][None])
 

time: 137 us -> 105 us (0.77)
  the two profiles are of different devices: /device:TPU:5 before, /device:TPU:2 now
where the time goes in v4:
time: 105 us
  waiting for transfers between devices  37.7 us (36%)
  starting transfers between devices  35.3 us (34%)
  blocking collectives  15.8 us (15%)
  matrix products  5.86 us (6%)
  local copies, waits for them, and re-layouts  4.94 us (5%)
  other arithmetic  4.15 us (4%)
    all_to_all x1, waiting for transfers between devices, per_device(): parts = lax.all_to_all(parts, 'r', split_axis=0, concat_axis=0, tiled=True)  20.2 us
    ppermute x4, starting transfers between devices, passed_along(): return lax.ppermute(value, axis, pairs)  18.6 us
    all_gather x1, blocking collectives, per_device(): gathered = lax.all_gather(by_group, 'r', axis=1, tiled=True)  15.8 us
    ppermute x4, waiting for transfers between devices, passed_along(): return lax.ppermute(value, axis, pairs)  9.33 us
    all_to_all x1, waiting for transfers between devices, per_device(): lax.all_to_all(summed, 'y', split_axis=2, concat_axis=2, tiled=True)  8.17 us
    all_to_all x1, starting transfers between devices, per_device(): lax.all_to_all(own_kv, 'y', split_axis=1, concat_axis=1, tiled=True)  7.56 us
    all_to_all x1, starting transfers between devices, per_device(): lax.all_to_all(summed, 'y', split_axis=2, concat_axis=2, tiled=True)  4.96 us
    all_to_all x1, starting transfers between devices, per_device(): parts = lax.all_to_all(parts, 'r', split_axis=0, concat_axis=0, tiled=True)  4.15 us
  transfers between devices with their start and end apart: 7, of which 4 were waited for; matrix products, arithmetic and copies ran while one was open for 6% of the time, Pallas kernels for 0%

profile of v4, /device:TPU:2, one launch (start us, length us, event | category | flops | bytes accessed | tf_op | source)
XLA Modules:
  0.0 104.6 jit_solution(7485644487023534739)
XLA Ops:
  0.6 0.8 maximum_bitcast_fusion
  1.5 0.7 copy.31
  2.2 7.6 %all-to-all-start = ((bf16[2,8,3200]{2,0,1:T(2,128)(2,1)}), bf16[2,8,3200]{2,0,1:T(2,128)(2,1)S(1)}, u32[]{:S(2)}, u32[]{:S(2)}) async-start(bf16[2,8,3200]{2,0,1:T(2,128)(2,1)} %copy.31), calls=%async_computation | async-start | bytes 204800 | tf_op jit(solution)/shard_map/all_to_all | solution.py:63
  9.7 0.8 slice_bitcast_fusion.2
  10.5 10.9 %collective-permute-start = (bf16[2,128,128]{2,1,0:T(8,128)(2,1)S(1)}, bf16[2,128,128]{2,1,0:T(8,128)(2,1)S(1)}, u32[]{:S(2)}, u32[]{:S(2)}) collective-permute-start(bf16[2,128,128]{2,1,0:T(8,128)(2,1)S(1)} %pad_maximum_fusion.2), channel_id=1, source_target_pairs={{64,0},{128,64},{192,128},{256,192},{320,256},{384,320},{448,384},... | collective-permute-start | bytes 196616 | tf_op jit(solution)/shard_map/ppermute | solution.py:16
  21.5 0.8 compare_convert_fusion
  22.2 0.7 compare_bitcast_fusion
  22.9 0.0 all-to-all-done
  22.9 15.8 %all_gather.3 = bf16[2,64,3200]{2,0,1:T(2,128)(2,1)S(1)} all-gather(bf16[2,8,3200]{2,0,1:T(2,128)(2,1)S(1)} %all-to-all-done), channel_id=1, replica_groups=mesh['seq'=16,'y'=8,'r'=8] {'r'}, dimensions={1}, use_global_device_ids=true | all-gather | bytes 921600 | tf_op jit(solution)/shard_map/all_gather | solution.py:64
  38.7 0.1 copy.32
  38.8 0.4 reshape.52
  39.2 0.0 copy-start
  39.2 0.1 fusion.36
  39.3 0.2 copy.33
  39.5 0.6 copy-done
  40.1 0.4 fusion.39
  40.5 0.2 copy.34
  40.7 0.0 collective-permute-done
  40.7 0.4 fusion.38
  41.1 0.2 fusion.20
  41.3 0.0 copy-start.1
  41.3 0.3 fusion.24
  41.7 3.9 %collective-permute-start.1 = (f32[130,128]{1,0:T(8,128)S(1)}, f32[130,128]{1,0:T(8,128)S(1)}, u32[]{:S(2)}, u32[]{:S(2)}) collective-permute-start(f32[130,128]{1,0:T(8,128)S(1)} %pad_maximum_fusion.1), channel_id=1, source_target_pairs={{0,64},{64,128},{128,192},{192,256},{256,320},{320,384},{384,448},... | collective-permute-start | bytes 199688 | tf_op jit(solution)/shard_map/ppermute | solution.py:16
  45.6 0.3 fusion.15
  45.9 5.2 %collective-permute-done.1 = f32[130,128]{1,0:T(8,128)S(1)} collective-permute-done((f32[130,128]{1,0:T(8,128)S(1)}, f32[130,128]{1,0:T(8,128)S(1)}, u32[]{:S(2)}, u32[]{:S(2)}) %collective-permute-start.1) | collective-permute-done | bytes 66592 | tf_op jit(solution)/shard_map/ppermute | solution.py:16
  51.2 0.1 slice_select_fusion
  51.3 1.1 %multiply_reduce_fusion = (f32[256]{0:T(256)S(1)}, bf16[256,128]{1,0:T(8,128)(2,1)}) fusion(bf16[256,128]{1,0:T(8,128)(2,1)S(1)} %copy-done.1, f32[256]{0:T(256)S(1)} %get-tuple-element.16, f32[128,128]{1,0:T(8,128)S(1)} %slice_select_fusion, f32[256]{0:T(256)S(1)} %get-tuple-element.18, bf16[1600,128]{1,0:T(8,128)(2,1)S(1)} %bitcast.82, ...), kind=kOutput, calls=%fused_computation.42 | convolution fusion | flops 106004224 | bytes 2250752 | tf_op jit(solution)/shard_map/dot_general | solution.py:27
  52.4 0.6 fusion.3
  53.0 0.4 fusion.10
  53.4 1.9 %collective-permute-start.2 = (f32[3,128]{1,0:T(4,128)S(1)}, f32[3,128]{1,0:T(4,128)S(1)}, u32[]{:S(2)}, u32[]{:S(2)}) collective-permute-start(f32[3,128]{1,0:T(4,128)S(1)} %pad_maximum_fusion.3), channel_id=1, source_target_pairs={{64,0},{128,64},{192,128},{256,192},{320,256},{384,320},{448,384},... | collective-permute-start | bytes 4616 | tf_op jit(solution)/shard_map/ppermute | solution.py:16
  55.3 0.4 fusion.14
  55.7 4.1 %collective-permute-done.2 = f32[3,128]{1,0:T(4,128)S(1)} collective-permute-done((f32[3,128]{1,0:T(4,128)S(1)}, f32[3,128]{1,0:T(4,128)S(1)}, u32[]{:S(2)}, u32[]{:S(2)}) %collective-permute-start.2) | collective-permute-done | bytes 1568 | tf_op jit(solution)/shard_map/ppermute | solution.py:16
  59.8 0.3 fusion.6
  60.1 0.3 fusion.9
  60.4 0.3 fusion.13
  60.7 1.0 copy_bitcast_fusion
  61.7 4.2 %all-to-all-start.1 = ((bf16[8,2,25,8,128]{4,3,2,1,0:T(8,128)(2,1)}), bf16[8,2,25,8,128]{4,3,2,1,0:T(8,128)(2,1)S(1)}, u32[]{:S(2)}, u32[]{:S(2)}) async-start(bf16[8,2,25,8,128]{4,3,2,1,0:T(8,128)(2,1)} %copy_bitcast_fusion), calls=%async_computation.1 | async-start | bytes 1638400 | tf_op jit(solution)/shard_map/all_to_all | solution.py:144
  65.9 0.3 fusion.40
  66.2 1.9 %collective-permute-start.3 = (f32[128,128]{1,0:T(8,128)S(1)}, f32[128,128]{1,0:T(8,128)S(1)}, u32[]{:S(2)}, u32[]{:S(2)}) collective-permute-start(f32[128,128]{1,0:T(8,128)S(1)} %fusion.40), channel_id=1, source_target_pairs={{0,64},{64,128},{128,192},{192,256},{256,320},{320,384},{384,448},... | collective-permute-start | bytes 196616 | tf_op jit(solution)/shard_map/ppermute | solution.py:16
  68.1 20.2 %all-to-all-done.1 = bf16[8,2,25,8,128]{4,3,2,1,0:T(8,128)(2,1)S(1)} async-done(((bf16[8,2,25,8,128]{4,3,2,1,0:T(8,128)(2,1)}), bf16[8,2,25,8,128]{4,3,2,1,0:T(8,128)(2,1)S(1)}, u32[]{:S(2)}, u32[]{:S(2)}) %all-to-all-start.1) | async-done | bytes 819232 | tf_op jit(solution)/shard_map/all_to_all | solution.py:144
  88.3 0.1 reduce_sum.42
  88.4 0.7 copy.38
  89.1 5.0 %all-to-all-start.2 = ((bf16[2,25,8,128]{3,1,0,2:T(8,128)(2,1)}), bf16[2,25,8,128]{3,1,0,2:T(8,128)(2,1)S(1)}, u32[]{:S(2)}, u32[]{:S(2)}) async-start(bf16[2,25,8,128]{3,1,0,2:T(8,128)(2,1)} %copy.38), calls=%async_computation.2 | async-start | bytes 262144 | tf_op jit(solution)/shard_map/all_to_all | solution.py:146
  94.0 0.0 collective-permute-done.3
  94.0 1.1 %add_convert_fusion = bf16[256,128]{1,0:T(8,128)(2,1)} fusion(f32[128,128]{1,0:T(8,128)S(1)} %collective-permute-done.3, bf16[1600,256]{1,0:T(8,128)(2,1)S(1)} %fusion.3, bf16[1600,128]{1,0:T(8,128)(2,1)S(1)} %bitcast.79), kind=kOutput, calls=%fused_computation.41 | convolution fusion | flops 104923136 | bytes 1359872 | tf_op jit(solution)/shard_map/dot_general | solution.py:40
  95.1 8.2 %all-to-all-done.2 = bf16[2,25,8,128]{3,1,0,2:T(8,128)(2,1)S(1)} async-done(((bf16[2,25,8,128]{3,1,0,2:T(8,128)(2,1)}), bf16[2,25,8,128]{3,1,0,2:T(8,128)(2,1)S(1)}, u32[]{:S(2)}, u32[]{:S(2)}) %all-to-all-start.2) | async-done | bytes 102432 | tf_op jit(solution)/shard_map/all_to_all | solution.py:146
  103.3 0.6 copy.39
  103.9 0.6 copy.40
  (14 shorter events, 0.1 us)
Async XLA Ops:
  2.2 20.7 %all-to-all-start = ((bf16[2,8,3200]{2,0,1:T(2,128)(2,1)}), bf16[2,8,3200]{2,0,1:T(2,128)(2,1)S(1)}, u32[]{:S(2)}, u32[]{:S(2)}) async-start(bf16[2,8,3200]{2,0,1:T(2,128)(2,1)} %copy.31), calls=%async_computation | async-start | bytes 204800 | tf_op jit(solution)/shard_map/all_to_all | solution.py:63
  10.5 30.2 %collective-permute-start = (bf16[2,128,128]{2,1,0:T(8,128)(2,1)S(1)}, bf16[2,128,128]{2,1,0:T(8,128)(2,1)S(1)}, u32[]{:S(2)}, u32[]{:S(2)}) collective-permute-start(bf16[2,128,128]{2,1,0:T(8,128)(2,1)S(1)} %pad_maximum_fusion.2), channel_id=1, source_target_pairs={{64,0},{128,64},{192,128},{256,192},{320,256},{384,320},{448,384},... | collective-permute-start | bytes 196616 | tf_op jit(solution)/shard_map/ppermute | solution.py:16
  39.2 0.8 copy-start
  41.3 9.8 %copy-start.2 = (s32[256,2]{0,1:T(2,128)S(1)}, s32[256,2]{0,1:T(2,128)}, u32[]{:S(2)}) copy-start(s32[256,2]{0,1:T(2,128)} %param.9) | copy-start | bytes 6148
  41.3 9.9 %copy-start.1 = (bf16[256,128]{1,0:T(8,128)(2,1)S(1)}, bf16[256,128]{1,0:T(8,128)(2,1)}, u32[]{:S(2)}) copy-start(bf16[256,128]{1,0:T(8,128)(2,1)} %param.8) | copy-start | bytes 196612
  41.7 9.4 %collective-permute-start.1 = (f32[130,128]{1,0:T(8,128)S(1)}, f32[130,128]{1,0:T(8,128)S(1)}, u32[]{:S(2)}, u32[]{:S(2)}) collective-permute-start(f32[130,128]{1,0:T(8,128)S(1)} %pad_maximum_fusion.1), channel_id=1, source_target_pairs={{0,64},{64,128},{128,192},{192,256},{256,320},{320,384},{384,448},... | collective-permute-start | bytes 199688 | tf_op jit(solution)/shard_map/ppermute | solution.py:16
  53.4 6.4 %collective-permute-start.2 = (f32[3,128]{1,0:T(4,128)S(1)}, f32[3,128]{1,0:T(4,128)S(1)}, u32[]{:S(2)}, u32[]{:S(2)}) collective-permute-start(f32[3,128]{1,0:T(4,128)S(1)} %pad_maximum_fusion.3), channel_id=1, source_target_pairs={{64,0},{128,64},{192,128},{256,192},{320,256},{384,320},{448,384},... | collective-permute-start | bytes 4616 | tf_op jit(solution)/shard_map/ppermute | solution.py:16
  61.7 26.6 %all-to-all-start.1 = ((bf16[8,2,25,8,128]{4,3,2,1,0:T(8,128)(2,1)}), bf16[8,2,25,8,128]{4,3,2,1,0:T(8,128)(2,1)S(1)}, u32[]{:S(2)}, u32[]{:S(2)}) async-start(bf16[8,2,25,8,128]{4,3,2,1,0:T(8,128)(2,1)} %copy_bitcast_fusion), calls=%async_computation.1 | async-start | bytes 1638400 | tf_op jit(solution)/shard_map/all_to_all | solution.py:144
  66.2 27.8 %collective-permute-start.3 = (f32[128,128]{1,0:T(8,128)S(1)}, f32[128,128]{1,0:T(8,128)S(1)}, u32[]{:S(2)}, u32[]{:S(2)}) collective-permute-start(f32[128,128]{1,0:T(8,128)S(1)} %fusion.40), channel_id=1, source_target_pairs={{0,64},{64,128},{128,192},{192,256},{256,320},{320,384},{384,448},... | collective-permute-start | bytes 196616 | tf_op jit(solution)/shard_map/ppermute | solution.py:16
  89.1 14.2 %all-to-all-start.2 = ((bf16[2,25,8,128]{3,1,0,2:T(8,128)(2,1)}), bf16[2,25,8,128]{3,1,0,2:T(8,128)(2,1)S(1)}, u32[]{:S(2)}, u32[]{:S(2)}) async-start(bf16[2,25,8,128]{3,1,0,2:T(8,128)(2,1)} %copy.38), calls=%async_computation.2 | async-start | bytes 262144 | tf_op jit(solution)/shard_map/all_to_all | solution.py:146

commit v5 on v4

--- a/solution.py
+++ b/solution.py
@@ -14,6 +14,10 @@
     length = lax.axis_size(axis)
     pairs = [(i, i + by) for i in range(length) if 0 <= i + by < length]
     return lax.ppermute(value, axis, pairs)
+
+
+def partner(value):
+    return lax.ppermute(value, "c", [(0, 1), (1, 0)])
 
 
 def block_forward(query_rows, key_rows, value_rows, keep_mask):
@@ -49,8 +53,8 @@
 
 def per_device(queries, keys, values, cotangent, mask):
     groups = lax.axis_size("y")
-    copies = lax.axis_size("r")
-    blocks = groups * copies
+    far = lax.axis_size("xh")
+    blocks = groups * far * lax.axis_size("c")
     rows = keys.shape[1]
     tokens = queries.shape[0]
     half = tokens // 2
@@ -61,7 +65,8 @@
     own_kv = jnp.stack([keys[0], values[0]])
     own_kv = jnp.transpose(own_kv, (0, 2, 1, 3)).reshape(2, KVH, rows * HD)
     by_group = lax.all_to_all(own_kv, "y", split_axis=1, concat_axis=1, tiled=True)
-    gathered = lax.all_gather(by_group, "r", axis=1, tiled=True)
+    across = lax.all_gather(by_group, "xh", axis=1, tiled=True)
+    gathered = jnp.concatenate([across, partner(across)], axis=1)
     gathered = jnp.transpose(gathered.reshape(2, blocks, rows, HD), (0, 2, 1, 3))
     gathered = gathered.reshape(2, rows * blocks, HD)
     key_own, value_own = gathered[0], gathered[1]
@@ -140,19 +145,24 @@
             gv_own.astype(jnp.float32) + gv_next.astype(jnp.float32),
         ]
     ).astype(jnp.bfloat16)
-    parts = jnp.transpose(parts.reshape(2, rows, copies, groups, HD), (2, 0, 1, 3, 4))
-    parts = lax.all_to_all(parts, "r", split_axis=0, concat_axis=0, tiled=True)
-    summed = jnp.sum(parts.astype(jnp.float32), axis=0).astype(jnp.bfloat16)
-    returned = lax.all_to_all(summed, "y", split_axis=2, concat_axis=2, tiled=True)
+    parts = parts.reshape(2, rows, 2, far, groups, HD)
+    summed = parts[:, :, 0].astype(jnp.float32) + partner(parts[:, :, 1]).astype(jnp.float32)
+    summed = jnp.transpose(summed.astype(jnp.bfloat16), (2, 0, 1, 3, 4))
+    summed = lax.all_to_all(summed, "xh", split_axis=0, concat_axis=0, tiled=True)
+    summed = jnp.sum(summed.astype(jnp.float32), axis=0).astype(jnp.bfloat16)
+    summed = jnp.transpose(summed, (2, 0, 1, 3))
+    returned = lax.all_to_all(summed, "y", split_axis=0, concat_axis=0, tiled=True)
+    returned = jnp.transpose(returned, (1, 2, 0, 3))
     return (attended, grad_query, returned[0][None], returned[1][None])
 
 
 def solution(mesh):
     seq_devices, head_devices = mesh.devices.shape
     split = Mesh(
-        mesh.devices.reshape(seq_devices, KVH, head_devices // KVH), ("seq", "y", "r")
+        mesh.devices.reshape(seq_devices, KVH, head_devices // KVH // 2, 2),
+        ("seq", "y", "xh", "c"),
     )
-    heads = ("y", "r")
+    heads = ("y", "xh", "c")
     return jax.shard_map(
         per_device,
         mesh=split,

time: 105 us -> 99.6 us (0.949)
  waiting for transfers between devices: 37.7 us -> 28.4 us
  starting transfers between devices: 35.3 us -> 39.2 us
    all_to_all x2, waiting for transfers between devices: 28.3 us -> 18.9 us  [the longest x1 11.2 us: per_device(): lax.all_to_all(summed, 'xh', split_axis=0, concat_axis=0, tiled=True)]
    ppermute x0 -> x2, starting transfers between devices: none -> 3.83 us  [partner(): return lax.ppermute(value, 'c', [(0, 1), (1, 0)])]
    ppermute x0 -> x2, waiting for transfers between devices: none -> 1.96 us  [partner(): return lax.ppermute(value, 'c', [(0, 1), (1, 0)])]
    ppermute x4, waiting for transfers between devices: 9.33 us -> 7.62 us  [passed_along(): return lax.ppermute(value, axis, pairs)]
    ppermute x4, starting transfers between devices: 18.6 us -> 19.8 us  [passed_along(): return lax.ppermute(value, axis, pairs)]
    all_to_all x2, starting transfers between devices: 9.11 us -> 8.02 us  [the longest x1 4.09 us: per_device(): lax.all_to_all(summed, 'xh', split_axis=0, concat_axis=0, tiled=True)]
    concatenate x0 -> x1, other arithmetic: none -> 1.06 us  [per_device(): gathered = jnp.concatenate([across, partner(across)], axis=1)]
  transfers between devices with their start and end apart: 7 -> 9, of which waited for: 4 -> 6; matrix products, arithmetic and copies ran while one was open for 6% -> 8% of each run, Pallas kernels for 0% -> 0%
where the time goes in v5:
time: 99.6 us; the launch traced here: 98.9 us
  starting transfers between devices  39.2 us (39%)
  waiting for transfers between devices  28.4 us (29%)
  blocking collectives  14.9 us (15%)
  matrix products  5.88 us (6%)
  other arithmetic  5.06 us (5%)
  local copies, waits for them, and re-layouts  4.6 us (5%)
    ppermute x4, starting transfers between devices, passed_along(): return lax.ppermute(value, axis, pairs)  19.8 us
    all_gather x1, blocking collectives, per_device(): across = lax.all_gather(by_group, 'xh', axis=1, tiled=True)  14.9 us
    all_to_all x1, waiting for transfers between devices, per_device(): lax.all_to_all(summed, 'xh', split_axis=0, concat_axis=0, tiled=True)  11.2 us
    all_to_all x1, waiting for transfers between devices, per_device(): lax.all_to_all(summed, 'y', split_axis=0, concat_axis=0, tiled=True)  7.69 us
    ppermute x4, waiting for transfers between devices, passed_along(): return lax.ppermute(value, axis, pairs)  7.62 us
    all_to_all x1, starting transfers between devices, per_device(): lax.all_to_all(own_kv, 'y', split_axis=1, concat_axis=1, tiled=True)  7.56 us
    all_to_all x1, starting transfers between devices, per_device(): lax.all_to_all(summed, 'xh', split_axis=0, concat_axis=0, tiled=True)  4.09 us
    all_to_all x1, starting transfers between devices, per_device(): lax.all_to_all(summed, 'y', split_axis=0, concat_axis=0, tiled=True)  3.93 us
  transfers between devices with their start and end apart: 9, of which 6 were waited for; matrix products, arithmetic and copies ran while one was open for 8% of the time, Pallas kernels for 0%

profile of v5, /device:TPU:2, one launch (start us, length us, event | category | flops | bytes accessed | tf_op | source)
XLA Modules:
  0.0 98.9 jit_solution(13095734902284195294)
XLA Ops:
  0.6 0.8 maximum_bitcast_fusion
  1.5 0.7 copy.33
  2.2 7.6 %all-to-all-start = ((bf16[2,8,3200]{2,0,1:T(2,128)(2,1)}), bf16[2,8,3200]{2,0,1:T(2,128)(2,1)S(1)}, u32[]{:S(2)}, u32[]{:S(2)}) async-start(bf16[2,8,3200]{2,0,1:T(2,128)(2,1)} %copy.33), calls=%async_computation | async-start | bytes 204800 | tf_op jit(solution)/shard_map/all_to_all | solution.py:67
  9.7 0.8 slice_bitcast_fusion.2
  10.5 10.9 %collective-permute-start.1 = (bf16[2,128,128]{2,1,0:T(8,128)(2,1)S(1)}, bf16[2,128,128]{2,1,0:T(8,128)(2,1)S(1)}, u32[]{:S(2)}, u32[]{:S(2)}) collective-permute-start(bf16[2,128,128]{2,1,0:T(8,128)(2,1)S(1)} %pad_maximum_fusion.3), channel_id=1, source_target_pairs={{64,0},{128,64},{192,128},{256,192},{320,256},{384,320},{448,384},... | collective-permute-start | bytes 196616 | tf_op jit(solution)/shard_map/ppermute | solution.py:16
  21.5 14.9 %all_gather.3 = bf16[2,32,3200]{2,0,1:T(2,128)(2,1)S(1)} all-gather(bf16[2,8,3200]{2,0,1:T(2,128)(2,1)S(1)} %all-to-all-done), channel_id=1, replica_groups=mesh['seq'=16,'y'=8,'xh'=4,'c'=2] {'xh'}, dimensions={1}, use_global_device_ids=true | all-gather | bytes 512000 | tf_op jit(solution)/shard_map/all_gather | solution.py:68
  36.3 1.9 %collective-permute-start = (bf16[2,32,3200]{2,0,1:T(2,128)(2,1)S(1)}, bf16[2,32,3200]{2,0,1:T(2,128)(2,1)S(1)}, u32[]{:S(2)}, u32[]{:S(2)}) collective-permute-start(bf16[2,32,3200]{2,0,1:T(2,128)(2,1)S(1)} %all_gather.3), channel_id=1, source_target_pairs={{0,1},{1,0},{2,3},{3,2},{4,5},{5,4},{6,7},{7,6},{8,9},{9,8},{10,11... | collective-permute-start | bytes 1228808 | tf_op jit(solution)/shard_map/ppermute | solution.py:20
  38.2 0.7 compare_bitcast_fusion
  38.9 0.8 compare_convert_fusion
  39.7 0.2 collective-permute-done
  40.0 1.1 %pad_maximum_fusion = bf16[2,64,3200]{2,0,1:T(2,128)(2,1)S(1)} fusion(bf16[2,32,3200]{2,0,1:T(2,128)(2,1)S(1)} %collective-permute-done, bf16[2,32,3200]{2,0,1:T(2,128)(2,1)S(1)} %all_gather.3), kind=kLoop, calls=%fused_computation.28 | loop fusion | flops 409600 | bytes 1638400 | tf_op jit(solution)/shard_map/concatenate | solution.py:69
  41.0 0.1 copy.34
  41.1 0.4 reshape.54
  41.6 0.2 copy.35
  41.8 0.2 copy.36
  42.0 0.4 fusion.41
  42.4 0.2 fusion.21
  42.6 0.3 fusion.25
  42.9 5.0 %collective-permute-start.2 = (f32[130,128]{1,0:T(8,128)S(1)}, f32[130,128]{1,0:T(8,128)S(1)}, u32[]{:S(2)}, u32[]{:S(2)}) collective-permute-start(f32[130,128]{1,0:T(8,128)S(1)} %pad_maximum_fusion.2), channel_id=1, source_target_pairs={{0,64},{64,128},{128,192},{192,256},{256,320},{320,384},{384,448},... | collective-permute-start | bytes 199688 | tf_op jit(solution)/shard_map/ppermute | solution.py:16
  48.0 0.4 fusion.42
  48.4 0.3 fusion.15
  48.8 3.5 %collective-permute-done.2 = f32[130,128]{1,0:T(8,128)S(1)} collective-permute-done((f32[130,128]{1,0:T(8,128)S(1)}, f32[130,128]{1,0:T(8,128)S(1)}, u32[]{:S(2)}, u32[]{:S(2)}) %collective-permute-start.2) | collective-permute-done | bytes 66592 | tf_op jit(solution)/shard_map/ppermute | solution.py:16
  52.4 0.4 fusion.10
  52.8 0.1 slice_select_fusion
  52.9 1.1 %multiply_reduce_fusion = (f32[256]{0:T(256)S(1)}, bf16[256,128]{1,0:T(8,128)(2,1)}) fusion(bf16[256,128]{1,0:T(8,128)(2,1)S(1)} %copy-done.1, f32[256]{0:T(256)S(1)} %get-tuple-element.16, f32[128,128]{1,0:T(8,128)S(1)} %slice_select_fusion, f32[256]{0:T(256)S(1)} %get-tuple-element.18, bf16[1600,128]{1,0:T(8,128)(2,1)S(1)} %bitcast.92, ...), kind=kOutput, calls=%fused_computation.50 | convolution fusion | flops 106004224 | bytes 2250752 | tf_op jit(solution)/shard_map/dot_general | solution.py:31
  54.0 0.6 fusion.3
  54.6 1.9 %collective-permute-start.3 = (f32[3,128]{1,0:T(4,128)S(1)}, f32[3,128]{1,0:T(4,128)S(1)}, u32[]{:S(2)}, u32[]{:S(2)}) collective-permute-start(f32[3,128]{1,0:T(4,128)S(1)} %pad_maximum_fusion.4), channel_id=1, source_target_pairs={{64,0},{128,64},{192,128},{256,192},{320,256},{384,320},{448,384},... | collective-permute-start | bytes 4616 | tf_op jit(solution)/shard_map/ppermute | solution.py:16
  56.5 0.4 fusion.14
  56.9 4.1 %collective-permute-done.3 = f32[3,128]{1,0:T(4,128)S(1)} collective-permute-done((f32[3,128]{1,0:T(4,128)S(1)}, f32[3,128]{1,0:T(4,128)S(1)}, u32[]{:S(2)}, u32[]{:S(2)}) %collective-permute-start.3) | collective-permute-done | bytes 1568 | tf_op jit(solution)/shard_map/ppermute | solution.py:16
  61.0 0.3 fusion.9
  61.3 0.3 fusion.6
  61.6 0.2 fusion.13
  61.9 0.1 fusion.28
  61.9 0.1 copy.51
  62.0 1.9 %collective-permute-start.5 = (bf16[2,25,4,8,128]{4,3,1,0,2:T(8,128)(2,1)S(1)}, bf16[2,25,4,8,128]{4,3,1,0,2:T(8,128)(2,1)S(1)}, u32[]{:S(2)}, u32[]{:S(2)}) collective-permute-start(bf16[2,25,4,8,128]{4,3,1,0,2:T(8,128)(2,1)S(1)} %bitcast.98), channel_id=1, source_target_pairs={{0,1},{1,0},{2,3},{3,2},{4,5},{5,4},{6,7},{7,6},{8,9},{9,8},{10,11... | collective-permute-start | bytes 1228808 | tf_op jit(solution)/shard_map/ppermute | solution.py:20
  63.9 1.7 %collective-permute-done.5 = bf16[2,25,4,8,128]{4,3,1,0,2:T(8,128)(2,1)S(1)} collective-permute-done((bf16[2,25,4,8,128]{4,3,1,0,2:T(8,128)(2,1)S(1)}, bf16[2,25,4,8,128]{4,3,1,0,2:T(8,128)(2,1)S(1)}, u32[]{:S(2)}, u32[]{:S(2)}) %collective-permute-start.5) | collective-permute-done | bytes 409632 | tf_op jit(solution)/shard_map/ppermute | solution.py:20
  65.7 0.9 fusion.27
  66.5 4.1 %all-to-all-start.1 = ((bf16[4,2,25,8,128]{4,3,2,1,0:T(8,128)(2,1)}), bf16[4,2,25,8,128]{4,3,2,1,0:T(8,128)(2,1)S(1)}, u32[]{:S(2)}, u32[]{:S(2)}) async-start(bf16[4,2,25,8,128]{4,3,2,1,0:T(8,128)(2,1)} %fusion.27), calls=%async_computation.1 | async-start | bytes 819200 | tf_op jit(solution)/shard_map/all_to_all | solution.py:151
  70.6 0.3 fusion.43
  70.9 1.9 %collective-permute-start.4 = (f32[128,128]{1,0:T(8,128)S(1)}, f32[128,128]{1,0:T(8,128)S(1)}, u32[]{:S(2)}, u32[]{:S(2)}) collective-permute-start(f32[128,128]{1,0:T(8,128)S(1)} %fusion.43), channel_id=1, source_target_pairs={{0,64},{64,128},{128,192},{192,256},{256,320},{320,384},{384,448},... | collective-permute-start | bytes 196616 | tf_op jit(solution)/shard_map/ppermute | solution.py:16
  72.9 11.2 %all-to-all-done.1 = bf16[4,2,25,8,128]{4,3,2,1,0:T(8,128)(2,1)S(1)} async-done(((bf16[4,2,25,8,128]{4,3,2,1,0:T(8,128)(2,1)}), bf16[4,2,25,8,128]{4,3,2,1,0:T(8,128)(2,1)S(1)}, u32[]{:S(2)}, u32[]{:S(2)}) %all-to-all-start.1) | async-done | bytes 409632 | tf_op jit(solution)/shard_map/all_to_all | solution.py:151
  84.1 0.7 copy.40
  84.8 3.9 %all-to-all-start.2 = ((bf16[8,2,25,128]{3,1,2,0:T(2,128)(2,1)}), bf16[8,2,25,128]{3,1,2,0:T(2,128)(2,1)S(1)}, u32[]{:S(2)}, u32[]{:S(2)}) async-start(bf16[8,2,25,128]{3,1,2,0:T(2,128)(2,1)} %copy.40), calls=%async_computation.2 | async-start | bytes 204800 | tf_op jit(solution)/shard_map/all_to_all | solution.py:154
  88.8 1.1 %add_convert_fusion = bf16[256,128]{1,0:T(8,128)(2,1)} fusion(f32[128,128]{1,0:T(8,128)S(1)} %collective-permute-done.4, bf16[1600,256]{1,0:T(8,128)(2,1)S(1)} %fusion.3, bf16[1600,128]{1,0:T(8,128)(2,1)S(1)} %bitcast.89), kind=kOutput, calls=%fused_computation.49 | convolution fusion | flops 104923136 | bytes 1359872 | tf_op jit(solution)/shard_map/dot_general | solution.py:44
  89.8 7.7 %all-to-all-done.2 = bf16[8,2,25,128]{3,1,2,0:T(2,128)(2,1)S(1)} async-done(((bf16[8,2,25,128]{3,1,2,0:T(2,128)(2,1)}), bf16[8,2,25,128]{3,1,2,0:T(2,128)(2,1)S(1)}, u32[]{:S(2)}, u32[]{:S(2)}) %all-to-all-start.2) | async-done | bytes 102432 | tf_op jit(solution)/shard_map/all_to_all | solution.py:154
  97.5 0.1 fusion.40
  97.7 0.6 copy.41
  98.3 0.6 copy.42
  (21 shorter events, 0.2 us)
Async XLA Ops:
  2.2 19.3 %all-to-all-start = ((bf16[2,8,3200]{2,0,1:T(2,128)(2,1)}), bf16[2,8,3200]{2,0,1:T(2,128)(2,1)S(1)}, u32[]{:S(2)}, u32[]{:S(2)}) async-start(bf16[2,8,3200]{2,0,1:T(2,128)(2,1)} %copy.33), calls=%async_computation | async-start | bytes 204800 | tf_op jit(solution)/shard_map/all_to_all | solution.py:67
  10.5 31.4 %collective-permute-start.1 = (bf16[2,128,128]{2,1,0:T(8,128)(2,1)S(1)}, bf16[2,128,128]{2,1,0:T(8,128)(2,1)S(1)}, u32[]{:S(2)}, u32[]{:S(2)}) collective-permute-start(bf16[2,128,128]{2,1,0:T(8,128)(2,1)S(1)} %pad_maximum_fusion.3), channel_id=1, source_target_pairs={{64,0},{128,64},{192,128},{256,192},{320,256},{384,320},{448,384},... | collective-permute-start | bytes 196616 | tf_op jit(solution)/shard_map/ppermute | solution.py:16
  36.3 3.6 %collective-permute-start = (bf16[2,32,3200]{2,0,1:T(2,128)(2,1)S(1)}, bf16[2,32,3200]{2,0,1:T(2,128)(2,1)S(1)}, u32[]{:S(2)}, u32[]{:S(2)}) collective-permute-start(bf16[2,32,3200]{2,0,1:T(2,128)(2,1)S(1)} %all_gather.3), channel_id=1, source_target_pairs={{0,1},{1,0},{2,3},{3,2},{4,5},{5,4},{6,7},{7,6},{8,9},{9,8},{10,11... | collective-permute-start | bytes 1228808 | tf_op jit(solution)/shard_map/ppermute | solution.py:20
  42.0 6.0 %copy-start = (bf16[256,128]{1,0:T(8,128)(2,1)S(1)}, bf16[256,128]{1,0:T(8,128)(2,1)}, u32[]{:S(2)}) copy-start(bf16[256,128]{1,0:T(8,128)(2,1)} %param.5) | copy-start | bytes 196612
  42.9 9.3 %collective-permute-start.2 = (f32[130,128]{1,0:T(8,128)S(1)}, f32[130,128]{1,0:T(8,128)S(1)}, u32[]{:S(2)}, u32[]{:S(2)}) collective-permute-start(f32[130,128]{1,0:T(8,128)S(1)} %pad_maximum_fusion.2), channel_id=1, source_target_pairs={{0,64},{64,128},{128,192},{192,256},{256,320},{320,384},{384,448},... | collective-permute-start | bytes 199688 | tf_op jit(solution)/shard_map/ppermute | solution.py:16
  48.0 4.3 %copy-start.2 = (s32[256,2]{0,1:T(2,128)S(1)}, s32[256,2]{0,1:T(2,128)}, u32[]{:S(2)}) copy-start(s32[256,2]{0,1:T(2,128)} %param.9) | copy-start | bytes 6148
  48.0 4.4 %copy-start.1 = (bf16[256,128]{1,0:T(8,128)(2,1)S(1)}, bf16[256,128]{1,0:T(8,128)(2,1)}, u32[]{:S(2)}) copy-start(bf16[256,128]{1,0:T(8,128)(2,1)} %param.8) | copy-start | bytes 196612
  54.6 6.4 %collective-permute-start.3 = (f32[3,128]{1,0:T(4,128)S(1)}, f32[3,128]{1,0:T(4,128)S(1)}, u32[]{:S(2)}, u32[]{:S(2)}) collective-permute-start(f32[3,128]{1,0:T(4,128)S(1)} %pad_maximum_fusion.4), channel_id=1, source_target_pairs={{64,0},{128,64},{192,128},{256,192},{320,256},{384,320},{448,384},... | collective-permute-start | bytes 4616 | tf_op jit(solution)/shard_map/ppermute | solution.py:16
  62.0 3.6 %collective-permute-start.5 = (bf16[2,25,4,8,128]{4,3,1,0,2:T(8,128)(2,1)S(1)}, bf16[2,25,4,8,128]{4,3,1,0,2:T(8,128)(2,1)S(1)}, u32[]{:S(2)}, u32[]{:S(2)}) collective-permute-start(bf16[2,25,4,8,128]{4,3,1,0,2:T(8,128)(2,1)S(1)} %bitcast.98), channel_id=1, source_target_pairs={{0,1},{1,0},{2,3},{3,2},{4,5},{5,4},{6,7},{7,6},{8,9},{9,8},{10,11... | collective-permute-start | bytes 1228808 | tf_op jit(solution)/shard_map/ppermute | solution.py:20
  66.5 17.5 %all-to-all-start.1 = ((bf16[4,2,25,8,128]{4,3,2,1,0:T(8,128)(2,1)}), bf16[4,2,25,8,128]{4,3,2,1,0:T(8,128)(2,1)S(1)}, u32[]{:S(2)}, u32[]{:S(2)}) async-start(bf16[4,2,25,8,128]{4,3,2,1,0:T(8,128)(2,1)} %fusion.27), calls=%async_computation.1 | async-start | bytes 819200 | tf_op jit(solution)/shard_map/all_to_all | solution.py:151
  70.9 17.8 %collective-permute-start.4 = (f32[128,128]{1,0:T(8,128)S(1)}, f32[128,128]{1,0:T(8,128)S(1)}, u32[]{:S(2)}, u32[]{:S(2)}) collective-permute-start(f32[128,128]{1,0:T(8,128)S(1)} %fusion.43), channel_id=1, source_target_pairs={{0,64},{64,128},{128,192},{192,256},{256,320},{320,384},{384,448},... | collective-permute-start | bytes 196616 | tf_op jit(solution)/shard_map/ppermute | solution.py:16
  84.8 12.7 %all-to-all-start.2 = ((bf16[8,2,25,128]{3,1,2,0:T(2,128)(2,1)}), bf16[8,2,25,128]{3,1,2,0:T(2,128)(2,1)S(1)}, u32[]{:S(2)}, u32[]{:S(2)}) async-start(bf16[8,2,25,128]{3,1,2,0:T(2,128)(2,1)} %copy.40), calls=%async_computation.2 | async-start | bytes 204800 | tf_op jit(solution)/shard_map/all_to_all | solution.py:154

commit v6 on v5

--- a/solution.py
+++ b/solution.py
@@ -14,6 +14,11 @@
     length = lax.axis_size(axis)
     pairs = [(i, i + by) for i in range(length) if 0 <= i + by < length]
     return lax.ppermute(value, axis, pairs)
+
+
+def shifted(value, axis, by):
+    length = lax.axis_size(axis)
+    return lax.ppermute(value, axis, [(i, (i + by) % length) for i in range(length)])
 
 
 def partner(value):
@@ -53,8 +58,7 @@
 
 def per_device(queries, keys, values, cotangent, mask):
     groups = lax.axis_size("y")
-    far = lax.axis_size("xh")
-    blocks = groups * far * lax.axis_size("c")
+    blocks = groups * lax.axis_size("xh") * lax.axis_size("c")
     rows = keys.shape[1]
     tokens = queries.shape[0]
     half = tokens // 2
@@ -65,7 +69,10 @@
     own_kv = jnp.stack([keys[0], values[0]])
     own_kv = jnp.transpose(own_kv, (0, 2, 1, 3)).reshape(2, KVH, rows * HD)
     by_group = lax.all_to_all(own_kv, "y", split_axis=1, concat_axis=1, tiled=True)
-    across = lax.all_gather(by_group, "xh", axis=1, tiled=True)
+    far = lax.axis_size("xh")
+    across = jnp.concatenate(
+        [by_group] + [shifted(by_group, "xh", k) for k in range(1, far)], axis=1
+    )
     gathered = jnp.concatenate([across, partner(across)], axis=1)
     gathered = jnp.transpose(gathered.reshape(2, blocks, rows, HD), (0, 2, 1, 3))
     gathered = gathered.reshape(2, rows * blocks, HD)
@@ -147,9 +154,11 @@
     ).astype(jnp.bfloat16)
     parts = parts.reshape(2, rows, 2, far, groups, HD)
     summed = parts[:, :, 0].astype(jnp.float32) + partner(parts[:, :, 1]).astype(jnp.float32)
-    summed = jnp.transpose(summed.astype(jnp.bfloat16), (2, 0, 1, 3, 4))
-    summed = lax.all_to_all(summed, "xh", split_axis=0, concat_axis=0, tiled=True)
-    summed = jnp.sum(summed.astype(jnp.float32), axis=0).astype(jnp.bfloat16)
+    summed = summed.astype(jnp.bfloat16)
+    total = summed[:, :, 0].astype(jnp.float32)
+    for k in range(1, far):
+        total = total + shifted(summed[:, :, k], "xh", -k).astype(jnp.float32)
+    summed = total.astype(jnp.bfloat16)
     summed = jnp.transpose(summed, (2, 0, 1, 3))
     returned = lax.all_to_all(summed, "y", split_axis=0, concat_axis=0, tiled=True)
     returned = jnp.transpose(returned, (1, 2, 0, 3))

time: 99.6 us -> 109 us (1.094)
  the two profiles are of different devices: /device:TPU:2 before, /device:TPU:6 now
where the time goes in v6:
time: 109 us; the launch traced here: 108 us
  starting transfers between devices  52.2 us (48%)
  waiting for transfers between devices  35.8 us (33%)
  local copies, waits for them, and re-layouts  6.52 us (6%)
  other arithmetic  6.43 us (6%)
  matrix products  5.94 us (5%)
    ppermute x6, starting transfers between devices, shifted(): lax.ppermute(value, axis, [(i, (i + by) % length) for i in range(length)])  23.7 us
    ppermute x6, waiting for transfers between devices, shifted(): lax.ppermute(value, axis, [(i, (i + by) % length) for i in range(length)])  12.9 us
    ppermute x4, starting transfers between devices, passed_along(): return lax.ppermute(value, axis, pairs)  12.3 us
    ppermute x4, waiting for transfers between devices, passed_along(): return lax.ppermute(value, axis, pairs)  7.98 us
    all_to_all x1, waiting for transfers between devices, per_device(): lax.all_to_all(summed, 'y', split_axis=0, concat_axis=0, tiled=True)  7.69 us
    all_to_all x1, starting transfers between devices, per_device(): lax.all_to_all(own_kv, 'y', split_axis=1, concat_axis=1, tiled=True)  7.56 us
    all_to_all x1, starting transfers between devices, per_device(): lax.all_to_all(summed, 'y', split_axis=0, concat_axis=0, tiled=True)  4.78 us
    all_to_all x1, waiting for transfers between devices, per_device(): lax.all_to_all(own_kv, 'y', split_axis=1, concat_axis=1, tiled=True)  4.07 us
  transfers between devices with their start and end apart: 14, of which 10 were waited for; matrix products, arithmetic and copies ran while one was open for 7% of the time, Pallas kernels for 0%

profile of v6, /device:TPU:6, one launch (start us, length us, event | category | flops | bytes accessed | tf_op | source)
XLA Modules:
  0.0 107.8 jit_solution(6527203609549094307)
XLA Ops:
  0.6 0.8 maximum_bitcast_fusion
  1.5 0.7 copy.35
  2.2 7.6 %all-to-all-start = ((bf16[2,8,3200]{2,0,1:T(2,128)(2,1)}), bf16[2,8,3200]{2,0,1:T(2,128)(2,1)S(1)}, u32[]{:S(2)}, u32[]{:S(2)}) async-start(bf16[2,8,3200]{2,0,1:T(2,128)(2,1)} %copy.35), calls=%async_computation | async-start | bytes 204800 | tf_op jit(solution)/shard_map/all_to_all | solution.py:71
  9.7 0.8 slice_bitcast_fusion.6
  10.5 2.4 %collective-permute-start.4 = (bf16[2,128,128]{2,1,0:T(8,128)(2,1)S(1)}, bf16[2,128,128]{2,1,0:T(8,128)(2,1)S(1)}, u32[]{:S(2)}, u32[]{:S(2)}) collective-permute-start(bf16[2,128,128]{2,1,0:T(8,128)(2,1)S(1)} %pad_maximum_fusion.3), channel_id=1, source_target_pairs={{64,0},{128,64},{192,128},{256,192},{320,256},{384,320},{448,384},... | collective-permute-start | bytes 196616 | tf_op jit(solution)/shard_map/ppermute | solution.py:16
  13.0 0.8 compare_convert_fusion
  13.8 0.7 compare_bitcast_fusion
  14.4 4.1 %all-to-all-done = bf16[2,8,3200]{2,0,1:T(2,128)(2,1)S(1)} async-done(((bf16[2,8,3200]{2,0,1:T(2,128)(2,1)}), bf16[2,8,3200]{2,0,1:T(2,128)(2,1)S(1)}, u32[]{:S(2)}, u32[]{:S(2)}) %all-to-all-start) | async-done | bytes 102432 | tf_op jit(solution)/shard_map/all_to_all | solution.py:71
  18.5 4.6 %collective-permute-start = (bf16[2,8,3200]{2,0,1:T(2,128)(2,1)S(1)}, bf16[2,8,3200]{2,0,1:T(2,128)(2,1)S(1)}, u32[]{:S(2)}, u32[]{:S(2)}) collective-permute-start(bf16[2,8,3200]{2,0,1:T(2,128)(2,1)S(1)} %all-to-all-done), channel_id=1, source_target_pairs={{0,2},{2,4},{4,6},{6,0},{1,3},{3,5},{5,7},{7,1},{8,10},{10,12},{12... | collective-permute-start | bytes 307208 | tf_op jit(solution)/shard_map/ppermute | solution.py:21
  23.2 7.7 %collective-permute-start.1 = (bf16[2,8,3200]{2,0,1:T(2,128)(2,1)S(1)}, bf16[2,8,3200]{2,0,1:T(2,128)(2,1)S(1)}, u32[]{:S(2)}, u32[]{:S(2)}) collective-permute-start(bf16[2,8,3200]{2,0,1:T(2,128)(2,1)S(1)} %all-to-all-done), channel_id=1, source_target_pairs={{0,4},{2,6},{4,0},{6,2},{1,5},{3,7},{5,1},{7,3},{8,12},{10,14},{12... | collective-permute-start | bytes 307208 | tf_op jit(solution)/shard_map/ppermute | solution.py:21
  30.8 1.9 %collective-permute-start.2 = (bf16[2,8,3200]{2,0,1:T(2,128)(2,1)S(1)}, bf16[2,8,3200]{2,0,1:T(2,128)(2,1)S(1)}, u32[]{:S(2)}, u32[]{:S(2)}) collective-permute-start(bf16[2,8,3200]{2,0,1:T(2,128)(2,1)S(1)} %all-to-all-done), channel_id=1, source_target_pairs={{0,6},{2,0},{4,2},{6,4},{1,7},{3,1},{5,3},{7,5},{8,14},{10,8},{12,... | collective-permute-start | bytes 307208 | tf_op jit(solution)/shard_map/ppermute | solution.py:21
  32.8 3.4 %collective-permute-done.1 = bf16[2,8,3200]{2,0,1:T(2,128)(2,1)S(1)} collective-permute-done((bf16[2,8,3200]{2,0,1:T(2,128)(2,1)S(1)}, bf16[2,8,3200]{2,0,1:T(2,128)(2,1)S(1)}, u32[]{:S(2)}, u32[]{:S(2)}) %collective-permute-start.1) | collective-permute-done | bytes 102432 | tf_op jit(solution)/shard_map/ppermute | solution.py:21
  36.3 3.2 %collective-permute-done.2 = bf16[2,8,3200]{2,0,1:T(2,128)(2,1)S(1)} collective-permute-done((bf16[2,8,3200]{2,0,1:T(2,128)(2,1)S(1)}, bf16[2,8,3200]{2,0,1:T(2,128)(2,1)S(1)}, u32[]{:S(2)}, u32[]{:S(2)}) %collective-permute-start.2) | collective-permute-done | bytes 102432 | tf_op jit(solution)/shard_map/ppermute | solution.py:21
  39.5 0.6 pad_maximum_fusion.1
  40.1 1.9 %collective-permute-start.3 = (bf16[2,32,3200]{2,0,1:T(2,128)(2,1)S(1)}, bf16[2,32,3200]{2,0,1:T(2,128)(2,1)S(1)}, u32[]{:S(2)}, u32[]{:S(2)}) collective-permute-start(bf16[2,32,3200]{2,0,1:T(2,128)(2,1)S(1)} %pad_maximum_fusion.1), channel_id=1, source_target_pairs={{0,1},{1,0},{2,3},{3,2},{4,5},{5,4},{6,7},{7,6},{8,9},{9,8},{10,11... | collective-permute-start | bytes 1228808 | tf_op jit(solution)/shard_map/ppermute | solution.py:25
  42.3 1.4 %collective-permute-done.3 = bf16[2,32,3200]{2,0,1:T(2,128)(2,1)S(1)} collective-permute-done((bf16[2,32,3200]{2,0,1:T(2,128)(2,1)S(1)}, bf16[2,32,3200]{2,0,1:T(2,128)(2,1)S(1)}, u32[]{:S(2)}, u32[]{:S(2)}) %collective-permute-start.3) | collective-permute-done | bytes 409632 | tf_op jit(solution)/shard_map/ppermute | solution.py:25
  44.1 0.4 reshape.56
  44.8 0.6 copy-done
  45.4 0.4 fusion.46
  46.0 0.4 fusion.45
  46.7 0.3 fusion.26
  47.0 4.1 %collective-permute-start.5 = (f32[130,128]{1,0:T(8,128)S(1)}, f32[130,128]{1,0:T(8,128)S(1)}, u32[]{:S(2)}, u32[]{:S(2)}) collective-permute-start(f32[130,128]{1,0:T(8,128)S(1)} %pad_maximum_fusion.2), channel_id=1, source_target_pairs={{0,64},{64,128},{128,192},{192,256},{256,320},{320,384},{384,448},... | collective-permute-start | bytes 199688 | tf_op jit(solution)/shard_map/ppermute | solution.py:16
  51.4 3.9 %collective-permute-done.5 = f32[130,128]{1,0:T(8,128)S(1)} collective-permute-done((f32[130,128]{1,0:T(8,128)S(1)}, f32[130,128]{1,0:T(8,128)S(1)}, u32[]{:S(2)}, u32[]{:S(2)}) %collective-permute-start.5) | collective-permute-done | bytes 66592 | tf_op jit(solution)/shard_map/ppermute | solution.py:16
  55.5 1.1 %multiply_reduce_fusion = (f32[256]{0:T(256)S(1)}, bf16[256,128]{1,0:T(8,128)(2,1)}) fusion(bf16[256,128]{1,0:T(8,128)(2,1)S(1)} %copy-done.1, f32[256]{0:T(256)S(1)} %get-tuple-element.16, f32[128,128]{1,0:T(8,128)S(1)} %slice_select_fusion, f32[256]{0:T(256)S(1)} %get-tuple-element.18, bf16[1600,128]{1,0:T(8,128)(2,1)S(1)} %bitcast.101, ...), kind=kOutput, calls=%fused_computation.52 | convolution fusion | flops 106004224 | bytes 2250752 | tf_op jit(solution)/shard_map/dot_general | solution.py:36
  56.6 0.6 fusion.3
  57.2 0.4 fusion.10
  57.6 1.9 %collective-permute-start.6 = (f32[3,128]{1,0:T(4,128)S(1)}, f32[3,128]{1,0:T(4,128)S(1)}, u32[]{:S(2)}, u32[]{:S(2)}) collective-permute-start(f32[3,128]{1,0:T(4,128)S(1)} %pad_maximum_fusion.4), channel_id=1, source_target_pairs={{64,0},{128,64},{192,128},{256,192},{320,256},{384,320},{448,384},... | collective-permute-start | bytes 4616 | tf_op jit(solution)/shard_map/ppermute | solution.py:16
  59.6 0.4 fusion.14
  59.9 4.1 %collective-permute-done.6 = f32[3,128]{1,0:T(4,128)S(1)} collective-permute-done((f32[3,128]{1,0:T(4,128)S(1)}, f32[3,128]{1,0:T(4,128)S(1)}, u32[]{:S(2)}, u32[]{:S(2)}) %collective-permute-start.6) | collective-permute-done | bytes 1568 | tf_op jit(solution)/shard_map/ppermute | solution.py:16
  64.3 0.6 copy.41
  64.9 0.3 fusion.6
  65.5 0.6 copy.40
  66.2 0.9 fusion.28
  67.1 1.9 %collective-permute-start.8 = (bf16[2,25,4,8,128]{4,0,1,3,2:T(2,128)(2,1)S(1)}, bf16[2,25,4,8,128]{4,0,1,3,2:T(2,128)(2,1)S(1)}, u32[]{:S(2)}, u32[]{:S(2)}) collective-permute-start(bf16[2,25,4,8,128]{4,0,1,3,2:T(2,128)(2,1)S(1)} %fusion.28), channel_id=1, source_target_pairs={{0,1},{1,0},{2,3},{3,2},{4,5},{5,4},{6,7},{7,6},{8,9},{9,8},{10,11... | collective-permute-start | bytes 1228808 | tf_op jit(solution)/shard_map/ppermute | solution.py:25
  69.0 1.7 %collective-permute-done.8 = bf16[2,25,4,8,128]{4,0,1,3,2:T(2,128)(2,1)S(1)} collective-permute-done((bf16[2,25,4,8,128]{4,0,1,3,2:T(2,128)(2,1)S(1)}, bf16[2,25,4,8,128]{4,0,1,3,2:T(2,128)(2,1)S(1)}, u32[]{:S(2)}, u32[]{:S(2)}) %collective-permute-start.8) | collective-permute-done | bytes 409632 | tf_op jit(solution)/shard_map/ppermute | solution.py:25
  70.8 1.1 fusion.18
  72.0 1.9 %collective-permute-start.11 = (bf16[2,25,8,128]{3,0,1,2:T(2,128)(2,1)S(1)}, bf16[2,25,8,128]{3,0,1,2:T(2,128)(2,1)S(1)}, u32[]{:S(2)}, u32[]{:S(2)}) collective-permute-start(bf16[2,25,8,128]{3,0,1,2:T(2,128)(2,1)S(1)} %get-tuple-element.22), channel_id=1, source_target_pairs={{0,2},{2,4},{4,6},{6,0},{1,3},{3,5},{5,7},{7,1},{8,10},{10,12},{12... | collective-permute-start | bytes 307208 | tf_op jit(solution)/shard_map/ppermute | solution.py:21
  74.0 4.2 %collective-permute-start.10 = (bf16[2,25,8,128]{3,0,1,2:T(2,128)(2,1)S(1)}, bf16[2,25,8,128]{3,0,1,2:T(2,128)(2,1)S(1)}, u32[]{:S(2)}, u32[]{:S(2)}) collective-permute-start(bf16[2,25,8,128]{3,0,1,2:T(2,128)(2,1)S(1)} %get-tuple-element.23), channel_id=1, source_target_pairs={{0,4},{2,6},{4,0},{6,2},{1,5},{3,7},{5,1},{7,3},{8,12},{10,14},{12... | collective-permute-start | bytes 307208 | tf_op jit(solution)/shard_map/ppermute | solution.py:21
  78.2 3.3 %collective-permute-start.9 = (bf16[2,25,8,128]{3,0,1,2:T(2,128)(2,1)S(1)}, bf16[2,25,8,128]{3,0,1,2:T(2,128)(2,1)S(1)}, u32[]{:S(2)}, u32[]{:S(2)}) collective-permute-start(bf16[2,25,8,128]{3,0,1,2:T(2,128)(2,1)S(1)} %get-tuple-element.21), channel_id=1, source_target_pairs={{0,6},{2,0},{4,2},{6,4},{1,7},{3,1},{5,3},{7,5},{8,14},{10,8},{12,... | collective-permute-start | bytes 307208 | tf_op jit(solution)/shard_map/ppermute | solution.py:21
  81.5 0.3 fusion.47
  81.9 3.9 %collective-permute-start.7 = (f32[128,128]{1,0:T(8,128)S(1)}, f32[128,128]{1,0:T(8,128)S(1)}, u32[]{:S(2)}, u32[]{:S(2)}) collective-permute-start(f32[128,128]{1,0:T(8,128)S(1)} %fusion.47), channel_id=1, source_target_pairs={{0,64},{64,128},{128,192},{192,256},{256,320},{320,384},{384,448},... | collective-permute-start | bytes 196616 | tf_op jit(solution)/shard_map/ppermute | solution.py:16
  86.0 6.1 %collective-permute-done.9 = bf16[2,25,8,128]{3,0,1,2:T(2,128)(2,1)S(1)} collective-permute-done((bf16[2,25,8,128]{3,0,1,2:T(2,128)(2,1)S(1)}, bf16[2,25,8,128]{3,0,1,2:T(2,128)(2,1)S(1)}, u32[]{:S(2)}, u32[]{:S(2)}) %collective-permute-start.9) | collective-permute-done | bytes 102432 | tf_op jit(solution)/shard_map/ppermute | solution.py:21
  92.0 0.8 fusion.35
  92.9 4.8 %all-to-all-start.1 = ((bf16[8,2,25,128]{3,1,2,0:T(2,128)(2,1)}), bf16[8,2,25,128]{3,1,2,0:T(2,128)(2,1)S(1)}, u32[]{:S(2)}, u32[]{:S(2)}) async-start(bf16[8,2,25,128]{3,1,2,0:T(2,128)(2,1)} %fusion.35), calls=%async_computation.1 | async-start | bytes 204800 | tf_op jit(solution)/shard_map/all_to_all | solution.py:163
  97.7 1.1 add_convert_fusion
  98.7 7.7 %all-to-all-done.1 = bf16[8,2,25,128]{3,1,2,0:T(2,128)(2,1)S(1)} async-done(((bf16[8,2,25,128]{3,1,2,0:T(2,128)(2,1)}), bf16[8,2,25,128]{3,1,2,0:T(2,128)(2,1)S(1)}, u32[]{:S(2)}, u32[]{:S(2)}) %all-to-all-start.1) | async-done | bytes 102432 | tf_op jit(solution)/shard_map/all_to_all | solution.py:163
  106.6 0.6 copy.42
  107.2 0.6 copy.43
  (36 shorter events, 2.9 us)
Async XLA Ops:
  2.2 16.3 %all-to-all-start = ((bf16[2,8,3200]{2,0,1:T(2,128)(2,1)}), bf16[2,8,3200]{2,0,1:T(2,128)(2,1)S(1)}, u32[]{:S(2)}, u32[]{:S(2)}) async-start(bf16[2,8,3200]{2,0,1:T(2,128)(2,1)} %copy.35), calls=%async_computation | async-start | bytes 204800 | tf_op jit(solution)/shard_map/all_to_all | solution.py:71
  10.5 35.5 %collective-permute-start.4 = (bf16[2,128,128]{2,1,0:T(8,128)(2,1)S(1)}, bf16[2,128,128]{2,1,0:T(8,128)(2,1)S(1)}, u32[]{:S(2)}, u32[]{:S(2)}) collective-permute-start(bf16[2,128,128]{2,1,0:T(8,128)(2,1)S(1)} %pad_maximum_fusion.3), channel_id=1, source_target_pairs={{64,0},{128,64},{192,128},{256,192},{320,256},{384,320},{448,384},... | collective-permute-start | bytes 196616 | tf_op jit(solution)/shard_map/ppermute | solution.py:16
  18.5 14.3 %collective-permute-start = (bf16[2,8,3200]{2,0,1:T(2,128)(2,1)S(1)}, bf16[2,8,3200]{2,0,1:T(2,128)(2,1)S(1)}, u32[]{:S(2)}, u32[]{:S(2)}) collective-permute-start(bf16[2,8,3200]{2,0,1:T(2,128)(2,1)S(1)} %all-to-all-done), channel_id=1, source_target_pairs={{0,2},{2,4},{4,6},{6,0},{1,3},{3,5},{5,7},{7,1},{8,10},{10,12},{12... | collective-permute-start | bytes 307208 | tf_op jit(solution)/shard_map/ppermute | solution.py:21
  23.2 13.1 %collective-permute-start.1 = (bf16[2,8,3200]{2,0,1:T(2,128)(2,1)S(1)}, bf16[2,8,3200]{2,0,1:T(2,128)(2,1)S(1)}, u32[]{:S(2)}, u32[]{:S(2)}) collective-permute-start(bf16[2,8,3200]{2,0,1:T(2,128)(2,1)S(1)} %all-to-all-done), channel_id=1, source_target_pairs={{0,4},{2,6},{4,0},{6,2},{1,5},{3,7},{5,1},{7,3},{8,12},{10,14},{12... | collective-permute-start | bytes 307208 | tf_op jit(solution)/shard_map/ppermute | solution.py:21
  30.8 8.7 %collective-permute-start.2 = (bf16[2,8,3200]{2,0,1:T(2,128)(2,1)S(1)}, bf16[2,8,3200]{2,0,1:T(2,128)(2,1)S(1)}, u32[]{:S(2)}, u32[]{:S(2)}) collective-permute-start(bf16[2,8,3200]{2,0,1:T(2,128)(2,1)S(1)} %all-to-all-done), channel_id=1, source_target_pairs={{0,6},{2,0},{4,2},{6,4},{1,7},{3,1},{5,3},{7,5},{8,14},{10,8},{12,... | collective-permute-start | bytes 307208 | tf_op jit(solution)/shard_map/ppermute | solution.py:21
  40.1 3.6 %collective-permute-start.3 = (bf16[2,32,3200]{2,0,1:T(2,128)(2,1)S(1)}, bf16[2,32,3200]{2,0,1:T(2,128)(2,1)S(1)}, u32[]{:S(2)}, u32[]{:S(2)}) collective-permute-start(bf16[2,32,3200]{2,0,1:T(2,128)(2,1)S(1)} %pad_maximum_fusion.1), channel_id=1, source_target_pairs={{0,1},{1,0},{2,3},{3,2},{4,5},{5,4},{6,7},{7,6},{8,9},{9,8},{10,11... | collective-permute-start | bytes 1228808 | tf_op jit(solution)/shard_map/ppermute | solution.py:25
  44.6 0.8 copy-start
  46.7 8.6 %copy-start.2 = (s32[256,2]{0,1:T(2,128)S(1)}, s32[256,2]{0,1:T(2,128)}, u32[]{:S(2)}) copy-start(s32[256,2]{0,1:T(2,128)} %param.9) | copy-start | bytes 6148
  46.7 8.8 %copy-start.1 = (bf16[256,128]{1,0:T(8,128)(2,1)S(1)}, bf16[256,128]{1,0:T(8,128)(2,1)}, u32[]{:S(2)}) copy-start(bf16[256,128]{1,0:T(8,128)(2,1)} %param.8) | copy-start | bytes 196612
  47.0 8.3 %collective-permute-start.5 = (f32[130,128]{1,0:T(8,128)S(1)}, f32[130,128]{1,0:T(8,128)S(1)}, u32[]{:S(2)}, u32[]{:S(2)}) collective-permute-start(f32[130,128]{1,0:T(8,128)S(1)} %pad_maximum_fusion.2), channel_id=1, source_target_pairs={{0,64},{64,128},{128,192},{192,256},{256,320},{320,384},{384,448},... | collective-permute-start | bytes 199688 | tf_op jit(solution)/shard_map/ppermute | solution.py:16
  57.6 6.4 %collective-permute-start.6 = (f32[3,128]{1,0:T(4,128)S(1)}, f32[3,128]{1,0:T(4,128)S(1)}, u32[]{:S(2)}, u32[]{:S(2)}) collective-permute-start(f32[3,128]{1,0:T(4,128)S(1)} %pad_maximum_fusion.4), channel_id=1, source_target_pairs={{64,0},{128,64},{192,128},{256,192},{320,256},{384,320},{448,384},... | collective-permute-start | bytes 4616 | tf_op jit(solution)/shard_map/ppermute | solution.py:16
  67.1 3.6 %collective-permute-start.8 = (bf16[2,25,4,8,128]{4,0,1,3,2:T(2,128)(2,1)S(1)}, bf16[2,25,4,8,128]{4,0,1,3,2:T(2,128)(2,1)S(1)}, u32[]{:S(2)}, u32[]{:S(2)}) collective-permute-start(bf16[2,25,4,8,128]{4,0,1,3,2:T(2,128)(2,1)S(1)} %fusion.28), channel_id=1, source_target_pairs={{0,1},{1,0},{2,3},{3,2},{4,5},{5,4},{6,7},{7,6},{8,9},{9,8},{10,11... | collective-permute-start | bytes 1228808 | tf_op jit(solution)/shard_map/ppermute | solution.py:25
  72.0 13.8 %collective-permute-start.11 = (bf16[2,25,8,128]{3,0,1,2:T(2,128)(2,1)S(1)}, bf16[2,25,8,128]{3,0,1,2:T(2,128)(2,1)S(1)}, u32[]{:S(2)}, u32[]{:S(2)}) collective-permute-start(bf16[2,25,8,128]{3,0,1,2:T(2,128)(2,1)S(1)} %get-tuple-element.22), channel_id=1, source_target_pairs={{0,2},{2,4},{4,6},{6,0},{1,3},{3,5},{5,7},{7,1},{8,10},{10,12},{12... | collective-permute-start | bytes 307208 | tf_op jit(solution)/shard_map/ppermute | solution.py:21
  74.0 12.0 %collective-permute-start.10 = (bf16[2,25,8,128]{3,0,1,2:T(2,128)(2,1)S(1)}, bf16[2,25,8,128]{3,0,1,2:T(2,128)(2,1)S(1)}, u32[]{:S(2)}, u32[]{:S(2)}) collective-permute-start(bf16[2,25,8,128]{3,0,1,2:T(2,128)(2,1)S(1)} %get-tuple-element.23), channel_id=1, source_target_pairs={{0,4},{2,6},{4,0},{6,2},{1,5},{3,7},{5,1},{7,3},{8,12},{10,14},{12... | collective-permute-start | bytes 307208 | tf_op jit(solution)/shard_map/ppermute | solution.py:21
  78.2 13.8 %collective-permute-start.9 = (bf16[2,25,8,128]{3,0,1,2:T(2,128)(2,1)S(1)}, bf16[2,25,8,128]{3,0,1,2:T(2,128)(2,1)S(1)}, u32[]{:S(2)}, u32[]{:S(2)}) collective-permute-start(bf16[2,25,8,128]{3,0,1,2:T(2,128)(2,1)S(1)} %get-tuple-element.21), channel_id=1, source_target_pairs={{0,6},{2,0},{4,2},{6,4},{1,7},{3,1},{5,3},{7,5},{8,14},{10,8},{12,... | collective-permute-start | bytes 307208 | tf_op jit(solution)/shard_map/ppermute | solution.py:21
  81.9 15.8 %collective-permute-start.7 = (f32[128,128]{1,0:T(8,128)S(1)}, f32[128,128]{1,0:T(8,128)S(1)}, u32[]{:S(2)}, u32[]{:S(2)}) collective-permute-start(f32[128,128]{1,0:T(8,128)S(1)} %fusion.47), channel_id=1, source_target_pairs={{0,64},{64,128},{128,192},{192,256},{256,320},{320,384},{384,448},... | collective-permute-start | bytes 196616 | tf_op jit(solution)/shard_map/ppermute | solution.py:16
  92.9 13.6 %all-to-all-start.1 = ((bf16[8,2,25,128]{3,1,2,0:T(2,128)(2,1)}), bf16[8,2,25,128]{3,1,2,0:T(2,128)(2,1)S(1)}, u32[]{:S(2)}, u32[]{:S(2)}) async-start(bf16[8,2,25,128]{3,1,2,0:T(2,128)(2,1)} %fusion.35), calls=%async_computation.1 | async-start | bytes 204800 | tf_op jit(solution)/shard_map/all_to_all | solution.py:163

commit v7 on v5

--- a/solution.py
+++ b/solution.py
@@ -53,8 +53,7 @@
 
 def per_device(queries, keys, values, cotangent, mask):
     groups = lax.axis_size("y")
-    far = lax.axis_size("xh")
-    blocks = groups * far * lax.axis_size("c")
+    blocks = groups * lax.axis_size("xh") * lax.axis_size("c")
     rows = keys.shape[1]
     tokens = queries.shape[0]
     half = tokens // 2
@@ -63,9 +62,11 @@
     query_next, grad_next = served[0], served[1]
 
     own_kv = jnp.stack([keys[0], values[0]])
-    own_kv = jnp.transpose(own_kv, (0, 2, 1, 3)).reshape(2, KVH, rows * HD)
-    by_group = lax.all_to_all(own_kv, "y", split_axis=1, concat_axis=1, tiled=True)
-    across = lax.all_gather(by_group, "xh", axis=1, tiled=True)
+    far = lax.axis_size("xh")
+    own_kv = jnp.transpose(own_kv, (2, 0, 1, 3)).reshape(KVH, 1, 2, rows * HD)
+    own_kv = jnp.broadcast_to(own_kv, (KVH, far, 2, rows * HD)).reshape(-1, 2, rows * HD)
+    across = lax.all_to_all(own_kv, ("y", "xh"), split_axis=0, concat_axis=0, tiled=True)
+    across = jnp.transpose(across, (1, 0, 2))
     gathered = jnp.concatenate([across, partner(across)], axis=1)
     gathered = jnp.transpose(gathered.reshape(2, blocks, rows, HD), (0, 2, 1, 3))
     gathered = gathered.reshape(2, rows * blocks, HD)
@@ -145,14 +146,13 @@
             gv_own.astype(jnp.float32) + gv_next.astype(jnp.float32),
         ]
     ).astype(jnp.bfloat16)
-    parts = parts.reshape(2, rows, 2, far, groups, HD)
+    parts = parts.reshape(2, rows, 2, groups, far, HD)
     summed = parts[:, :, 0].astype(jnp.float32) + partner(parts[:, :, 1]).astype(jnp.float32)
-    summed = jnp.transpose(summed.astype(jnp.bfloat16), (2, 0, 1, 3, 4))
-    summed = lax.all_to_all(summed, "xh", split_axis=0, concat_axis=0, tiled=True)
-    summed = jnp.sum(summed.astype(jnp.float32), axis=0).astype(jnp.bfloat16)
-    summed = jnp.transpose(summed, (2, 0, 1, 3))
-    returned = lax.all_to_all(summed, "y", split_axis=0, concat_axis=0, tiled=True)
-    returned = jnp.transpose(returned, (1, 2, 0, 3))
+    summed = jnp.transpose(summed.astype(jnp.bfloat16), (2, 3, 0, 1, 4))
+    summed = summed.reshape(groups * far, 2, rows, HD)
+    summed = lax.all_to_all(summed, ("y", "xh"), split_axis=0, concat_axis=0, tiled=True)
+    summed = summed.reshape(KVH, far, 2, rows, HD).astype(jnp.float32).sum(axis=1)
+    returned = jnp.transpose(summed, (1, 2, 0, 3)).astype(jnp.bfloat16)
     return (attended, grad_query, returned[0][None], returned[1][None])
 
 

time: 99.6 us -> 88.2 us (0.89)
  the two profiles are of different devices: /device:TPU:2 before, /device:TPU:386 now
where the time goes in v7:
time: 88.2 us; the launch traced here: 87.6 us
  starting transfers between devices  36.6 us (41%)
  waiting for transfers between devices  36.3 us (41%)
  matrix products  5.86 us (7%)
  local copies, waits for them, and re-layouts  4.35 us (5%)
  other arithmetic  3.65 us (4%)
  between operations  0.96 us (1%)
    ppermute x4, starting transfers between devices, passed_along(): return lax.ppermute(value, axis, pairs)  16.3 us
    all_to_all x1, waiting for transfers between devices, per_device(): lax.all_to_all(own_kv, ('y', 'xh'), split_axis=0, concat_axis=0, tiled=True)  14.5 us
    all_to_all x1, starting transfers between devices, per_device(): lax.all_to_all(own_kv, ('y', 'xh'), split_axis=0, concat_axis=0, tiled=True)  12 us
    ppermute x4, waiting for transfers between devices, passed_along(): return lax.ppermute(value, axis, pairs)  11.1 us
    all_to_all x1, waiting for transfers between devices, per_device(): lax.all_to_all(summed, ('y', 'xh'), split_axis=0, concat_axis=0, tiled=True)  7.27 us
    all_to_all x1, starting transfers between devices, per_device(): lax.all_to_all(summed, ('y', 'xh'), split_axis=0, concat_axis=0, tiled=True)  4.51 us
    ppermute x2, starting transfers between devices, partner(): return lax.ppermute(value, 'c', [(0, 1), (1, 0)])  3.83 us
    ppermute x2, waiting for transfers between devices, partner(): return lax.ppermute(value, 'c', [(0, 1), (1, 0)])  3.38 us
  transfers between devices with their start and end apart: 8, of which 7 were waited for; matrix products, arithmetic and copies ran while one was open for 5% of the time, Pallas kernels for 0%

profile of v7, /device:TPU:386, one launch (start us, length us, event | category | flops | bytes accessed | tf_op | source)
XLA Modules:
  0.0 87.6 jit_solution(4282190188948916050)
XLA Ops:
  0.7 0.9 %maximum_bitcast_fusion = bf16[8,2,3200]{2,0,1:T(8,128)(2,1)S(1)} fusion(bf16[1,25,8,128]{3,2,1,0:T(8,128)(2,1)} %param.7, bf16[1,25,8,128]{3,2,1,0:T(8,128)(2,1)} %param.6), kind=kLoop, calls=%fused_computation.54 | loop fusion | flops 51200 | bytes 204800 | tf_op jit(solution)/shard_map/broadcast_in_dim | solution.py:67
  1.6 0.1 copy.22
  1.6 1.0 %broadcast_in_dim.58 = bf16[8,4,2,3200]{3,2,1,0:T(2,128)(2,1)} broadcast(bf16[8,2,3200]{2,1,0:T(2,128)(2,1)S(1)} %copy.22), dimensions={0,2,3} | broadcast | bytes 512000 | tf_op jit(solution)/shard_map/broadcast_in_dim | solution.py:67
  2.6 12.0 %all-to-all-start = ((bf16[32,2,3200]{2,1,0:T(2,128)(2,1)}), bf16[32,2,3200]{2,1,0:T(2,128)(2,1)S(1)}, u32[]{:S(2)}, u32[]{:S(2)}) async-start(bf16[32,2,3200]{2,1,0:T(2,128)(2,1)} %bitcast.3), calls=%async_computation | async-start | bytes 819200 | tf_op jit(solution)/shard_map/all_to_all | solution.py:68
  14.6 0.0 copy-done.1
  14.6 0.0 copy-done
  14.6 3.3 %collective-permute-start.1 = (bf16[2,128,128]{2,1,0:T(8,128)(2,1)S(1)}, bf16[2,128,128]{2,1,0:T(8,128)(2,1)S(1)}, u32[]{:S(2)}, u32[]{:S(2)}) collective-permute-start(bf16[2,128,128]{2,1,0:T(8,128)(2,1)S(1)} %pad_maximum_fusion.3), channel_id=1, source_target_pairs={{64,0},{128,64},{192,128},{256,192},{320,256},{384,320},{448,384},... | collective-permute-start | bytes 196616 | tf_op jit(solution)/shard_map/ppermute | solution.py:16
  18.0 14.5 %all-to-all-done = bf16[32,2,3200]{2,1,0:T(2,128)(2,1)S(1)} async-done(((bf16[32,2,3200]{2,1,0:T(2,128)(2,1)}), bf16[32,2,3200]{2,1,0:T(2,128)(2,1)S(1)}, u32[]{:S(2)}, u32[]{:S(2)}) %all-to-all-start) | async-done | bytes 409632 | tf_op jit(solution)/shard_map/all_to_all | solution.py:68
  32.5 1.9 %collective-permute-start = (bf16[2,32,3200]{2,0,1:T(2,128)(2,1)S(1)}, bf16[2,32,3200]{2,0,1:T(2,128)(2,1)S(1)}, u32[]{:S(2)}, u32[]{:S(2)}) collective-permute-start(bf16[2,32,3200]{2,0,1:T(2,128)(2,1)S(1)} %bitcast.106), channel_id=1, source_target_pairs={{0,1},{1,0},{2,3},{3,2},{4,5},{5,4},{6,7},{7,6},{8,9},{9,8},{10,11... | collective-permute-start | bytes 1228808 | tf_op jit(solution)/shard_map/ppermute | solution.py:20
  34.5 1.7 %collective-permute-done = bf16[2,32,3200]{2,0,1:T(2,128)(2,1)S(1)} collective-permute-done((bf16[2,32,3200]{2,0,1:T(2,128)(2,1)S(1)}, bf16[2,32,3200]{2,0,1:T(2,128)(2,1)S(1)}, u32[]{:S(2)}, u32[]{:S(2)}) %collective-permute-start) | collective-permute-done | bytes 409632 | tf_op jit(solution)/shard_map/ppermute | solution.py:20
  36.1 1.1 %pad_maximum_fusion = bf16[2,64,3200]{2,0,1:T(2,128)(2,1)S(1)} fusion(bf16[2,32,3200]{2,0,1:T(2,128)(2,1)S(1)} %collective-permute-done, bf16[2,32,3200]{2,0,1:T(2,128)(2,1)S(1)} %bitcast.107), kind=kLoop, calls=%fused_computation.28 | loop fusion | flops 409600 | bytes 1638400 | tf_op jit(solution)/shard_map/concatenate | solution.py:70
  37.2 0.1 copy.23
  37.3 0.4 reshape.62
  37.7 0.1 fusion.41
  37.8 0.2 copy.24
  38.0 0.4 fusion.44
  38.4 0.2 copy.25
  38.6 0.0 collective-permute-done.1
  38.6 0.4 fusion.43
  39.0 0.2 fusion.21
  39.2 0.3 fusion.25
  39.6 7.1 %collective-permute-start.2 = (f32[130,128]{1,0:T(8,128)S(1)}, f32[130,128]{1,0:T(8,128)S(1)}, u32[]{:S(2)}, u32[]{:S(2)}) collective-permute-start(f32[130,128]{1,0:T(8,128)S(1)} %pad_maximum_fusion.2), channel_id=1, source_target_pairs={{0,64},{64,128},{128,192},{192,256},{256,320},{320,384},{384,448},... | collective-permute-start | bytes 199688 | tf_op jit(solution)/shard_map/ppermute | solution.py:16
  46.6 0.3 fusion.15
  46.9 1.6 %collective-permute-done.2 = f32[130,128]{1,0:T(8,128)S(1)} collective-permute-done((f32[130,128]{1,0:T(8,128)S(1)}, f32[130,128]{1,0:T(8,128)S(1)}, u32[]{:S(2)}, u32[]{:S(2)}) %collective-permute-start.2) | collective-permute-done | bytes 66592 | tf_op jit(solution)/shard_map/ppermute | solution.py:16
  48.6 0.1 slice_select_fusion
  48.7 1.1 %multiply_reduce_fusion = (f32[256]{0:T(256)S(1)}, bf16[256,128]{1,0:T(8,128)(2,1)}) fusion(bf16[256,128]{1,0:T(8,128)(2,1)S(1)} %copy-done.1, f32[256]{0:T(256)S(1)} %get-tuple-element.8, f32[128,128]{1,0:T(8,128)S(1)} %slice_select_fusion, f32[256]{0:T(256)S(1)} %get-tuple-element.10, bf16[1600,128]{1,0:T(8,128)(2,1)S(1)} %bitcast.99, ...), kind=kOutput, calls=%fused_computation.52 | convolution fusion | flops 106004224 | bytes 2250752 | tf_op jit(solution)/shard_map/dot_general | solution.py:31
  49.8 0.6 fusion.3
  50.4 0.4 fusion.10
  50.9 1.9 %collective-permute-start.3 = (f32[3,128]{1,0:T(4,128)S(1)}, f32[3,128]{1,0:T(4,128)S(1)}, u32[]{:S(2)}, u32[]{:S(2)}) collective-permute-start(f32[3,128]{1,0:T(4,128)S(1)} %pad_maximum_fusion.4), channel_id=1, source_target_pairs={{64,0},{128,64},{192,128},{256,192},{320,256},{384,320},{448,384},... | collective-permute-start | bytes 4616 | tf_op jit(solution)/shard_map/ppermute | solution.py:16
  52.8 0.4 fusion.14
  53.2 5.7 %collective-permute-done.3 = f32[3,128]{1,0:T(4,128)S(1)} collective-permute-done((f32[3,128]{1,0:T(4,128)S(1)}, f32[3,128]{1,0:T(4,128)S(1)}, u32[]{:S(2)}, u32[]{:S(2)}) %collective-permute-start.3) | collective-permute-done | bytes 1568 | tf_op jit(solution)/shard_map/ppermute | solution.py:16
  58.8 0.3 fusion.6
  59.2 0.3 fusion.9
  59.4 0.3 fusion.13
  59.7 0.3 fusion.30
  60.0 1.9 %collective-permute-start.5 = (bf16[2,25,8,4,128]{4,3,2,1,0:T(4,128)(2,1)S(1)}, bf16[2,25,8,4,128]{4,3,2,1,0:T(4,128)(2,1)S(1)}, u32[]{:S(2)}, u32[]{:S(2)}) collective-permute-start(bf16[2,25,8,4,128]{4,3,2,1,0:T(4,128)(2,1)S(1)} %fusion.30), channel_id=1, source_target_pairs={{0,1},{1,0},{2,3},{3,2},{4,5},{5,4},{6,7},{7,6},{8,9},{9,8},{10,11... | collective-permute-start | bytes 1228808 | tf_op jit(solution)/shard_map/ppermute | solution.py:20
  61.9 1.7 %collective-permute-done.5 = bf16[2,25,8,4,128]{4,3,2,1,0:T(4,128)(2,1)S(1)} collective-permute-done((bf16[2,25,8,4,128]{4,3,2,1,0:T(4,128)(2,1)S(1)}, bf16[2,25,8,4,128]{4,3,2,1,0:T(4,128)(2,1)S(1)}, u32[]{:S(2)}, u32[]{:S(2)}) %collective-permute-start.5) | collective-permute-done | bytes 409632 | tf_op jit(solution)/shard_map/ppermute | solution.py:20
  63.6 0.3 fusion.27
  63.9 1.1 %copy.28 = bf16[8,4,2,25,128]{4,2,3,1,0:T(2,128)(2,1)} copy(bf16[8,4,2,25,128]{4,1,0,3,2:T(4,128)(2,1)S(1)} %fusion.27) | data formatting | bytes 819200 | tf_op jit(solution)/shard_map/transpose | solution.py:151
  65.0 4.5 %all-to-all-start.1 = ((bf16[32,2,25,128]{3,1,2,0:T(2,128)(2,1)}), bf16[32,2,25,128]{3,1,2,0:T(2,128)(2,1)S(1)}, u32[]{:S(2)}, u32[]{:S(2)}) async-start(bf16[32,2,25,128]{3,1,2,0:T(2,128)(2,1)} %bitcast.28), calls=%async_computation.1 | async-start | bytes 819200 | tf_op jit(solution)/shard_map/all_to_all | solution.py:153
  69.5 0.3 fusion.45
  69.8 3.9 %collective-permute-start.4 = (f32[128,128]{1,0:T(8,128)S(1)}, f32[128,128]{1,0:T(8,128)S(1)}, u32[]{:S(2)}, u32[]{:S(2)}) collective-permute-start(f32[128,128]{1,0:T(8,128)S(1)} %fusion.45), channel_id=1, source_target_pairs={{0,64},{64,128},{128,192},{192,256},{256,320},{320,384},{384,448},... | collective-permute-start | bytes 196616 | tf_op jit(solution)/shard_map/ppermute | solution.py:16
  73.8 3.8 %collective-permute-done.4 = f32[128,128]{1,0:T(8,128)S(1)} collective-permute-done((f32[128,128]{1,0:T(8,128)S(1)}, f32[128,128]{1,0:T(8,128)S(1)}, u32[]{:S(2)}, u32[]{:S(2)}) %collective-permute-start.4) | collective-permute-done | bytes 65568 | tf_op jit(solution)/shard_map/ppermute | solution.py:16
  77.6 1.1 %add_convert_fusion = bf16[256,128]{1,0:T(8,128)(2,1)} fusion(f32[128,128]{1,0:T(8,128)S(1)} %collective-permute-done.4, bf16[1600,256]{1,0:T(8,128)(2,1)S(1)} %fusion.3, bf16[1600,128]{1,0:T(8,128)(2,1)S(1)} %bitcast.96), kind=kOutput, calls=%fused_computation.51 | convolution fusion | flops 104923136 | bytes 1359872 | tf_op jit(solution)/shard_map/dot_general | solution.py:44
  78.6 7.3 %all-to-all-done.1 = bf16[32,2,25,128]{3,1,2,0:T(2,128)(2,1)S(1)} async-done(((bf16[32,2,25,128]{3,1,2,0:T(2,128)(2,1)}), bf16[32,2,25,128]{3,1,2,0:T(2,128)(2,1)S(1)}, u32[]{:S(2)}, u32[]{:S(2)}) %all-to-all-start.1) | async-done | bytes 409632 | tf_op jit(solution)/shard_map/all_to_all | solution.py:153
  85.9 0.4 bitcast_reduce_fusion
  86.4 0.6 copy.30
  87.0 0.6 copy.31
  (19 shorter events, 0.2 us)
Async XLA Ops:
  0.6 14.0 %copy-start.1 = (bf16[256,128]{1,0:T(8,128)(2,1)S(1)}, bf16[256,128]{1,0:T(8,128)(2,1)}, u32[]{:S(2)}) copy-start(bf16[256,128]{1,0:T(8,128)(2,1)} %param.8) | copy-start | bytes 196612
  0.6 14.0 %copy-start = (bf16[256,128]{1,0:T(8,128)(2,1)S(1)}, bf16[256,128]{1,0:T(8,128)(2,1)}, u32[]{:S(2)}) copy-start(bf16[256,128]{1,0:T(8,128)(2,1)} %param.5) | copy-start | bytes 196612
  0.7 33.8 %copy-start.2 = (s32[256,2]{0,1:T(2,128)S(1)}, s32[256,2]{0,1:T(2,128)}, u32[]{:S(2)}) copy-start(s32[256,2]{0,1:T(2,128)} %param.9) | copy-start | bytes 6148
  2.6 29.9 %all-to-all-start = ((bf16[32,2,3200]{2,1,0:T(2,128)(2,1)}), bf16[32,2,3200]{2,1,0:T(2,128)(2,1)S(1)}, u32[]{:S(2)}, u32[]{:S(2)}) async-start(bf16[32,2,3200]{2,1,0:T(2,128)(2,1)} %bitcast.3), calls=%async_computation | async-start | bytes 819200 | tf_op jit(solution)/shard_map/all_to_all | solution.py:68
  14.6 23.9 %collective-permute-start.1 = (bf16[2,128,128]{2,1,0:T(8,128)(2,1)S(1)}, bf16[2,128,128]{2,1,0:T(8,128)(2,1)S(1)}, u32[]{:S(2)}, u32[]{:S(2)}) collective-permute-start(bf16[2,128,128]{2,1,0:T(8,128)(2,1)S(1)} %pad_maximum_fusion.3), channel_id=1, source_target_pairs={{64,0},{128,64},{192,128},{256,192},{320,256},{384,320},{448,384},... | collective-permute-start | bytes 196616 | tf_op jit(solution)/shard_map/ppermute | solution.py:16
  32.5 3.6 %collective-permute-start = (bf16[2,32,3200]{2,0,1:T(2,128)(2,1)S(1)}, bf16[2,32,3200]{2,0,1:T(2,128)(2,1)S(1)}, u32[]{:S(2)}, u32[]{:S(2)}) collective-permute-start(bf16[2,32,3200]{2,0,1:T(2,128)(2,1)S(1)} %bitcast.106), channel_id=1, source_target_pairs={{0,1},{1,0},{2,3},{3,2},{4,5},{5,4},{6,7},{7,6},{8,9},{9,8},{10,11... | collective-permute-start | bytes 1228808 | tf_op jit(solution)/shard_map/ppermute | solution.py:20
  39.6 9.0 %collective-permute-start.2 = (f32[130,128]{1,0:T(8,128)S(1)}, f32[130,128]{1,0:T(8,128)S(1)}, u32[]{:S(2)}, u32[]{:S(2)}) collective-permute-start(f32[130,128]{1,0:T(8,128)S(1)} %pad_maximum_fusion.2), channel_id=1, source_target_pairs={{0,64},{64,128},{128,192},{192,256},{256,320},{320,384},{384,448},... | collective-permute-start | bytes 199688 | tf_op jit(solution)/shard_map/ppermute | solution.py:16
  50.9 7.9 %collective-permute-start.3 = (f32[3,128]{1,0:T(4,128)S(1)}, f32[3,128]{1,0:T(4,128)S(1)}, u32[]{:S(2)}, u32[]{:S(2)}) collective-permute-start(f32[3,128]{1,0:T(4,128)S(1)} %pad_maximum_fusion.4), channel_id=1, source_target_pairs={{64,0},{128,64},{192,128},{256,192},{320,256},{384,320},{448,384},... | collective-permute-start | bytes 4616 | tf_op jit(solution)/shard_map/ppermute | solution.py:16
  60.0 3.6 %collective-permute-start.5 = (bf16[2,25,8,4,128]{4,3,2,1,0:T(4,128)(2,1)S(1)}, bf16[2,25,8,4,128]{4,3,2,1,0:T(4,128)(2,1)S(1)}, u32[]{:S(2)}, u32[]{:S(2)}) collective-permute-start(bf16[2,25,8,4,128]{4,3,2,1,0:T(4,128)(2,1)S(1)} %fusion.30), channel_id=1, source_target_pairs={{0,1},{1,0},{2,3},{3,2},{4,5},{5,4},{6,7},{7,6},{8,9},{9,8},{10,11... | collective-permute-start | bytes 1228808 | tf_op jit(solution)/shard_map/ppermute | solution.py:20
  65.0 20.9 %all-to-all-start.1 = ((bf16[32,2,25,128]{3,1,2,0:T(2,128)(2,1)}), bf16[32,2,25,128]{3,1,2,0:T(2,128)(2,1)S(1)}, u32[]{:S(2)}, u32[]{:S(2)}) async-start(bf16[32,2,25,128]{3,1,2,0:T(2,128)(2,1)} %bitcast.28), calls=%async_computation.1 | async-start | bytes 819200 | tf_op jit(solution)/shard_map/all_to_all | solution.py:153
  69.8 7.7 %collective-permute-start.4 = (f32[128,128]{1,0:T(8,128)S(1)}, f32[128,128]{1,0:T(8,128)S(1)}, u32[]{:S(2)}, u32[]{:S(2)}) collective-permute-start(f32[128,128]{1,0:T(8,128)S(1)} %fusion.45), channel_id=1, source_target_pairs={{0,64},{64,128},{128,192},{192,256},{256,320},{320,384},{384,448},... | collective-permute-start | bytes 196616 | tf_op jit(solution)/shard_map/ppermute | solution.py:16

commit v8 on v7

--- a/solution.py
+++ b/solution.py
@@ -58,8 +58,17 @@
     tokens = queries.shape[0]
     half = tokens // 2
 
-    served = passed_along(jnp.stack([queries[:half], cotangent[:half]]), "seq", -1)
-    query_next, grad_next = served[0], served[1]
+    flags = mask[:half].astype(jnp.bfloat16)
+    served = jnp.stack(
+        [
+            jnp.concatenate([queries[:half], flags[:, 0].reshape(-1, HD)]),
+            jnp.concatenate([cotangent[:half], flags[:, 1].reshape(-1, HD)]),
+        ]
+    )
+    served = passed_along(served, "seq", -1)
+    query_next, grad_next = served[0, :half], served[1, :half]
+    keep_own_next = served[0, half:].reshape(half).astype(jnp.float32)
+    keep_prev_next = served[1, half:].reshape(half).astype(jnp.float32)
 
     own_kv = jnp.stack([keys[0], values[0]])
     far = lax.axis_size("xh")
@@ -118,22 +127,45 @@
     ).astype(jnp.bfloat16)
     row_delta = jnp.sum(cotangent.astype(jnp.float32) * attended.astype(jnp.float32), axis=1)
 
-    control = jnp.stack(
-        [
-            jnp.where(seen, highest[:half], got_peak),
-            jnp.where(seen, 1.0 / totals[:half], 0.0),
-            row_delta[:half],
-        ]
-    )
-    control = passed_along(control, "seq", -1)
+    mine = jnp.concatenate(
+        [partial_own[:half], peak_own[:half].reshape(-1, HD), total_own[:half].reshape(-1, HD)]
+    )
+    mine = passed_along(mine, "seq", -1)
+    seen_next = keep_prev_next > 0
+    live_next = (keep_own_next + keep_prev_next > 0).astype(jnp.float32)
+    peak_own_next = mine[half : half + half // HD].reshape(half)
+    total_own_next = mine[half + half // HD :].reshape(half)
+    peak_prev_next = jnp.where(seen_next, peak_next, NEGATIVE)
+    highest_next = jnp.maximum(peak_own_next, peak_prev_next)
+    scale_own_next = jnp.exp(peak_own_next - highest_next)
+    scale_prev_next = jnp.exp(peak_prev_next - highest_next)
+    totals_next = scale_own_next * total_own_next + scale_prev_next * jnp.where(
+        seen_next, total_next, 0.0
+    )
+    totals_next = jnp.where(live_next > 0, totals_next, 1.0)
+    attended_next = (
+        live_next[:, None]
+        * (
+            scale_own_next[:, None] * mine[:half]
+            + scale_prev_next[:, None] * jnp.where(seen_next[:, None], partial_next, 0.0)
+        )
+        / totals_next[:, None]
+    ).astype(jnp.bfloat16)
+    delta_next = jnp.sum(
+        grad_next.astype(jnp.float32) * attended_next.astype(jnp.float32), axis=1
+    )
 
     weights_own = live_rows[:, None] * jnp.exp(score_own - highest[:, None]) / totals[:, None]
     gq_own, gk_own, gv_own = finish_backward(
         weights_own, cotangent, row_delta, queries, key_own, value_own
     )
-    weights_next = jnp.exp(score_next - control[0][:, None]) * control[1][:, None]
+    weights_next = jnp.where(
+        seen_next[:, None],
+        jnp.exp(score_next - highest_next[:, None]) / totals_next[:, None],
+        0.0,
+    )
     gq_next, gk_next, gv_next = finish_backward(
-        weights_next, grad_next, control[2], query_next, key_own, value_own
+        weights_next, grad_next, delta_next, query_next, key_own, value_own
     )
     gq_prev = passed_along(gq_next, "seq", 1)
     grad_query = (

time: 88.2 us -> 87.8 us (level)
  the two profiles are of different devices: /device:TPU:386 before, /device:TPU:402 now
where the time goes in v8:
time: 87.8 us; the launch traced here: 87.3 us
  starting transfers between devices  36.2 us (41%)
  waiting for transfers between devices  35.9 us (41%)
  matrix products  5.92 us (7%)
  local copies, waits for them, and re-layouts  4.38 us (5%)
  other arithmetic  3.86 us (4%)
  between operations  0.99 us (1%)
    ppermute x4, starting transfers between devices, passed_along(): return lax.ppermute(value, axis, pairs)  15.7 us
    all_to_all x1, waiting for transfers between devices, per_device(): lax.all_to_all(own_kv, ('y', 'xh'), split_axis=0, concat_axis=0, tiled=True)  15 us
    all_to_all x1, starting transfers between devices, per_device(): lax.all_to_all(own_kv, ('y', 'xh'), split_axis=0, concat_axis=0, tiled=True)  12.1 us
    ppermute x4, waiting for transfers between devices, passed_along(): return lax.ppermute(value, axis, pairs)  9.98 us
    all_to_all x1, waiting for transfers between devices, per_device(): lax.all_to_all(summed, ('y', 'xh'), split_axis=0, concat_axis=0, tiled=True)  7.55 us
    all_to_all x1, starting transfers between devices, per_device(): lax.all_to_all(summed, ('y', 'xh'), split_axis=0, concat_axis=0, tiled=True)  4.6 us
    ppermute x2, starting transfers between devices, partner(): return lax.ppermute(value, 'c', [(0, 1), (1, 0)])  3.83 us
    ppermute x2, waiting for transfers between devices, partner(): return lax.ppermute(value, 'c', [(0, 1), (1, 0)])  3.39 us
  transfers between devices with their start and end apart: 8, of which 7 were waited for; matrix products, arithmetic and copies ran while one was open for 4% of the time, Pallas kernels for 0%

profile of v8, /device:TPU:402, one launch (start us, length us, event | category | flops | bytes accessed | tf_op | source)
XLA Modules:
  0.0 87.3 jit_solution(2904780264420789347)
XLA Ops:
  0.6 0.0 slice-start
  0.7 0.0 slice-start.1
  0.7 0.9 maximum_bitcast_fusion
  1.5 0.1 copy.19
  1.6 1.0 %broadcast_in_dim.90 = bf16[8,4,2,3200]{3,2,1,0:T(2,128)(2,1)} broadcast(bf16[8,2,3200]{2,1,0:T(2,128)(2,1)S(1)} %copy.19), dimensions={0,2,3} | broadcast | bytes 512000 | tf_op jit(solution)/shard_map/broadcast_in_dim | solution.py:76
  2.6 12.1 %all-to-all-start = ((bf16[32,2,3200]{2,1,0:T(2,128)(2,1)}), bf16[32,2,3200]{2,1,0:T(2,128)(2,1)S(1)}, u32[]{:S(2)}, u32[]{:S(2)}) async-start(bf16[32,2,3200]{2,1,0:T(2,128)(2,1)} %bitcast.3), calls=%async_computation | async-start | bytes 819200 | tf_op jit(solution)/shard_map/all_to_all | solution.py:77
  14.8 3.3 %collective-permute-start.1 = (bf16[2,129,128]{2,1,0:T(8,128)(2,1)S(1)}, bf16[2,129,128]{2,1,0:T(8,128)(2,1)S(1)}, u32[]{:S(2)}, u32[]{:S(2)}) collective-permute-start(bf16[2,129,128]{2,1,0:T(8,128)(2,1)S(1)} %pad_maximum_fusion.2), channel_id=1, source_target_pairs={{64,0},{128,64},{192,128},{256,192},{320,256},{384,320},{448,384},... | collective-permute-start | bytes 198152 | tf_op jit(solution)/shard_map/ppermute | solution.py:16
  18.1 15.0 %all-to-all-done = bf16[32,2,3200]{2,1,0:T(2,128)(2,1)S(1)} async-done(((bf16[32,2,3200]{2,1,0:T(2,128)(2,1)}), bf16[32,2,3200]{2,1,0:T(2,128)(2,1)S(1)}, u32[]{:S(2)}, u32[]{:S(2)}) %all-to-all-start) | async-done | bytes 409632 | tf_op jit(solution)/shard_map/all_to_all | solution.py:77
  33.1 1.9 %collective-permute-start = (bf16[2,32,3200]{2,0,1:T(2,128)(2,1)S(1)}, bf16[2,32,3200]{2,0,1:T(2,128)(2,1)S(1)}, u32[]{:S(2)}, u32[]{:S(2)}) collective-permute-start(bf16[2,32,3200]{2,0,1:T(2,128)(2,1)S(1)} %bitcast.125), channel_id=1, source_target_pairs={{0,1},{1,0},{2,3},{3,2},{4,5},{5,4},{6,7},{7,6},{8,9},{9,8},{10,11... | collective-permute-start | bytes 1228808 | tf_op jit(solution)/shard_map/ppermute | solution.py:20
  35.1 1.7 %collective-permute-done = bf16[2,32,3200]{2,0,1:T(2,128)(2,1)S(1)} collective-permute-done((bf16[2,32,3200]{2,0,1:T(2,128)(2,1)S(1)}, bf16[2,32,3200]{2,0,1:T(2,128)(2,1)S(1)}, u32[]{:S(2)}, u32[]{:S(2)}) %collective-permute-start) | collective-permute-done | bytes 409632 | tf_op jit(solution)/shard_map/ppermute | solution.py:20
  36.8 1.1 %pad_maximum_fusion = bf16[2,64,3200]{2,0,1:T(2,128)(2,1)S(1)} fusion(bf16[2,32,3200]{2,0,1:T(2,128)(2,1)S(1)} %collective-permute-done, bf16[2,32,3200]{2,0,1:T(2,128)(2,1)S(1)} %bitcast.126), kind=kLoop, calls=%fused_computation.28 | loop fusion | flops 409600 | bytes 1638400 | tf_op jit(solution)/shard_map/concatenate | solution.py:79
  37.8 0.1 copy.20
  37.9 0.4 reshape.157
  38.3 0.1 fusion.48
  38.4 0.2 copy.21
  38.6 0.2 copy.22
  38.8 0.4 fusion.50
  39.1 0.2 fusion.22
  39.4 0.3 fusion.24
  39.7 6.5 %collective-permute-start.2 = (f32[130,128]{1,0:T(8,128)S(1)}, f32[130,128]{1,0:T(8,128)S(1)}, u32[]{:S(2)}, u32[]{:S(2)}) collective-permute-start(f32[130,128]{1,0:T(8,128)S(1)} %pad_maximum_fusion.3), channel_id=1, source_target_pairs={{0,64},{64,128},{128,192},{192,256},{256,320},{320,384},{384,448},... | collective-permute-start | bytes 199688 | tf_op jit(solution)/shard_map/ppermute | solution.py:16
  46.3 0.4 fusion.51
  46.7 0.3 fusion.15
  47.0 1.2 %collective-permute-done.2 = f32[130,128]{1,0:T(8,128)S(1)} collective-permute-done((f32[130,128]{1,0:T(8,128)S(1)}, f32[130,128]{1,0:T(8,128)S(1)}, u32[]{:S(2)}, u32[]{:S(2)}) %collective-permute-start.2) | collective-permute-done | bytes 66592 | tf_op jit(solution)/shard_map/ppermute | solution.py:16
  48.2 0.1 slice_select_fusion
  48.3 1.1 %multiply_reduce_fusion = (f32[256]{0:T(256)S(1)}, bf16[256,128]{1,0:T(8,128)(2,1)}, f32[256,128]{1,0:T(8,128)S(1)}) fusion(bf16[256,128]{1,0:T(8,128)(2,1)S(1)} %copy-done.1, f32[256]{0:T(256)S(1)} %get-tuple-element.15, f32[128,128]{1,0:T(8,128)S(1)} %slice_select_fusion, f32[256]{0:T(256)S(1)} %get-tuple-element.17, f32[256]{0:T(256)S(1)} %get-tuple-element.16, ...), kind=kOutput, calls=%fused_computation.50 | convolution fusion | flops 106004224 | bytes 2381824 | tf_op jit(solution)/shard_map/dot_general | solution.py:31
  49.4 1.9 %collective-permute-start.3 = (f32[130,128]{1,0:T(8,128)S(1)}, f32[130,128]{1,0:T(8,128)S(1)}, u32[]{:S(2)}, u32[]{:S(2)}) collective-permute-start(f32[130,128]{1,0:T(8,128)S(1)} %pad_maximum_fusion.4), channel_id=1, source_target_pairs={{64,0},{128,64},{192,128},{256,192},{320,256},{384,320},{448,384},... | collective-permute-start | bytes 199688 | tf_op jit(solution)/shard_map/ppermute | solution.py:16
  51.4 0.4 fusion.10
  51.8 0.6 fusion.3
  52.4 0.4 fusion.14
  52.7 5.3 %collective-permute-done.3 = f32[130,128]{1,0:T(8,128)S(1)} collective-permute-done((f32[130,128]{1,0:T(8,128)S(1)}, f32[130,128]{1,0:T(8,128)S(1)}, u32[]{:S(2)}, u32[]{:S(2)}) %collective-permute-start.3) | collective-permute-done | bytes 66592 | tf_op jit(solution)/shard_map/ppermute | solution.py:16
  58.1 0.2 multiply_reduce_fusion.1
  58.3 0.4 fusion.6
  58.7 0.3 fusion.9
  59.0 0.2 fusion.13
  59.2 0.3 fusion.29
  59.5 1.9 %collective-permute-start.5 = (bf16[2,25,8,4,128]{4,3,2,1,0:T(4,128)(2,1)S(1)}, bf16[2,25,8,4,128]{4,3,2,1,0:T(4,128)(2,1)S(1)}, u32[]{:S(2)}, u32[]{:S(2)}) collective-permute-start(bf16[2,25,8,4,128]{4,3,2,1,0:T(4,128)(2,1)S(1)} %fusion.29), channel_id=1, source_target_pairs={{0,1},{1,0},{2,3},{3,2},{4,5},{5,4},{6,7},{7,6},{8,9},{9,8},{10,11... | collective-permute-start | bytes 1228808 | tf_op jit(solution)/shard_map/ppermute | solution.py:20
  61.5 1.7 %collective-permute-done.5 = bf16[2,25,8,4,128]{4,3,2,1,0:T(4,128)(2,1)S(1)} collective-permute-done((bf16[2,25,8,4,128]{4,3,2,1,0:T(4,128)(2,1)S(1)}, bf16[2,25,8,4,128]{4,3,2,1,0:T(4,128)(2,1)S(1)}, u32[]{:S(2)}, u32[]{:S(2)}) %collective-permute-start.5) | collective-permute-done | bytes 409632 | tf_op jit(solution)/shard_map/ppermute | solution.py:20
  63.2 0.3 fusion.26
  63.5 1.1 %copy.24 = bf16[8,4,2,25,128]{4,2,3,1,0:T(2,128)(2,1)} copy(bf16[8,4,2,25,128]{4,1,0,3,2:T(4,128)(2,1)S(1)} %fusion.26) | data formatting | bytes 819200 | tf_op jit(solution)/shard_map/transpose | solution.py:183
  64.6 4.6 %all-to-all-start.1 = ((bf16[32,2,25,128]{3,1,2,0:T(2,128)(2,1)}), bf16[32,2,25,128]{3,1,2,0:T(2,128)(2,1)S(1)}, u32[]{:S(2)}, u32[]{:S(2)}) async-start(bf16[32,2,25,128]{3,1,2,0:T(2,128)(2,1)} %bitcast.30), calls=%async_computation.1 | async-start | bytes 819200 | tf_op jit(solution)/shard_map/all_to_all | solution.py:185
  69.2 0.3 fusion.52
  69.5 3.9 %collective-permute-start.4 = (f32[128,128]{1,0:T(8,128)S(1)}, f32[128,128]{1,0:T(8,128)S(1)}, u32[]{:S(2)}, u32[]{:S(2)}) collective-permute-start(f32[128,128]{1,0:T(8,128)S(1)} %fusion.52), channel_id=1, source_target_pairs={{0,64},{64,128},{128,192},{192,256},{256,320},{320,384},{384,448},... | collective-permute-start | bytes 196616 | tf_op jit(solution)/shard_map/ppermute | solution.py:16
  73.4 3.5 %collective-permute-done.4 = f32[128,128]{1,0:T(8,128)S(1)} collective-permute-done((f32[128,128]{1,0:T(8,128)S(1)}, f32[128,128]{1,0:T(8,128)S(1)}, u32[]{:S(2)}, u32[]{:S(2)}) %collective-permute-start.4) | collective-permute-done | bytes 65568 | tf_op jit(solution)/shard_map/ppermute | solution.py:16
  76.9 1.1 %add_convert_fusion = bf16[256,128]{1,0:T(8,128)(2,1)} fusion(f32[128,128]{1,0:T(8,128)S(1)} %collective-permute-done.4, bf16[1600,256]{1,0:T(8,128)(2,1)S(1)} %fusion.3, bf16[1600,128]{1,0:T(8,128)(2,1)S(1)} %bitcast.117), kind=kOutput, calls=%fused_computation.49 | convolution fusion | flops 104923136 | bytes 1359872 | tf_op jit(solution)/shard_map/dot_general | solution.py:44
  78.0 7.6 %all-to-all-done.1 = bf16[32,2,25,128]{3,1,2,0:T(2,128)(2,1)S(1)} async-done(((bf16[32,2,25,128]{3,1,2,0:T(2,128)(2,1)}), bf16[32,2,25,128]{3,1,2,0:T(2,128)(2,1)S(1)}, u32[]{:S(2)}, u32[]{:S(2)}) %all-to-all-start.1) | async-done | bytes 409632 | tf_op jit(solution)/shard_map/all_to_all | solution.py:185
  85.5 0.4 bitcast_reduce_fusion
  86.0 0.6 copy.26
  86.6 0.6 copy.27
  (25 shorter events, 0.2 us)
Async XLA Ops:
  0.6 14.0 %copy-start.2 = (s32[256,2]{0,1:T(2,128)S(1)}, s32[256,2]{0,1:T(2,128)}, u32[]{:S(2)}) copy-start(s32[256,2]{0,1:T(2,128)} %param.9) | copy-start | bytes 6148
  0.6 14.1 %slice-start = ((bf16[256,128]{1,0:T(8,128)(2,1)}), bf16[128,128]{1,0:T(8,128)(2,1)S(1)}, s32[]{:S(2)}) async-start(bf16[256,128]{1,0:T(8,128)(2,1)} %param.5), calls=%async_computation.2 | async-start | bytes 65536 | tf_op jit(solution)/shard_map/slice | solution.py:64
  0.7 14.1 %slice-start.1 = ((bf16[256,128]{1,0:T(8,128)(2,1)}), bf16[128,128]{1,0:T(8,128)(2,1)S(1)}, s32[]{:S(2)}) async-start(bf16[256,128]{1,0:T(8,128)(2,1)} %param.8), calls=%async_computation.3 | async-start | bytes 65536 | tf_op jit(solution)/shard_map/slice | solution.py:65
  2.6 30.5 %all-to-all-start = ((bf16[32,2,3200]{2,1,0:T(2,128)(2,1)}), bf16[32,2,3200]{2,1,0:T(2,128)(2,1)S(1)}, u32[]{:S(2)}, u32[]{:S(2)}) async-start(bf16[32,2,3200]{2,1,0:T(2,128)(2,1)} %bitcast.3), calls=%async_computation | async-start | bytes 819200 | tf_op jit(solution)/shard_map/all_to_all | solution.py:77
  14.8 20.3 %collective-permute-start.1 = (bf16[2,129,128]{2,1,0:T(8,128)(2,1)S(1)}, bf16[2,129,128]{2,1,0:T(8,128)(2,1)S(1)}, u32[]{:S(2)}, u32[]{:S(2)}) collective-permute-start(bf16[2,129,128]{2,1,0:T(8,128)(2,1)S(1)} %pad_maximum_fusion.2), channel_id=1, source_target_pairs={{64,0},{128,64},{192,128},{256,192},{320,256},{384,320},{448,384},... | collective-permute-start | bytes 198152 | tf_op jit(solution)/shard_map/ppermute | solution.py:16
  33.1 3.6 %collective-permute-start = (bf16[2,32,3200]{2,0,1:T(2,128)(2,1)S(1)}, bf16[2,32,3200]{2,0,1:T(2,128)(2,1)S(1)}, u32[]{:S(2)}, u32[]{:S(2)}) collective-permute-start(bf16[2,32,3200]{2,0,1:T(2,128)(2,1)S(1)} %bitcast.125), channel_id=1, source_target_pairs={{0,1},{1,0},{2,3},{3,2},{4,5},{5,4},{6,7},{7,6},{8,9},{9,8},{10,11... | collective-permute-start | bytes 1228808 | tf_op jit(solution)/shard_map/ppermute | solution.py:20
  38.7 7.5 %copy-start = (bf16[256,128]{1,0:T(8,128)(2,1)S(1)}, bf16[256,128]{1,0:T(8,128)(2,1)}, u32[]{:S(2)}) copy-start(bf16[256,128]{1,0:T(8,128)(2,1)} %param.5) | copy-start | bytes 196612
  39.7 8.4 %collective-permute-start.2 = (f32[130,128]{1,0:T(8,128)S(1)}, f32[130,128]{1,0:T(8,128)S(1)}, u32[]{:S(2)}, u32[]{:S(2)}) collective-permute-start(f32[130,128]{1,0:T(8,128)S(1)} %pad_maximum_fusion.3), channel_id=1, source_target_pairs={{0,64},{64,128},{128,192},{192,256},{256,320},{320,384},{384,448},... | collective-permute-start | bytes 199688 | tf_op jit(solution)/shard_map/ppermute | solution.py:16
  46.2 2.0 %copy-start.1 = (bf16[256,128]{1,0:T(8,128)(2,1)S(1)}, bf16[256,128]{1,0:T(8,128)(2,1)}, u32[]{:S(2)}) copy-start(bf16[256,128]{1,0:T(8,128)(2,1)} %param.8) | copy-start | bytes 196612
  49.4 8.7 %collective-permute-start.3 = (f32[130,128]{1,0:T(8,128)S(1)}, f32[130,128]{1,0:T(8,128)S(1)}, u32[]{:S(2)}, u32[]{:S(2)}) collective-permute-start(f32[130,128]{1,0:T(8,128)S(1)} %pad_maximum_fusion.4), channel_id=1, source_target_pairs={{64,0},{128,64},{192,128},{256,192},{320,256},{384,320},{448,384},... | collective-permute-start | bytes 199688 | tf_op jit(solution)/shard_map/ppermute | solution.py:16
  59.5 3.6 %collective-permute-start.5 = (bf16[2,25,8,4,128]{4,3,2,1,0:T(4,128)(2,1)S(1)}, bf16[2,25,8,4,128]{4,3,2,1,0:T(4,128)(2,1)S(1)}, u32[]{:S(2)}, u32[]{:S(2)}) collective-permute-start(bf16[2,25,8,4,128]{4,3,2,1,0:T(4,128)(2,1)S(1)} %fusion.29), channel_id=1, source_target_pairs={{0,1},{1,0},{2,3},{3,2},{4,5},{5,4},{6,7},{7,6},{8,9},{9,8},{10,11... | collective-permute-start | bytes 1228808 | tf_op jit(solution)/shard_map/ppermute | solution.py:20
  64.6 21.0 %all-to-all-start.1 = ((bf16[32,2,25,128]{3,1,2,0:T(2,128)(2,1)}), bf16[32,2,25,128]{3,1,2,0:T(2,128)(2,1)S(1)}, u32[]{:S(2)}, u32[]{:S(2)}) async-start(bf16[32,2,25,128]{3,1,2,0:T(2,128)(2,1)} %bitcast.30), calls=%async_computation.1 | async-start | bytes 819200 | tf_op jit(solution)/shard_map/all_to_all | solution.py:185
  69.5 7.4 %collective-permute-start.4 = (f32[128,128]{1,0:T(8,128)S(1)}, f32[128,128]{1,0:T(8,128)S(1)}, u32[]{:S(2)}, u32[]{:S(2)}) collective-permute-start(f32[128,128]{1,0:T(8,128)S(1)} %fusion.52), channel_id=1, source_target_pairs={{0,64},{64,128},{128,192},{192,256},{256,320},{320,384},{384,448},... | collective-permute-start | bytes 196616 | tf_op jit(solution)/shard_map/ppermute | solution.py:16

commit v9 on v8

--- a/solution.py
+++ b/solution.py
@@ -88,6 +88,12 @@
         queries, key_own, value_own, keep_own
     )
 
+    mine = jnp.concatenate(
+        [partial_own[:half], peak_own[:half].reshape(-1, HD), total_own[:half].reshape(-1, HD)]
+    )
+    mine, query_next = lax.optimization_barrier((mine, query_next))
+    mine = passed_along(mine, "seq", -1)
+
     score_next = jnp.einsum(
         "rd,kd->rk", query_next, key_own, preferred_element_type=jnp.float32
     ) * HD ** (-0.5)
@@ -127,10 +133,6 @@
     ).astype(jnp.bfloat16)
     row_delta = jnp.sum(cotangent.astype(jnp.float32) * attended.astype(jnp.float32), axis=1)
 
-    mine = jnp.concatenate(
-        [partial_own[:half], peak_own[:half].reshape(-1, HD), total_own[:half].reshape(-1, HD)]
-    )
-    mine = passed_along(mine, "seq", -1)
     seen_next = keep_prev_next > 0
     live_next = (keep_own_next + keep_prev_next > 0).astype(jnp.float32)
     peak_own_next = mine[half : half + half // HD].reshape(half)

time: 87.8 us -> 89.3 us (1.017)
  the two profiles are of different devices: /device:TPU:402 before, /device:TPU:400 now
where the time goes in v9:
time: 89.3 us; the launch traced here: 88.7 us
  waiting for transfers between devices  37.4 us (42%)
  starting transfers between devices  35.5 us (40%)
  matrix products  5.36 us (6%)
  local copies, waits for them, and re-layouts  4.96 us (6%)
  other arithmetic  4.47 us (5%)
  between operations  1.01 us (1%)
    all_to_all x1, waiting for transfers between devices, per_device(): lax.all_to_all(own_kv, ('y', 'xh'), split_axis=0, concat_axis=0, tiled=True)  15.6 us
    ppermute x4, starting transfers between devices, passed_along(): return lax.ppermute(value, axis, pairs)  14.2 us
    all_to_all x1, starting transfers between devices, per_device(): lax.all_to_all(own_kv, ('y', 'xh'), split_axis=0, concat_axis=0, tiled=True)  13 us
    ppermute x4, waiting for transfers between devices, passed_along(): return lax.ppermute(value, axis, pairs)  10.8 us
    all_to_all x1, waiting for transfers between devices, per_device(): lax.all_to_all(summed, ('y', 'xh'), split_axis=0, concat_axis=0, tiled=True)  7.56 us
    all_to_all x1, starting transfers between devices, per_device(): lax.all_to_all(summed, ('y', 'xh'), split_axis=0, concat_axis=0, tiled=True)  4.58 us
    ppermute x2, starting transfers between devices, partner(): return lax.ppermute(value, 'c', [(0, 1), (1, 0)])  3.83 us
    ppermute x2, waiting for transfers between devices, partner(): return lax.ppermute(value, 'c', [(0, 1), (1, 0)])  3.39 us
  transfers between devices with their start and end apart: 8, of which 7 were waited for; matrix products, arithmetic and copies ran while one was open for 2% of the time, Pallas kernels for 0%

profile of v9, /device:TPU:400, one launch (start us, length us, event | category | flops | bytes accessed | tf_op | source)
XLA Modules:
  0.0 88.7 jit_solution(558792625544469732)
XLA Ops:
  0.6 0.0 slice-start
  0.7 0.9 maximum_bitcast_fusion
  1.5 0.1 copy.19
  1.6 1.0 %broadcast_in_dim.90 = bf16[8,4,2,3200]{3,2,1,0:T(2,128)(2,1)} broadcast(bf16[8,2,3200]{2,1,0:T(2,128)(2,1)S(1)} %copy.19), dimensions={0,2,3} | broadcast | bytes 512000 | tf_op jit(solution)/shard_map/broadcast_in_dim | solution.py:76
  2.6 13.0 %all-to-all-start = ((bf16[32,2,3200]{2,1,0:T(2,128)(2,1)}), bf16[32,2,3200]{2,1,0:T(2,128)(2,1)S(1)}, u32[]{:S(2)}, u32[]{:S(2)}) async-start(bf16[32,2,3200]{2,1,0:T(2,128)(2,1)} %bitcast.3), calls=%async_computation | async-start | bytes 819200 | tf_op jit(solution)/shard_map/all_to_all | solution.py:77
  15.6 1.9 %collective-permute-start.1 = (bf16[2,129,128]{2,1,0:T(8,128)(2,1)S(1)}, bf16[2,129,128]{2,1,0:T(8,128)(2,1)S(1)}, u32[]{:S(2)}, u32[]{:S(2)}) collective-permute-start(bf16[2,129,128]{2,1,0:T(8,128)(2,1)S(1)} %pad_maximum_fusion.3), channel_id=1, source_target_pairs={{64,0},{128,64},{192,128},{256,192},{320,256},{384,320},{448,384},... | collective-permute-start | bytes 198152 | tf_op jit(solution)/shard_map/ppermute | solution.py:16
  17.6 15.6 %all-to-all-done = bf16[32,2,3200]{2,1,0:T(2,128)(2,1)S(1)} async-done(((bf16[32,2,3200]{2,1,0:T(2,128)(2,1)}), bf16[32,2,3200]{2,1,0:T(2,128)(2,1)S(1)}, u32[]{:S(2)}, u32[]{:S(2)}) %all-to-all-start) | async-done | bytes 409632 | tf_op jit(solution)/shard_map/all_to_all | solution.py:77
  33.2 1.9 %collective-permute-start = (bf16[2,32,3200]{2,0,1:T(2,128)(2,1)S(1)}, bf16[2,32,3200]{2,0,1:T(2,128)(2,1)S(1)}, u32[]{:S(2)}, u32[]{:S(2)}) collective-permute-start(bf16[2,32,3200]{2,0,1:T(2,128)(2,1)S(1)} %bitcast.123), channel_id=1, source_target_pairs={{0,1},{1,0},{2,3},{3,2},{4,5},{5,4},{6,7},{7,6},{8,9},{9,8},{10,11... | collective-permute-start | bytes 1228808 | tf_op jit(solution)/shard_map/ppermute | solution.py:20
  35.2 1.7 %collective-permute-done = bf16[2,32,3200]{2,0,1:T(2,128)(2,1)S(1)} collective-permute-done((bf16[2,32,3200]{2,0,1:T(2,128)(2,1)S(1)}, bf16[2,32,3200]{2,0,1:T(2,128)(2,1)S(1)}, u32[]{:S(2)}, u32[]{:S(2)}) %collective-permute-start) | collective-permute-done | bytes 409632 | tf_op jit(solution)/shard_map/ppermute | solution.py:20
  36.9 1.1 %pad_maximum_fusion = bf16[2,64,3200]{2,0,1:T(2,128)(2,1)S(1)} fusion(bf16[2,32,3200]{2,0,1:T(2,128)(2,1)S(1)} %collective-permute-done, bf16[2,32,3200]{2,0,1:T(2,128)(2,1)S(1)} %bitcast.124), kind=kLoop, calls=%fused_computation.28 | loop fusion | flops 409600 | bytes 1638400 | tf_op jit(solution)/shard_map/concatenate | solution.py:79
  37.9 0.1 copy.20
  38.0 0.4 reshape.157
  38.5 0.1 fusion.48
  38.5 0.2 copy.21
  38.7 0.6 copy-done
  39.3 0.4 fusion.50
  39.7 0.3 fusion.15
  40.0 0.2 copy.22
  40.2 0.5 fusion.17
  40.7 0.4 fusion.51
  41.1 1.9 %collective-permute-start.3 = (f32[130,128]{1,0:T(8,128)S(1)}, f32[130,128]{1,0:T(8,128)S(1)}, u32[]{:S(2)}, u32[]{:S(2)}) collective-permute-start(f32[130,128]{1,0:T(8,128)S(1)} %pad_maximum_fusion.2), channel_id=1, source_target_pairs={{64,0},{128,64},{192,128},{256,192},{320,256},{384,320},{448,384},... | collective-permute-start | bytes 199688 | tf_op jit(solution)/shard_map/ppermute | solution.py:16
  43.0 0.2 fusion.22
  43.3 4.0 %collective-permute-done.3 = f32[130,128]{1,0:T(8,128)S(1)} collective-permute-done((f32[130,128]{1,0:T(8,128)S(1)}, f32[130,128]{1,0:T(8,128)S(1)}, u32[]{:S(2)}, u32[]{:S(2)}) %collective-permute-start.3) | collective-permute-done | bytes 66592 | tf_op jit(solution)/shard_map/ppermute | solution.py:16
  47.3 0.4 multiply_reduce_fusion.1
  47.8 6.0 %collective-permute-start.2 = (f32[130,128]{1,0:T(8,128)S(1)}, f32[130,128]{1,0:T(8,128)S(1)}, u32[]{:S(2)}, u32[]{:S(2)}) collective-permute-start(f32[130,128]{1,0:T(8,128)S(1)} %pad_maximum_fusion.4), channel_id=1, source_target_pairs={{0,64},{64,128},{128,192},{192,256},{256,320},{320,384},{384,448},... | collective-permute-start | bytes 199688 | tf_op jit(solution)/shard_map/ppermute | solution.py:16
  53.8 0.4 fusion.6
  54.2 1.5 %collective-permute-done.2 = f32[130,128]{1,0:T(8,128)S(1)} collective-permute-done((f32[130,128]{1,0:T(8,128)S(1)}, f32[130,128]{1,0:T(8,128)S(1)}, u32[]{:S(2)}, u32[]{:S(2)}) %collective-permute-start.2) | collective-permute-done | bytes 66592 | tf_op jit(solution)/shard_map/ppermute | solution.py:16
  55.8 0.4 fusion.10
  56.2 0.1 slice_select_fusion
  56.3 0.8 multiply_reduce_fusion
  57.1 0.6 fusion.3
  57.7 0.4 fusion.14
  58.1 0.3 fusion.13
  58.3 0.3 fusion.9
  58.6 0.3 fusion.29
  58.9 1.9 %collective-permute-start.5 = (bf16[2,25,8,4,128]{4,3,2,1,0:T(4,128)(2,1)S(1)}, bf16[2,25,8,4,128]{4,3,2,1,0:T(4,128)(2,1)S(1)}, u32[]{:S(2)}, u32[]{:S(2)}) collective-permute-start(bf16[2,25,8,4,128]{4,3,2,1,0:T(4,128)(2,1)S(1)} %fusion.29), channel_id=1, source_target_pairs={{0,1},{1,0},{2,3},{3,2},{4,5},{5,4},{6,7},{7,6},{8,9},{9,8},{10,11... | collective-permute-start | bytes 1228808 | tf_op jit(solution)/shard_map/ppermute | solution.py:20
  60.8 1.7 %collective-permute-done.5 = bf16[2,25,8,4,128]{4,3,2,1,0:T(4,128)(2,1)S(1)} collective-permute-done((bf16[2,25,8,4,128]{4,3,2,1,0:T(4,128)(2,1)S(1)}, bf16[2,25,8,4,128]{4,3,2,1,0:T(4,128)(2,1)S(1)}, u32[]{:S(2)}, u32[]{:S(2)}) %collective-permute-start.5) | collective-permute-done | bytes 409632 | tf_op jit(solution)/shard_map/ppermute | solution.py:20
  62.6 0.3 fusion.26
  62.9 1.1 %copy.24 = bf16[8,4,2,25,128]{4,2,3,1,0:T(2,128)(2,1)} copy(bf16[8,4,2,25,128]{4,1,0,3,2:T(4,128)(2,1)S(1)} %fusion.26) | data formatting | bytes 819200 | tf_op jit(solution)/shard_map/transpose | solution.py:185
  63.9 4.6 %all-to-all-start.1 = ((bf16[32,2,25,128]{3,1,2,0:T(2,128)(2,1)}), bf16[32,2,25,128]{3,1,2,0:T(2,128)(2,1)S(1)}, u32[]{:S(2)}, u32[]{:S(2)}) async-start(bf16[32,2,25,128]{3,1,2,0:T(2,128)(2,1)} %bitcast.30), calls=%async_computation.1 | async-start | bytes 819200 | tf_op jit(solution)/shard_map/all_to_all | solution.py:187
  68.5 0.3 fusion.52
  68.8 4.3 %collective-permute-start.4 = (f32[128,128]{1,0:T(8,128)S(1)}, f32[128,128]{1,0:T(8,128)S(1)}, u32[]{:S(2)}, u32[]{:S(2)}) collective-permute-start(f32[128,128]{1,0:T(8,128)S(1)} %fusion.52), channel_id=1, source_target_pairs={{0,64},{64,128},{128,192},{192,256},{256,320},{320,384},{384,448},... | collective-permute-start | bytes 196616 | tf_op jit(solution)/shard_map/ppermute | solution.py:16
  73.1 5.3 %collective-permute-done.4 = f32[128,128]{1,0:T(8,128)S(1)} collective-permute-done((f32[128,128]{1,0:T(8,128)S(1)}, f32[128,128]{1,0:T(8,128)S(1)}, u32[]{:S(2)}, u32[]{:S(2)}) %collective-permute-start.4) | collective-permute-done | bytes 65568 | tf_op jit(solution)/shard_map/ppermute | solution.py:16
  78.4 1.1 %add_convert_fusion = bf16[256,128]{1,0:T(8,128)(2,1)} fusion(f32[128,128]{1,0:T(8,128)S(1)} %collective-permute-done.4, bf16[1600,256]{1,0:T(8,128)(2,1)S(1)} %fusion.3, bf16[1600,128]{1,0:T(8,128)(2,1)S(1)} %bitcast.115), kind=kOutput, calls=%fused_computation.49 | convolution fusion | flops 104923136 | bytes 1359872 | tf_op jit(solution)/shard_map/dot_general | solution.py:44
  79.5 7.6 %all-to-all-done.1 = bf16[32,2,25,128]{3,1,2,0:T(2,128)(2,1)S(1)} async-done(((bf16[32,2,25,128]{3,1,2,0:T(2,128)(2,1)}), bf16[32,2,25,128]{3,1,2,0:T(2,128)(2,1)S(1)}, u32[]{:S(2)}, u32[]{:S(2)}) %all-to-all-start.1) | async-done | bytes 409632 | tf_op jit(solution)/shard_map/all_to_all | solution.py:187
  87.0 0.4 bitcast_reduce_fusion
  87.5 0.6 copy.26
  88.1 0.6 copy.27
  (26 shorter events, 0.2 us)
Async XLA Ops:
  0.6 14.9 %copy-start.2 = (s32[256,2]{0,1:T(2,128)S(1)}, s32[256,2]{0,1:T(2,128)}, u32[]{:S(2)}) copy-start(s32[256,2]{0,1:T(2,128)} %param.9) | copy-start | bytes 6148
  0.6 15.0 %slice-start = ((bf16[256,128]{1,0:T(8,128)(2,1)}), bf16[128,128]{1,0:T(8,128)(2,1)S(1)}, s32[]{:S(2)}) async-start(bf16[256,128]{1,0:T(8,128)(2,1)} %param.5), calls=%async_computation.2 | async-start | bytes 65536 | tf_op jit(solution)/shard_map/slice | solution.py:64
  0.7 15.0 %slice-start.1 = ((bf16[256,128]{1,0:T(8,128)(2,1)}), bf16[128,128]{1,0:T(8,128)(2,1)S(1)}, s32[]{:S(2)}) async-start(bf16[256,128]{1,0:T(8,128)(2,1)} %param.8), calls=%async_computation.3 | async-start | bytes 65536 | tf_op jit(solution)/shard_map/slice | solution.py:65
  2.6 30.7 %all-to-all-start = ((bf16[32,2,3200]{2,1,0:T(2,128)(2,1)}), bf16[32,2,3200]{2,1,0:T(2,128)(2,1)S(1)}, u32[]{:S(2)}, u32[]{:S(2)}) async-start(bf16[32,2,3200]{2,1,0:T(2,128)(2,1)} %bitcast.3), calls=%async_computation | async-start | bytes 819200 | tf_op jit(solution)/shard_map/all_to_all | solution.py:77
  15.6 19.5 %collective-permute-start.1 = (bf16[2,129,128]{2,1,0:T(8,128)(2,1)S(1)}, bf16[2,129,128]{2,1,0:T(8,128)(2,1)S(1)}, u32[]{:S(2)}, u32[]{:S(2)}) collective-permute-start(bf16[2,129,128]{2,1,0:T(8,128)(2,1)S(1)} %pad_maximum_fusion.3), channel_id=1, source_target_pairs={{64,0},{128,64},{192,128},{256,192},{320,256},{384,320},{448,384},... | collective-permute-start | bytes 198152 | tf_op jit(solution)/shard_map/ppermute | solution.py:16
  33.2 3.6 %collective-permute-start = (bf16[2,32,3200]{2,0,1:T(2,128)(2,1)S(1)}, bf16[2,32,3200]{2,0,1:T(2,128)(2,1)S(1)}, u32[]{:S(2)}, u32[]{:S(2)}) collective-permute-start(bf16[2,32,3200]{2,0,1:T(2,128)(2,1)S(1)} %bitcast.123), channel_id=1, source_target_pairs={{0,1},{1,0},{2,3},{3,2},{4,5},{5,4},{6,7},{7,6},{8,9},{9,8},{10,11... | collective-permute-start | bytes 1228808 | tf_op jit(solution)/shard_map/ppermute | solution.py:20
  38.4 0.8 copy-start
  41.1 6.2 %collective-permute-start.3 = (f32[130,128]{1,0:T(8,128)S(1)}, f32[130,128]{1,0:T(8,128)S(1)}, u32[]{:S(2)}, u32[]{:S(2)}) collective-permute-start(f32[130,128]{1,0:T(8,128)S(1)} %pad_maximum_fusion.2), channel_id=1, source_target_pairs={{64,0},{128,64},{192,128},{256,192},{320,256},{384,320},{448,384},... | collective-permute-start | bytes 199688 | tf_op jit(solution)/shard_map/ppermute | solution.py:16
  47.8 8.0 %collective-permute-start.2 = (f32[130,128]{1,0:T(8,128)S(1)}, f32[130,128]{1,0:T(8,128)S(1)}, u32[]{:S(2)}, u32[]{:S(2)}) collective-permute-start(f32[130,128]{1,0:T(8,128)S(1)} %pad_maximum_fusion.4), channel_id=1, source_target_pairs={{0,64},{64,128},{128,192},{192,256},{256,320},{320,384},{384,448},... | collective-permute-start | bytes 199688 | tf_op jit(solution)/shard_map/ppermute | solution.py:16
  53.8 1.9 %copy-start.1 = (bf16[256,128]{1,0:T(8,128)(2,1)S(1)}, bf16[256,128]{1,0:T(8,128)(2,1)}, u32[]{:S(2)}) copy-start(bf16[256,128]{1,0:T(8,128)(2,1)} %param.8) | copy-start | bytes 196612
  58.9 3.6 %collective-permute-start.5 = (bf16[2,25,8,4,128]{4,3,2,1,0:T(4,128)(2,1)S(1)}, bf16[2,25,8,4,128]{4,3,2,1,0:T(4,128)(2,1)S(1)}, u32[]{:S(2)}, u32[]{:S(2)}) collective-permute-start(bf16[2,25,8,4,128]{4,3,2,1,0:T(4,128)(2,1)S(1)} %fusion.29), channel_id=1, source_target_pairs={{0,1},{1,0},{2,3},{3,2},{4,5},{5,4},{6,7},{7,6},{8,9},{9,8},{10,11... | collective-permute-start | bytes 1228808 | tf_op jit(solution)/shard_map/ppermute | solution.py:20
  63.9 23.1 %all-to-all-start.1 = ((bf16[32,2,25,128]{3,1,2,0:T(2,128)(2,1)}), bf16[32,2,25,128]{3,1,2,0:T(2,128)(2,1)S(1)}, u32[]{:S(2)}, u32[]{:S(2)}) async-start(bf16[32,2,25,128]{3,1,2,0:T(2,128)(2,1)} %bitcast.30), calls=%async_computation.1 | async-start | bytes 819200 | tf_op jit(solution)/shard_map/all_to_all | solution.py:187
  68.8 9.5 %collective-permute-start.4 = (f32[128,128]{1,0:T(8,128)S(1)}, f32[128,128]{1,0:T(8,128)S(1)}, u32[]{:S(2)}, u32[]{:S(2)}) collective-permute-start(f32[128,128]{1,0:T(8,128)S(1)} %fusion.52), channel_id=1, source_target_pairs={{0,64},{64,128},{128,192},{192,256},{256,320},{320,384},{384,448},... | collective-permute-start | bytes 196616 | tf_op jit(solution)/shard_map/ppermute | solution.py:16

commit v10 on v8

--- a/solution.py
+++ b/solution.py
@@ -98,33 +98,10 @@
         value_own,
         preferred_element_type=jnp.float32,
     )
-    stats = jnp.concatenate(
-        [partial_next, peak_next.reshape(-1, HD), total_next.reshape(-1, HD)]
-    )
-    stats = passed_along(stats, "seq", 1)
     seen = keep_prev[:half] > 0
-    got_peak = stats[half : half + half // HD].reshape(half)
-    got_total = stats[half + half // HD :].reshape(half)
     rest = tokens - half
-    peak_prev = jnp.concatenate(
-        [jnp.where(seen, got_peak, NEGATIVE), jnp.full((rest,), NEGATIVE, jnp.float32)]
-    )
-    total_prev = jnp.concatenate(
-        [jnp.where(seen, got_total, 0.0), jnp.zeros((rest,), jnp.float32)]
-    )
-    partial_prev = jnp.concatenate(
-        [jnp.where(seen[:, None], stats[:half], 0.0), jnp.zeros((rest, HD), jnp.float32)]
-    )
-
-    highest = jnp.maximum(peak_own, peak_prev)
-    scale_own = jnp.exp(peak_own - highest)
-    scale_prev = jnp.exp(peak_prev - highest)
-    totals = scale_own * total_own + scale_prev * total_prev
-    attended = (
-        live_rows[:, None]
-        * (scale_own[:, None] * partial_own + scale_prev[:, None] * partial_prev)
-        / totals[:, None]
-    ).astype(jnp.bfloat16)
+    totals = jnp.where(live_rows > 0, total_own, 1.0)
+    attended = (live_rows[:, None] * partial_own / totals[:, None]).astype(jnp.bfloat16)
     row_delta = jnp.sum(cotangent.astype(jnp.float32) * attended.astype(jnp.float32), axis=1)
 
     mine = jnp.concatenate(
@@ -155,10 +132,6 @@
         grad_next.astype(jnp.float32) * attended_next.astype(jnp.float32), axis=1
     )
 
-    weights_own = live_rows[:, None] * jnp.exp(score_own - highest[:, None]) / totals[:, None]
-    gq_own, gk_own, gv_own = finish_backward(
-        weights_own, cotangent, row_delta, queries, key_own, value_own
-    )
     weights_next = jnp.where(
         seen_next[:, None],
         jnp.exp(score_next - highest_next[:, None]) / totals_next[:, None],
@@ -167,9 +140,34 @@
     gq_next, gk_next, gv_next = finish_backward(
         weights_next, grad_next, delta_next, query_next, key_own, value_own
     )
-    gq_prev = passed_along(gq_next, "seq", 1)
+    back = jnp.concatenate(
+        [
+            gq_next,
+            attended_next.astype(jnp.float32),
+            highest_next.reshape(-1, HD),
+            totals_next.reshape(-1, HD),
+            delta_next.reshape(-1, HD),
+        ]
+    )
+    back = passed_along(back, "seq", 1)
+    step = half // HD
+    got = [back[2 * half + i * step : 2 * half + (i + 1) * step].reshape(half) for i in range(3)]
+    highest = jnp.concatenate([jnp.where(seen, got[0], peak_own[:half]), peak_own[half:]])
+    totals = jnp.concatenate([jnp.where(seen, got[1], totals[:half]), totals[half:]])
+    row_delta = jnp.concatenate([jnp.where(seen, got[2], row_delta[:half]), row_delta[half:]])
+    attended = jnp.concatenate(
+        [
+            jnp.where(seen[:, None], back[half : 2 * half].astype(jnp.bfloat16), attended[:half]),
+            attended[half:],
+        ]
+    )
+
+    weights_own = live_rows[:, None] * jnp.exp(score_own - highest[:, None]) / totals[:, None]
+    gq_own, gk_own, gv_own = finish_backward(
+        weights_own, cotangent, row_delta, queries, key_own, value_own
+    )
     grad_query = (
-        gq_own + jnp.concatenate([gq_prev, jnp.zeros((rest, HD), jnp.float32)])
+        gq_own + jnp.concatenate([back[:half], jnp.zeros((rest, HD), jnp.float32)])
     ).astype(jnp.bfloat16)
 
     parts = jnp.stack(

time: 87.8 us -> 97.8 us (1.11)
  the two profiles are of different devices: /device:TPU:402 before, /device:TPU:386 now
where the time goes in v10:
time: 97.8 us; the launch traced here: 97.1 us
  waiting for transfers between devices  41.2 us (42%)
  starting transfers between devices  30.8 us (31%)
  local copies, waits for them, and re-layouts  9.59 us (10%)
  other arithmetic  7.34 us (8%)
  matrix products  6.94 us (7%)
  between operations  1.13 us (1%)
    all_to_all x1, waiting for transfers between devices, per_device(): lax.all_to_all(summed, ('y', 'xh'), split_axis=0, concat_axis=0, tiled=True)  15.7 us
    all_to_all x1, waiting for transfers between devices, per_device(): lax.all_to_all(own_kv, ('y', 'xh'), split_axis=0, concat_axis=0, tiled=True)  14.6 us
    all_to_all x1, starting transfers between devices, per_device(): lax.all_to_all(own_kv, ('y', 'xh'), split_axis=0, concat_axis=0, tiled=True)  12 us
    ppermute x3, starting transfers between devices, passed_along(): return lax.ppermute(value, axis, pairs)  10.1 us
    ppermute x3, waiting for transfers between devices, passed_along(): return lax.ppermute(value, axis, pairs)  8.58 us
    all_to_all x1, starting transfers between devices, per_device(): lax.all_to_all(summed, ('y', 'xh'), split_axis=0, concat_axis=0, tiled=True)  4.82 us
    unnamed x43, local copies, waits for them, and re-layouts  4.02 us
    ppermute x2, starting transfers between devices, partner(): return lax.ppermute(value, 'c', [(0, 1), (1, 0)])  3.96 us
  transfers between devices with their start and end apart: 7, of which 6 were waited for; matrix products, arithmetic and copies ran while one was open for 4% of the time, Pallas kernels for 0%

profile of v10, /device:TPU:386, one launch (start us, length us, event | category | flops | bytes accessed | tf_op | source)
XLA Modules:
  0.0 97.1 jit_solution(2335381050793619557)
XLA Ops:
  0.7 0.9 maximum_bitcast_fusion
  1.6 1.0 broadcast_in_dim.97
  2.6 12.0 %all-to-all-start = ((bf16[32,2,3200]{2,1,0:T(2,128)(2,1)}), bf16[32,2,3200]{2,1,0:T(2,128)(2,1)S(1)}, u32[]{:S(2)}, u32[]{:S(2)}) async-start(bf16[32,2,3200]{2,1,0:T(2,128)(2,1)} %bitcast.9), calls=%async_computation | async-start | bytes 819200 | tf_op jit(solution)/shard_map/all_to_all | solution.py:77
  14.6 3.3 %collective-permute-start = (bf16[2,129,128]{2,1,0:T(8,128)(2,1)S(1)}, bf16[2,129,128]{2,1,0:T(8,128)(2,1)S(1)}, u32[]{:S(2)}, u32[]{:S(2)}) collective-permute-start(bf16[2,129,128]{2,1,0:T(8,128)(2,1)S(1)} %pad_maximum_fusion.2), channel_id=1, source_target_pairs={{64,0},{128,64},{192,128},{256,192},{320,256},{384,320},{448,384},... | collective-permute-start | bytes 198152 | tf_op jit(solution)/shard_map/ppermute | solution.py:16
  18.0 14.6 %all-to-all-done = bf16[32,2,3200]{2,1,0:T(2,128)(2,1)S(1)} async-done(((bf16[32,2,3200]{2,1,0:T(2,128)(2,1)}), bf16[32,2,3200]{2,1,0:T(2,128)(2,1)S(1)}, u32[]{:S(2)}, u32[]{:S(2)}) %all-to-all-start) | async-done | bytes 409632 | tf_op jit(solution)/shard_map/all_to_all | solution.py:77
  32.6 1.9 %collective-permute-start.1 = (bf16[2,32,3200]{2,0,1:T(2,128)(2,1)S(1)}, bf16[2,32,3200]{2,0,1:T(2,128)(2,1)S(1)}, u32[]{:S(2)}, u32[]{:S(2)}) collective-permute-start(bf16[2,32,3200]{2,0,1:T(2,128)(2,1)S(1)} %bitcast.152), channel_id=1, source_target_pairs={{0,1},{1,0},{2,3},{3,2},{4,5},{5,4},{6,7},{7,6},{8,9},{9,8},{10,11... | collective-permute-start | bytes 1228808 | tf_op jit(solution)/shard_map/ppermute | solution.py:20
  34.5 0.5 compare_reduce_fusion.1
  35.1 0.6 fusion.51
  35.7 0.6 collective-permute-done.1
  36.3 1.1 %pad_maximum_fusion = bf16[2,64,3200]{2,0,1:T(2,128)(2,1)S(1)} fusion(bf16[2,32,3200]{2,0,1:T(2,128)(2,1)S(1)} %collective-permute-done.1, bf16[2,32,3200]{2,0,1:T(2,128)(2,1)S(1)} %bitcast.153), kind=kLoop, calls=%fused_computation.28 | loop fusion | flops 409600 | bytes 1638400 | tf_op jit(solution)/shard_map/concatenate | solution.py:79
  37.4 0.4 reshape.230
  38.3 0.4 copy-done.4
  38.7 0.4 fusion.56
  39.1 0.3 fusion.15
  39.5 1.1 %multiply_reduce_fusion = (f32[256]{0:T(256)}, bf16[256,128]{1,0:T(8,128)(2,1)S(1)}, f32[256,128]{1,0:T(8,128)S(1)}) fusion(bf16[256,128]{1,0:T(8,128)(2,1)S(1)} %copy-done.5, f32[256]{0:T(256)S(1)} %bitcast.162, f32[256]{0:T(256)S(1)} %bitcast.158, bf16[1600,128]{1,0:T(8,128)(2,1)S(1)} %bitcast.146, f32[1600,256]{1,0:T(8,128)S(1)} %get-tuple-element.37, ...), kind=kOutput, calls=%fused_computation.52 | convolution fusion | flops 105905920 | bytes 2314240 | tf_op jit(solution)/shard_map/dot_general | solution.py:31
  40.7 3.0 %collective-permute-start.2 = (f32[130,128]{1,0:T(8,128)S(1)}, f32[130,128]{1,0:T(8,128)S(1)}, u32[]{:S(2)}, u32[]{:S(2)}) collective-permute-start(f32[130,128]{1,0:T(8,128)S(1)} %pad_maximum_fusion.3), channel_id=1, source_target_pairs={{64,0},{128,64},{192,128},{256,192},{320,256},{384,320},{448,384},... | collective-permute-start | bytes 199688 | tf_op jit(solution)/shard_map/ppermute | solution.py:16
  43.7 0.4 fusion.57
  44.1 0.2 fusion.23
  44.3 5.8 %collective-permute-done.2 = f32[130,128]{1,0:T(8,128)S(1)} collective-permute-done((f32[130,128]{1,0:T(8,128)S(1)}, f32[130,128]{1,0:T(8,128)S(1)}, u32[]{:S(2)}, u32[]{:S(2)}) %collective-permute-start.2) | collective-permute-done | bytes 66592 | tf_op jit(solution)/shard_map/ppermute | solution.py:16
  50.1 0.5 bitcast_select_fusion
  50.7 0.4 multiply_reduce_fusion.1
  51.1 0.4 fusion.6
  51.7 0.8 copy-done.2
  52.4 0.3 fusion.58
  52.8 2.5 %concatenate.36 = f32[259,128]{1,0:T(8,128)} concatenate(f32[128,128]{1,0:T(8,128)S(1)} %fusion.58, f32[128,128]{1,0:T(8,128)S(1)} %get-tuple-element.15, f32[1,128]{1,0:T(1,128)} %get-tuple-element.22, f32[1,128]{1,0:T(1,128)} %get-tuple-element.12, f32[1,128]{1,0:T(1,128)} %bitcast.163), dimensions={0} | concatenate | bytes 265216 | tf_op jit(solution)/shard_map/concatenate | solution.py:143
  55.3 3.7 %collective-permute-start.3 = (f32[259,128]{1,0:T(8,128)}, f32[259,128]{1,0:T(8,128)S(1)}, u32[]{:S(2)}, u32[]{:S(2)}) collective-permute-start(f32[259,128]{1,0:T(8,128)} %concatenate.36), channel_id=1, source_target_pairs={{0,64},{64,128},{128,192},{192,256},{256,320},{320,384},{384,448},... | collective-permute-start | bytes 397832 | tf_op jit(solution)/shard_map/ppermute | solution.py:16
  59.0 0.7 broadcast_select_fusion
  59.7 2.8 %collective-permute-done.3 = f32[259,128]{1,0:T(8,128)S(1)} collective-permute-done((f32[259,128]{1,0:T(8,128)}, f32[259,128]{1,0:T(8,128)S(1)}, u32[]{:S(2)}, u32[]{:S(2)}) %collective-permute-start.3) | collective-permute-done | bytes 132640 | tf_op jit(solution)/shard_map/ppermute | solution.py:16
  62.5 0.8 fusion.44
  63.3 1.3 %fusion.10 = f32[1600,128]{1,0:T(8,128)S(1)} fusion(bf16[256,128]{1,0:T(8,128)(2,1)} %param.8, f32[1600,256]{1,0:T(8,128)S(1)} %get-tuple-element.37, f32[256]{0:T(256)S(1)} %pad_maximum_fusion.6, f32[256]{0:T(256)} %bitcast.159, f32[256]{0:T(256)S(1)} %pad_maximum_fusion.5), kind=kOutput, calls=%fused_computation.16 | convolution fusion | flops 106905600 | bytes 2526208 | tf_op jit(solution)/shard_map/rk,rd->kd/dot_general | solution.py:48
  64.6 0.6 fusion.3
  65.3 0.4 fusion.14
  65.7 0.5 copy-done.8
  66.2 0.3 fusion.9
  66.5 0.7 copy-done.3
  67.2 0.2 fusion.13
  67.5 0.3 fusion.29
  67.8 2.1 %collective-permute-start.4 = (bf16[2,25,8,4,128]{4,3,2,1,0:T(4,128)(2,1)S(1)}, bf16[2,25,8,4,128]{4,3,2,1,0:T(4,128)(2,1)S(1)}, u32[]{:S(2)}, u32[]{:S(2)}) collective-permute-start(bf16[2,25,8,4,128]{4,3,2,1,0:T(4,128)(2,1)S(1)} %fusion.29), channel_id=1, source_target_pairs={{0,1},{1,0},{2,3},{3,2},{4,5},{5,4},{6,7},{7,6},{8,9},{9,8},{10,11... | collective-permute-start | bytes 1228808 | tf_op jit(solution)/shard_map/ppermute | solution.py:20
  69.8 1.7 %collective-permute-done.4 = bf16[2,25,8,4,128]{4,3,2,1,0:T(4,128)(2,1)S(1)} collective-permute-done((bf16[2,25,8,4,128]{4,3,2,1,0:T(4,128)(2,1)S(1)}, bf16[2,25,8,4,128]{4,3,2,1,0:T(4,128)(2,1)S(1)}, u32[]{:S(2)}, u32[]{:S(2)}) %collective-permute-start.4) | collective-permute-done | bytes 409632 | tf_op jit(solution)/shard_map/ppermute | solution.py:20
  71.6 0.3 fusion.26
  71.9 1.1 %copy.24 = bf16[8,4,2,25,128]{4,2,3,1,0:T(2,128)(2,1)} copy(bf16[8,4,2,25,128]{4,1,0,3,2:T(4,128)(2,1)S(1)} %fusion.26) | data formatting | bytes 819200 | tf_op jit(solution)/shard_map/transpose | solution.py:181
  73.0 4.8 %all-to-all-start.1 = ((bf16[32,2,25,128]{3,1,2,0:T(2,128)(2,1)}), bf16[32,2,25,128]{3,1,2,0:T(2,128)(2,1)S(1)}, u32[]{:S(2)}, u32[]{:S(2)}) async-start(bf16[32,2,25,128]{3,1,2,0:T(2,128)(2,1)} %bitcast.36), calls=%async_computation.1 | async-start | bytes 819200 | tf_op jit(solution)/shard_map/all_to_all | solution.py:183
  77.9 0.6 pad_maximum_fusion.4
  78.5 1.1 %fusion.33 = bf16[256,128]{1,0:T(8,128)(2,1)} fusion(f32[259,128]{1,0:T(8,128)S(1)} %collective-permute-done.3, pred[256]{0:T(512)(128)(4,1)S(1)} %copy-done.15, bf16[1600,256]{1,0:T(8,128)(2,1)S(1)} %copy-done.1, bf16[1600,128]{1,0:T(8,128)(2,1)S(1)} %bitcast.144), kind=kOutput, calls=%fused_computation.50 | convolution fusion | flops 104955904 | bytes 1425664 | tf_op jit(solution)/shard_map/dot_general | solution.py:44
  79.6 15.7 %all-to-all-done.1 = bf16[32,2,25,128]{3,1,2,0:T(2,128)(2,1)S(1)} async-done(((bf16[32,2,25,128]{3,1,2,0:T(2,128)(2,1)}), bf16[32,2,25,128]{3,1,2,0:T(2,128)(2,1)S(1)}, u32[]{:S(2)}, u32[]{:S(2)}) %all-to-all-start.1) | async-done | bytes 409632 | tf_op jit(solution)/shard_map/all_to_all | solution.py:183
  95.4 0.4 bitcast_reduce_fusion
  95.8 0.6 copy.26
  96.4 0.6 copy.27
  (62 shorter events, 1.1 us)
Async XLA Ops:
  0.6 13.9 %copy-start.9 = (s32[256,2]{0,1:T(2,128)S(1)}, s32[256,2]{0,1:T(2,128)}, u32[]{:S(2)}) copy-start(s32[256,2]{0,1:T(2,128)} %param.9) | copy-start | bytes 6148
  0.6 13.9 %slice-start = ((bf16[256,128]{1,0:T(8,128)(2,1)}), bf16[128,128]{1,0:T(8,128)(2,1)S(1)}, s32[]{:S(2)}) async-start(bf16[256,128]{1,0:T(8,128)(2,1)} %param.5), calls=%async_computation.2 | async-start | bytes 65536 | tf_op jit(solution)/shard_map/slice | solution.py:64
  0.7 13.9 %slice-start.1 = ((bf16[256,128]{1,0:T(8,128)(2,1)}), bf16[128,128]{1,0:T(8,128)(2,1)S(1)}, s32[]{:S(2)}) async-start(bf16[256,128]{1,0:T(8,128)(2,1)} %param.8), calls=%async_computation.3 | async-start | bytes 65536 | tf_op jit(solution)/shard_map/slice | solution.py:65
  2.6 30.1 %all-to-all-start = ((bf16[32,2,3200]{2,1,0:T(2,128)(2,1)}), bf16[32,2,3200]{2,1,0:T(2,128)(2,1)S(1)}, u32[]{:S(2)}, u32[]{:S(2)}) async-start(bf16[32,2,3200]{2,1,0:T(2,128)(2,1)} %bitcast.9), calls=%async_computation | async-start | bytes 819200 | tf_op jit(solution)/shard_map/all_to_all | solution.py:77
  14.6 20.4 %collective-permute-start = (bf16[2,129,128]{2,1,0:T(8,128)(2,1)S(1)}, bf16[2,129,128]{2,1,0:T(8,128)(2,1)S(1)}, u32[]{:S(2)}, u32[]{:S(2)}) collective-permute-start(bf16[2,129,128]{2,1,0:T(8,128)(2,1)S(1)} %pad_maximum_fusion.2), channel_id=1, source_target_pairs={{64,0},{128,64},{192,128},{256,192},{320,256},{384,320},{448,384},... | collective-permute-start | bytes 198152 | tf_op jit(solution)/shard_map/ppermute | solution.py:16
  32.6 3.6 %collective-permute-start.1 = (bf16[2,32,3200]{2,0,1:T(2,128)(2,1)S(1)}, bf16[2,32,3200]{2,0,1:T(2,128)(2,1)S(1)}, u32[]{:S(2)}, u32[]{:S(2)}) collective-permute-start(bf16[2,32,3200]{2,0,1:T(2,128)(2,1)S(1)} %bitcast.152), channel_id=1, source_target_pairs={{0,1},{1,0},{2,3},{3,2},{4,5},{5,4},{6,7},{7,6},{8,9},{9,8},{10,11... | collective-permute-start | bytes 1228808 | tf_op jit(solution)/shard_map/ppermute | solution.py:20
  35.1 4.3 %copy-start.10 = (f32[256,1]{0,1:T(1,128)}, f32[256,1]{0,1:T(1,128)S(1)}, u32[]{:S(2)}) copy-start(f32[256,1]{0,1:T(1,128)S(1)} %get-tuple-element.9) | copy-start | bytes 3076
  35.1 16.0 %copy-start.7 = (bf16[2,129,128]{2,1,0:T(8,128)(2,1)}, bf16[2,129,128]{2,1,0:T(8,128)(2,1)S(1)}, u32[]{:S(2)}) copy-start(bf16[2,129,128]{2,1,0:T(8,128)(2,1)S(1)} %collective-permute-done) | copy-start | bytes 198148
  37.8 0.8 copy-start.4
  38.7 0.8 copy-start.5
  40.6 10.0 %copy-start.16 = (pred[128]{0:T(512)(128)(4,1)S(1)}, pred[128]{0:T(512)(128)(4,1)}, u32[]{:S(2)}) copy-start(pred[128]{0:T(512)(128)(4,1)} %fusion.51) | copy-start | bytes 388
  40.7 9.4 %collective-permute-start.2 = (f32[130,128]{1,0:T(8,128)S(1)}, f32[130,128]{1,0:T(8,128)S(1)}, u32[]{:S(2)}, u32[]{:S(2)}) collective-permute-start(f32[130,128]{1,0:T(8,128)S(1)} %pad_maximum_fusion.3), channel_id=1, source_target_pairs={{64,0},{128,64},{192,128},{256,192},{320,256},{384,320},{448,384},... | collective-permute-start | bytes 199688 | tf_op jit(solution)/shard_map/ppermute | solution.py:16
  50.7 0.9 copy-start.13
  50.7 0.9 copy-start.18
  51.1 0.6 copy-start.12
  51.7 0.8 copy-start.2
  55.3 7.2 %collective-permute-start.3 = (f32[259,128]{1,0:T(8,128)}, f32[259,128]{1,0:T(8,128)S(1)}, u32[]{:S(2)}, u32[]{:S(2)}) collective-permute-start(f32[259,128]{1,0:T(8,128)} %concatenate.36), channel_id=1, source_target_pairs={{0,64},{64,128},{128,192},{192,256},{256,320},{320,384},{384,448},... | collective-permute-start | bytes 397832 | tf_op jit(solution)/shard_map/ppermute | solution.py:16
  63.3 1.4 %copy-start.6 = (bf16[256,128]{1,0:T(8,128)(2,1)S(1)}, bf16[256,128]{1,0:T(8,128)(2,1)}, u32[]{:S(2)}) copy-start(bf16[256,128]{1,0:T(8,128)(2,1)} %param.8) | copy-start | bytes 196612
  63.3 1.4 %copy-start.11 = (f32[256,1]{0,1:T(1,128)S(1)}, f32[256,1]{0,1:T(1,128)}, u32[]{:S(2)}) copy-start(f32[256,1]{0,1:T(1,128)} %copy-done.10) | copy-start | bytes 3076
  65.2 1.3 %copy-start = (bf16[1600,256]{1,0:T(8,128)(2,1)}, bf16[1600,256]{1,0:T(8,128)(2,1)S(1)}, u32[]{:S(2)}) copy-start(bf16[1600,256]{1,0:T(8,128)(2,1)S(1)} %fusion.3) | copy-start | bytes 2457604
  65.2 1.0 copy-start.8
  65.3 0.9 copy-start.14
  65.3 0.9 copy-start.17
  65.3 0.9 copy-start.19
  66.2 1.0 %copy-start.3 = (bf16[128,1600]{0,1:T(8,128)(2,1)S(1)}, bf16[128,1600]{0,1:T(8,128)(2,1)}, u32[]{:S(2)}) copy-start(bf16[128,1600]{0,1:T(8,128)(2,1)} %copy-done.2) | copy-start | bytes 1228804
  67.8 10.8 %copy-start.1 = (bf16[1600,256]{1,0:T(8,128)(2,1)S(1)}, bf16[1600,256]{1,0:T(8,128)(2,1)}, u32[]{:S(2)}) copy-start(bf16[1600,256]{1,0:T(8,128)(2,1)} %copy-done) | copy-start | bytes 2457604
  67.8 10.8 %copy-start.15 = (pred[256]{0:T(512)(128)(4,1)S(1)}, pred[256]{0:T(512)(128)(4,1)}, u32[]{:S(2)}) copy-start(pred[256]{0:T(512)(128)(4,1)} %constant.2.clone.1) | copy-start | bytes 772
  67.8 3.8 %collective-permute-start.4 = (bf16[2,25,8,4,128]{4,3,2,1,0:T(4,128)(2,1)S(1)}, bf16[2,25,8,4,128]{4,3,2,1,0:T(4,128)(2,1)S(1)}, u32[]{:S(2)}, u32[]{:S(2)}) collective-permute-start(bf16[2,25,8,4,128]{4,3,2,1,0:T(4,128)(2,1)S(1)} %fusion.29), channel_id=1, source_target_pairs={{0,1},{1,0},{2,3},{3,2},{4,5},{5,4},{6,7},{7,6},{8,9},{9,8},{10,11... | collective-permute-start | bytes 1228808 | tf_op jit(solution)/shard_map/ppermute | solution.py:20
  73.0 22.4 %all-to-all-start.1 = ((bf16[32,2,25,128]{3,1,2,0:T(2,128)(2,1)}), bf16[32,2,25,128]{3,1,2,0:T(2,128)(2,1)S(1)}, u32[]{:S(2)}, u32[]{:S(2)}) async-start(bf16[32,2,25,128]{3,1,2,0:T(2,128)(2,1)} %bitcast.36), calls=%async_computation.1 | async-start | bytes 819200 | tf_op jit(solution)/shard_map/all_to_all | solution.py:183

commit v11 on v8

--- a/solution.py
+++ b/solution.py
@@ -20,10 +20,18 @@
     return lax.ppermute(value, "c", [(0, 1), (1, 0)])
 
 
-def block_forward(query_rows, key_rows, value_rows, keep_mask):
-    scores = jnp.einsum(
-        "rd,kd->rk", query_rows, key_rows, preferred_element_type=jnp.float32
+def scores_of(query_rows, key_halves):
+    return jnp.concatenate(
+        [
+            jnp.einsum("rd,kd->rk", query_rows, k, preferred_element_type=jnp.float32)
+            for k in key_halves
+        ],
+        axis=1,
     ) * HD ** (-0.5)
+
+
+def block_forward(query_rows, key_halves, value_rows, keep_mask):
+    scores = scores_of(query_rows, key_halves)
     scores = jnp.where(keep_mask[:, None] > 0, scores, NEGATIVE)
     highest = jnp.max(scores, axis=1)
     powered = jnp.exp(scores - highest[:, None])
@@ -76,21 +84,24 @@
     own_kv = jnp.broadcast_to(own_kv, (KVH, far, 2, rows * HD)).reshape(-1, 2, rows * HD)
     across = lax.all_to_all(own_kv, ("y", "xh"), split_axis=0, concat_axis=0, tiled=True)
     across = jnp.transpose(across, (1, 0, 2))
-    gathered = jnp.concatenate([across, partner(across)], axis=1)
-    gathered = jnp.transpose(gathered.reshape(2, blocks, rows, HD), (0, 2, 1, 3))
-    gathered = gathered.reshape(2, rows * blocks, HD)
-    key_own, value_own = gathered[0], gathered[1]
+    def rows_of(half_blocks):
+        half_blocks = half_blocks.reshape(2, blocks // 2, rows, HD)
+        return jnp.transpose(half_blocks, (0, 2, 1, 3)).reshape(2, rows * blocks // 2, HD)
+
+    mine = rows_of(across)
+    other = rows_of(partner(across))
+    key_halves = (mine[0], other[0])
+    key_own = jnp.concatenate(key_halves)
+    value_own = jnp.concatenate([mine[1], other[1]])
 
     keep_own = mask[:, 0]
     keep_prev = mask[:, 1]
     live_rows = (keep_own + keep_prev > 0).astype(jnp.float32)
     score_own, peak_own, total_own, partial_own = block_forward(
-        queries, key_own, value_own, keep_own
-    )
-
-    score_next = jnp.einsum(
-        "rd,kd->rk", query_next, key_own, preferred_element_type=jnp.float32
-    ) * HD ** (-0.5)
+        queries, key_halves, value_own, keep_own
+    )
+
+    score_next = scores_of(query_next, key_halves)
     peak_next = jnp.max(score_next, axis=1)
     total_next = jnp.sum(jnp.exp(score_next - peak_next[:, None]), axis=1)
     partial_next = jnp.dot(
@@ -178,8 +189,8 @@
             gv_own.astype(jnp.float32) + gv_next.astype(jnp.float32),
         ]
     ).astype(jnp.bfloat16)
-    parts = parts.reshape(2, rows, 2, groups, far, HD)
-    summed = parts[:, :, 0].astype(jnp.float32) + partner(parts[:, :, 1]).astype(jnp.float32)
+    parts = parts.reshape(2, 2, rows, groups, far, HD)
+    summed = parts[:, 0].astype(jnp.float32) + partner(parts[:, 1]).astype(jnp.float32)
     summed = jnp.transpose(summed.astype(jnp.bfloat16), (2, 3, 0, 1, 4))
     summed = summed.reshape(groups * far, 2, rows, HD)
     summed = lax.all_to_all(summed, ("y", "xh"), split_axis=0, concat_axis=0, tiled=True)

time: 87.8 us -> 88.3 us (level)
  the two profiles are of different devices: /device:TPU:402 before, /device:TPU:386 now
where the time goes in v11:
time: 88.3 us; the launch traced here: 87.8 us
  starting transfers between devices  37.4 us (42%)
  waiting for transfers between devices  34.8 us (39%)
  matrix products  6.38 us (7%)
  local copies, waits for them, and re-layouts  4.8 us (5%)
  other arithmetic  3.36 us (4%)
  between operations  1.02 us (1%)
    ppermute x4, waiting for transfers between devices, passed_along(): return lax.ppermute(value, axis, pairs)  23 us
    ppermute x4, starting transfers between devices, passed_along(): return lax.ppermute(value, axis, pairs)  15.6 us
    all_to_all x1, starting transfers between devices, per_device(): lax.all_to_all(own_kv, ('y', 'xh'), split_axis=0, concat_axis=0, tiled=True)  12 us
    all_to_all x1, waiting for transfers between devices, per_device(): lax.all_to_all(summed, ('y', 'xh'), split_axis=0, concat_axis=0, tiled=True)  7.09 us
    all_to_all x1, starting transfers between devices, per_device(): lax.all_to_all(summed, ('y', 'xh'), split_axis=0, concat_axis=0, tiled=True)  6.06 us
    ppermute x2, starting transfers between devices, partner(): return lax.ppermute(value, 'c', [(0, 1), (1, 0)])  3.83 us
    all_to_all x1, waiting for transfers between devices, per_device(): lax.all_to_all(own_kv, ('y', 'xh'), split_axis=0, concat_axis=0, tiled=True)  2.64 us
    ppermute x2, waiting for transfers between devices, partner(): return lax.ppermute(value, 'c', [(0, 1), (1, 0)])  2.01 us
  transfers between devices with their start and end apart: 8, of which 8 were waited for; matrix products, arithmetic and copies ran while one was open for 5% of the time, Pallas kernels for 0%

profile of v11, /device:TPU:386, one launch (start us, length us, event | category | flops | bytes accessed | tf_op | source)
XLA Modules:
  0.0 87.8 jit_solution(8025290279729704352)
XLA Ops:
  0.6 0.8 maximum_bitcast_fusion
  1.6 1.0 %broadcast_in_dim.90 = bf16[8,4,2,3200]{3,2,1,0:T(2,128)(2,1)} broadcast(bf16[8,2,3200]{2,1,0:T(2,128)(2,1)S(1)} %copy.24), dimensions={0,2,3} | broadcast | bytes 512000 | tf_op jit(solution)/shard_map/broadcast_in_dim | solution.py:84
  2.6 12.0 %all-to-all-start = ((bf16[32,2,3200]{2,1,0:T(2,128)(2,1)}), bf16[32,2,3200]{2,1,0:T(2,128)(2,1)S(1)}, u32[]{:S(2)}, u32[]{:S(2)}) async-start(bf16[32,2,3200]{2,1,0:T(2,128)(2,1)} %bitcast.3), calls=%async_computation | async-start | bytes 819200 | tf_op jit(solution)/shard_map/all_to_all | solution.py:85
  14.6 3.3 %collective-permute-start.1 = (bf16[2,129,128]{2,1,0:T(8,128)(2,1)S(1)}, bf16[2,129,128]{2,1,0:T(8,128)(2,1)S(1)}, u32[]{:S(2)}, u32[]{:S(2)}) collective-permute-start(bf16[2,129,128]{2,1,0:T(8,128)(2,1)S(1)} %pad_maximum_fusion.5), channel_id=1, source_target_pairs={{64,0},{128,64},{192,128},{256,192},{320,256},{384,320},{448,384},... | collective-permute-start | bytes 198152 | tf_op jit(solution)/shard_map/ppermute | solution.py:16
  18.0 12.0 %collective-permute-done.1 = bf16[2,129,128]{2,1,0:T(8,128)(2,1)S(1)} collective-permute-done((bf16[2,129,128]{2,1,0:T(8,128)(2,1)S(1)}, bf16[2,129,128]{2,1,0:T(8,128)(2,1)S(1)}, u32[]{:S(2)}, u32[]{:S(2)}) %collective-permute-start.1) | collective-permute-done | bytes 66080 | tf_op jit(solution)/shard_map/ppermute | solution.py:16
  30.0 2.6 %all-to-all-done = bf16[32,2,3200]{2,1,0:T(2,128)(2,1)S(1)} async-done(((bf16[32,2,3200]{2,1,0:T(2,128)(2,1)}), bf16[32,2,3200]{2,1,0:T(2,128)(2,1)S(1)}, u32[]{:S(2)}, u32[]{:S(2)}) %all-to-all-start) | async-done | bytes 409632 | tf_op jit(solution)/shard_map/all_to_all | solution.py:85
  32.6 1.9 %collective-permute-start = (bf16[2,32,3200]{2,0,1:T(2,128)(2,1)S(1)}, bf16[2,32,3200]{2,0,1:T(2,128)(2,1)S(1)}, u32[]{:S(2)}, u32[]{:S(2)}) collective-permute-start(bf16[2,32,3200]{2,0,1:T(2,128)(2,1)S(1)} %bitcast.137), channel_id=1, source_target_pairs={{0,1},{1,0},{2,3},{3,2},{4,5},{5,4},{6,7},{7,6},{8,9},{9,8},{10,11... | collective-permute-start | bytes 1228808 | tf_op jit(solution)/shard_map/ppermute | solution.py:20
  34.6 0.2 reshape.165
  34.9 0.1 copy.26
  35.0 0.2 fusion.41
  35.3 0.4 copy-done
  35.7 0.3 convolution_bitcast_fusion.1
  36.0 0.3 collective-permute-done
  36.3 0.2 reshape.166
  36.6 0.3 convolution_bitcast_fusion
  36.9 0.2 fusion.40
  37.1 0.2 fusion.35
  37.3 0.2 fusion.23
  37.7 0.3 fusion.25
  38.0 7.0 %collective-permute-start.2 = (f32[130,128]{1,0:T(8,128)S(1)}, f32[130,128]{1,0:T(8,128)S(1)}, u32[]{:S(2)}, u32[]{:S(2)}) collective-permute-start(f32[130,128]{1,0:T(8,128)S(1)} %pad_maximum_fusion.6), channel_id=1, source_target_pairs={{0,64},{64,128},{128,192},{192,256},{256,320},{320,384},{384,448},... | collective-permute-start | bytes 199688 | tf_op jit(solution)/shard_map/ppermute | solution.py:16
  45.0 0.3 fusion.56
  45.3 0.4 fusion.16
  45.7 1.2 %collective-permute-done.2 = f32[130,128]{1,0:T(8,128)S(1)} collective-permute-done((f32[130,128]{1,0:T(8,128)S(1)}, f32[130,128]{1,0:T(8,128)S(1)}, u32[]{:S(2)}, u32[]{:S(2)}) %collective-permute-start.2) | collective-permute-done | bytes 66592 | tf_op jit(solution)/shard_map/ppermute | solution.py:16
  46.9 0.1 slice_select_fusion
  47.1 1.2 %multiply_reduce_fusion = (f32[256]{0:T(256)S(1)}, bf16[256,128]{1,0:T(8,128)(2,1)}, f32[256,128]{1,0:T(8,128)S(1)}) fusion(bf16[256,128]{1,0:T(8,128)(2,1)S(1)} %copy-done.1, f32[256]{0:T(256)S(1)} %get-tuple-element.15, f32[128,128]{1,0:T(8,128)S(1)} %slice_select_fusion, f32[256]{0:T(256)S(1)} %get-tuple-element.17, f32[256]{0:T(256)S(1)} %get-tuple-element.16, ...), kind=kOutput, calls=%fused_computation.57 | convolution fusion | flops 108052224 | bytes 2382080 | tf_op jit(solution)/shard_map/dot_general | solution.py:39
  48.3 1.9 %collective-permute-start.3 = (f32[130,128]{1,0:T(8,128)S(1)}, f32[130,128]{1,0:T(8,128)S(1)}, u32[]{:S(2)}, u32[]{:S(2)}) collective-permute-start(f32[130,128]{1,0:T(8,128)S(1)} %pad_maximum_fusion.7), channel_id=1, source_target_pairs={{64,0},{128,64},{192,128},{256,192},{320,256},{384,320},{448,384},... | collective-permute-start | bytes 199688 | tf_op jit(solution)/shard_map/ppermute | solution.py:16
  50.2 0.5 fusion.10
  50.8 0.7 fusion.3
  51.4 0.4 fusion.14
  51.8 5.1 %collective-permute-done.3 = f32[130,128]{1,0:T(8,128)S(1)} collective-permute-done((f32[130,128]{1,0:T(8,128)S(1)}, f32[130,128]{1,0:T(8,128)S(1)}, u32[]{:S(2)}, u32[]{:S(2)}) %collective-permute-start.3) | collective-permute-done | bytes 66592 | tf_op jit(solution)/shard_map/ppermute | solution.py:16
  57.0 0.2 multiply_reduce_fusion.1
  57.2 0.4 fusion.6
  57.6 0.3 fusion.9
  57.9 0.2 fusion.13
  58.2 0.3 fusion.30
  58.4 1.9 %collective-permute-start.5 = (bf16[2,25,8,4,128]{4,3,2,1,0:T(4,128)(2,1)S(1)}, bf16[2,25,8,4,128]{4,3,2,1,0:T(4,128)(2,1)S(1)}, u32[]{:S(2)}, u32[]{:S(2)}) collective-permute-start(bf16[2,25,8,4,128]{4,3,2,1,0:T(4,128)(2,1)S(1)} %fusion.30), channel_id=1, source_target_pairs={{0,1},{1,0},{2,3},{3,2},{4,5},{5,4},{6,7},{7,6},{8,9},{9,8},{10,11... | collective-permute-start | bytes 1228808 | tf_op jit(solution)/shard_map/ppermute | solution.py:20
  60.4 1.7 %collective-permute-done.5 = bf16[2,25,8,4,128]{4,3,2,1,0:T(4,128)(2,1)S(1)} collective-permute-done((bf16[2,25,8,4,128]{4,3,2,1,0:T(4,128)(2,1)S(1)}, bf16[2,25,8,4,128]{4,3,2,1,0:T(4,128)(2,1)S(1)}, u32[]{:S(2)}, u32[]{:S(2)}) %collective-permute-start.5) | collective-permute-done | bytes 409632 | tf_op jit(solution)/shard_map/ppermute | solution.py:20
  62.1 0.3 fusion.27
  62.4 1.1 %copy.32 = bf16[8,4,2,25,128]{4,2,3,1,0:T(2,128)(2,1)} copy(bf16[8,4,2,25,128]{4,1,0,3,2:T(4,128)(2,1)S(1)} %fusion.27) | data formatting | bytes 819200 | tf_op jit(solution)/shard_map/transpose | solution.py:194
  63.4 6.1 %all-to-all-start.1 = ((bf16[32,2,25,128]{3,1,2,0:T(2,128)(2,1)}), bf16[32,2,25,128]{3,1,2,0:T(2,128)(2,1)S(1)}, u32[]{:S(2)}, u32[]{:S(2)}) async-start(bf16[32,2,25,128]{3,1,2,0:T(2,128)(2,1)} %bitcast.36), calls=%async_computation.1 | async-start | bytes 819200 | tf_op jit(solution)/shard_map/all_to_all | solution.py:196
  69.5 0.3 fusion.33
  69.8 3.3 %collective-permute-start.4 = (f32[128,128]{1,0:T(8,128)S(1)}, f32[128,128]{1,0:T(8,128)S(1)}, u32[]{:S(2)}, u32[]{:S(2)}) collective-permute-start(f32[128,128]{1,0:T(8,128)S(1)} %fusion.33), channel_id=1, source_target_pairs={{0,64},{64,128},{128,192},{192,256},{256,320},{320,384},{384,448},... | collective-permute-start | bytes 196616 | tf_op jit(solution)/shard_map/ppermute | solution.py:16
  73.1 4.7 %collective-permute-done.4 = f32[128,128]{1,0:T(8,128)S(1)} collective-permute-done((f32[128,128]{1,0:T(8,128)S(1)}, f32[128,128]{1,0:T(8,128)S(1)}, u32[]{:S(2)}, u32[]{:S(2)}) %collective-permute-start.4) | collective-permute-done | bytes 65568 | tf_op jit(solution)/shard_map/ppermute | solution.py:16
  77.8 1.1 %add_convert_fusion = bf16[256,128]{1,0:T(8,128)(2,1)} fusion(f32[128,128]{1,0:T(8,128)S(1)} %collective-permute-done.4, bf16[256,1600]{0,1:T(8,128)(2,1)S(1)} %fusion.3, bf16[800,128]{1,0:T(8,128)(2,1)S(1)} %bitcast.136, bf16[800,128]{1,0:T(8,128)(2,1)S(1)} %bitcast.132), kind=kOutput, calls=%fused_computation.56 | convolution fusion | flops 105742336 | bytes 1359872 | tf_op jit(solution)/shard_map/dot_general | solution.py:52
  78.9 7.1 %all-to-all-done.1 = bf16[32,2,25,128]{3,1,2,0:T(2,128)(2,1)S(1)} async-done(((bf16[32,2,25,128]{3,1,2,0:T(2,128)(2,1)}), bf16[32,2,25,128]{3,1,2,0:T(2,128)(2,1)S(1)}, u32[]{:S(2)}, u32[]{:S(2)}) %all-to-all-start.1) | async-done | bytes 409632 | tf_op jit(solution)/shard_map/all_to_all | solution.py:196
  86.0 0.4 bitcast_reduce_fusion
  86.5 0.6 copy.34
  87.1 0.6 copy.35
  (33 shorter events, 0.7 us)
Async XLA Ops:
  1.5 13.1 %copy-start.2 = (s32[256,2]{0,1:T(2,128)S(1)}, s32[256,2]{0,1:T(2,128)}, u32[]{:S(2)}) copy-start(s32[256,2]{0,1:T(2,128)} %param.9) | copy-start | bytes 6148
  1.5 13.1 %slice-start = ((bf16[256,128]{1,0:T(8,128)(2,1)}), bf16[128,128]{1,0:T(8,128)(2,1)S(1)}, s32[]{:S(2)}) async-start(bf16[256,128]{1,0:T(8,128)(2,1)} %param.5), calls=%async_computation.2 | async-start | bytes 65536 | tf_op jit(solution)/shard_map/slice | solution.py:72
  1.5 13.1 %slice-start.1 = ((bf16[256,128]{1,0:T(8,128)(2,1)}), bf16[128,128]{1,0:T(8,128)(2,1)S(1)}, s32[]{:S(2)}) async-start(bf16[256,128]{1,0:T(8,128)(2,1)} %param.8), calls=%async_computation.3 | async-start | bytes 65536 | tf_op jit(solution)/shard_map/slice | solution.py:73
  2.6 30.1 %all-to-all-start = ((bf16[32,2,3200]{2,1,0:T(2,128)(2,1)}), bf16[32,2,3200]{2,1,0:T(2,128)(2,1)S(1)}, u32[]{:S(2)}, u32[]{:S(2)}) async-start(bf16[32,2,3200]{2,1,0:T(2,128)(2,1)} %bitcast.3), calls=%async_computation | async-start | bytes 819200 | tf_op jit(solution)/shard_map/all_to_all | solution.py:85
  14.6 15.3 %collective-permute-start.1 = (bf16[2,129,128]{2,1,0:T(8,128)(2,1)S(1)}, bf16[2,129,128]{2,1,0:T(8,128)(2,1)S(1)}, u32[]{:S(2)}, u32[]{:S(2)}) collective-permute-start(bf16[2,129,128]{2,1,0:T(8,128)(2,1)S(1)} %pad_maximum_fusion.5), channel_id=1, source_target_pairs={{64,0},{128,64},{192,128},{256,192},{320,256},{384,320},{448,384},... | collective-permute-start | bytes 198152 | tf_op jit(solution)/shard_map/ppermute | solution.py:16
  32.6 3.6 %collective-permute-start = (bf16[2,32,3200]{2,0,1:T(2,128)(2,1)S(1)}, bf16[2,32,3200]{2,0,1:T(2,128)(2,1)S(1)}, u32[]{:S(2)}, u32[]{:S(2)}) collective-permute-start(bf16[2,32,3200]{2,0,1:T(2,128)(2,1)S(1)} %bitcast.137), channel_id=1, source_target_pairs={{0,1},{1,0},{2,3},{3,2},{4,5},{5,4},{6,7},{7,6},{8,9},{9,8},{10,11... | collective-permute-start | bytes 1228808 | tf_op jit(solution)/shard_map/ppermute | solution.py:20
  34.8 0.8 copy-start
  38.0 8.9 %collective-permute-start.2 = (f32[130,128]{1,0:T(8,128)S(1)}, f32[130,128]{1,0:T(8,128)S(1)}, u32[]{:S(2)}, u32[]{:S(2)}) collective-permute-start(f32[130,128]{1,0:T(8,128)S(1)} %pad_maximum_fusion.6), channel_id=1, source_target_pairs={{0,64},{64,128},{128,192},{192,256},{256,320},{320,384},{384,448},... | collective-permute-start | bytes 199688 | tf_op jit(solution)/shard_map/ppermute | solution.py:16
  45.3 1.8 %copy-start.1 = (bf16[256,128]{1,0:T(8,128)(2,1)S(1)}, bf16[256,128]{1,0:T(8,128)(2,1)}, u32[]{:S(2)}) copy-start(bf16[256,128]{1,0:T(8,128)(2,1)} %param.8) | copy-start | bytes 196612
  48.3 8.7 %collective-permute-start.3 = (f32[130,128]{1,0:T(8,128)S(1)}, f32[130,128]{1,0:T(8,128)S(1)}, u32[]{:S(2)}, u32[]{:S(2)}) collective-permute-start(f32[130,128]{1,0:T(8,128)S(1)} %pad_maximum_fusion.7), channel_id=1, source_target_pairs={{64,0},{128,64},{192,128},{256,192},{320,256},{384,320},{448,384},... | collective-permute-start | bytes 199688 | tf_op jit(solution)/shard_map/ppermute | solution.py:16
  58.4 3.6 %collective-permute-start.5 = (bf16[2,25,8,4,128]{4,3,2,1,0:T(4,128)(2,1)S(1)}, bf16[2,25,8,4,128]{4,3,2,1,0:T(4,128)(2,1)S(1)}, u32[]{:S(2)}, u32[]{:S(2)}) collective-permute-start(bf16[2,25,8,4,128]{4,3,2,1,0:T(4,128)(2,1)S(1)} %fusion.30), channel_id=1, source_target_pairs={{0,1},{1,0},{2,3},{3,2},{4,5},{5,4},{6,7},{7,6},{8,9},{9,8},{10,11... | collective-permute-start | bytes 1228808 | tf_op jit(solution)/shard_map/ppermute | solution.py:20
  63.4 22.6 %all-to-all-start.1 = ((bf16[32,2,25,128]{3,1,2,0:T(2,128)(2,1)}), bf16[32,2,25,128]{3,1,2,0:T(2,128)(2,1)S(1)}, u32[]{:S(2)}, u32[]{:S(2)}) async-start(bf16[32,2,25,128]{3,1,2,0:T(2,128)(2,1)} %bitcast.36), calls=%async_computation.1 | async-start | bytes 819200 | tf_op jit(solution)/shard_map/all_to_all | solution.py:196
  69.8 8.0 %collective-permute-start.4 = (f32[128,128]{1,0:T(8,128)S(1)}, f32[128,128]{1,0:T(8,128)S(1)}, u32[]{:S(2)}, u32[]{:S(2)}) collective-permute-start(f32[128,128]{1,0:T(8,128)S(1)} %fusion.33), channel_id=1, source_target_pairs={{0,64},{64,128},{128,192},{192,256},{256,320},{320,384},{384,448},... | collective-permute-start | bytes 196616 | tf_op jit(solution)/shard_map/ppermute | solution.py:16

commit v12 on v8

--- a/solution.py
+++ b/solution.py
@@ -34,7 +34,9 @@
     return (scores, highest, totals, partial_value)
 
 
-def finish_backward(weights, grad_rows, row_delta, query_rows, key_rows, value_rows):
+def finish_backward(
+    weights, grad_rows, row_delta, query_rows, key_rows, value_rows, narrow=jnp.bfloat16
+):
     grad_weights = jnp.einsum(
         "rd,kd->rk", grad_rows, value_rows, preferred_element_type=jnp.float32
     )
@@ -44,10 +46,10 @@
     query_grad = jnp.dot(grad_scores, key_rows, preferred_element_type=jnp.float32)
     key_part = jnp.einsum(
         "rk,rd->kd", grad_scores, query_rows, preferred_element_type=jnp.float32
-    ).astype(jnp.bfloat16)
+    ).astype(narrow)
     value_part = jnp.einsum(
         "rk,rd->kd", weights.astype(jnp.bfloat16), grad_rows, preferred_element_type=jnp.float32
-    ).astype(jnp.bfloat16)
+    ).astype(narrow)
     return (query_grad, key_part, value_part)
 
 
@@ -116,16 +118,39 @@
         [jnp.where(seen[:, None], stats[:half], 0.0), jnp.zeros((rest, HD), jnp.float32)]
     )
 
-    highest = jnp.maximum(peak_own, peak_prev)
-    scale_own = jnp.exp(peak_own - highest)
-    scale_prev = jnp.exp(peak_prev - highest)
-    totals = scale_own * total_own + scale_prev * total_prev
-    attended = (
-        live_rows[:, None]
-        * (scale_own[:, None] * partial_own + scale_prev[:, None] * partial_prev)
+    highest = jnp.maximum(peak_own[:half], peak_prev[:half])
+    scale_own = jnp.exp(peak_own[:half] - highest)
+    scale_prev = jnp.exp(peak_prev[:half] - highest)
+    totals = scale_own * total_own[:half] + scale_prev * total_prev[:half]
+    attended_head = (
+        live_rows[:half, None]
+        * (scale_own[:, None] * partial_own[:half] + scale_prev[:, None] * partial_prev[:half])
         / totals[:, None]
     ).astype(jnp.bfloat16)
-    row_delta = jnp.sum(cotangent.astype(jnp.float32) * attended.astype(jnp.float32), axis=1)
+    delta_head = jnp.sum(
+        cotangent[:half].astype(jnp.float32) * attended_head.astype(jnp.float32), axis=1
+    )
+    attended_tail = (
+        live_rows[half:, None] * partial_own[half:] / total_own[half:, None]
+    ).astype(jnp.bfloat16)
+    delta_tail = jnp.sum(
+        cotangent[half:].astype(jnp.float32) * attended_tail.astype(jnp.float32), axis=1
+    )
+    weights_tail = (
+        live_rows[half:, None]
+        * jnp.exp(score_own[half:] - peak_own[half:, None])
+        / total_own[half:, None]
+    )
+    gq_tail, gk_tail, gv_tail = finish_backward(
+        weights_tail,
+        cotangent[half:],
+        delta_tail,
+        queries[half:],
+        key_own,
+        value_own,
+        jnp.float32,
+    )
+    attended = jnp.concatenate([attended_head, attended_tail])
 
     mine = jnp.concatenate(
         [partial_own[:half], peak_own[:half].reshape(-1, HD), total_own[:half].reshape(-1, HD)]
@@ -155,10 +180,21 @@
         grad_next.astype(jnp.float32) * attended_next.astype(jnp.float32), axis=1
     )
 
-    weights_own = live_rows[:, None] * jnp.exp(score_own - highest[:, None]) / totals[:, None]
-    gq_own, gk_own, gv_own = finish_backward(
-        weights_own, cotangent, row_delta, queries, key_own, value_own
-    )
+    weights_head = (
+        live_rows[:half, None] * jnp.exp(score_own[:half] - highest[:, None]) / totals[:, None]
+    )
+    gq_head, gk_head, gv_head = finish_backward(
+        weights_head,
+        cotangent[:half],
+        delta_head,
+        queries[:half],
+        key_own,
+        value_own,
+        jnp.float32,
+    )
+    gq_own = jnp.concatenate([gq_head, gq_tail])
+    gk_own = (gk_head + gk_tail).astype(jnp.bfloat16)
+    gv_own = (gv_head + gv_tail).astype(jnp.bfloat16)
     weights_next = jnp.where(
         seen_next[:, None],
         jnp.exp(score_next - highest_next[:, None]) / totals_next[:, None],

time: 87.8 us -> 86.8 us (0.989)
  waiting for transfers between devices: 35.9 us -> 34.1 us
  other arithmetic: 3.86 us -> 5.32 us
    ppermute x4, waiting for transfers between devices: 9.98 us -> 8.12 us  [passed_along(): return lax.ppermute(value, axis, pairs)]
  transfers between devices with their start and end apart: 8 -> 8, of which waited for: 7 -> 7; matrix products, arithmetic and copies ran while one was open for 4% -> 6% of each run, Pallas kernels for 0% -> 0%
where the time goes in v12:
time: 86.8 us; the launch traced here: 86.3 us
  starting transfers between devices  36.2 us (42%)
  waiting for transfers between devices  34.1 us (39%)
  other arithmetic  5.32 us (6%)
  matrix products  5.21 us (6%)
  local copies, waits for them, and re-layouts  4.38 us (5%)
  between operations  1.04 us (1%)
    ppermute x4, starting transfers between devices, passed_along(): return lax.ppermute(value, axis, pairs)  15.7 us
    all_to_all x1, waiting for transfers between devices, per_device(): lax.all_to_all(own_kv, ('y', 'xh'), split_axis=0, concat_axis=0, tiled=True)  15 us
    all_to_all x1, starting transfers between devices, per_device(): lax.all_to_all(own_kv, ('y', 'xh'), split_axis=0, concat_axis=0, tiled=True)  12.1 us
    ppermute x4, waiting for transfers between devices, passed_along(): return lax.ppermute(value, axis, pairs)  8.12 us
    all_to_all x1, waiting for transfers between devices, per_device(): lax.all_to_all(summed, ('y', 'xh'), split_axis=0, concat_axis=0, tiled=True)  7.63 us
    all_to_all x1, starting transfers between devices, per_device(): lax.all_to_all(summed, ('y', 'xh'), split_axis=0, concat_axis=0, tiled=True)  4.61 us
    ppermute x2, starting transfers between devices, partner(): return lax.ppermute(value, 'c', [(0, 1), (1, 0)])  3.83 us
    ppermute x2, waiting for transfers between devices, partner(): return lax.ppermute(value, 'c', [(0, 1), (1, 0)])  3.39 us
  transfers between devices with their start and end apart: 8, of which 7 were waited for; matrix products, arithmetic and copies ran while one was open for 6% of the time, Pallas kernels for 0%

profile of v12, /device:TPU:402, one launch (start us, length us, event | category | flops | bytes accessed | tf_op | source)
XLA Modules:
  0.0 86.3 jit_solution(12875216873207381072)
XLA Ops:
  0.7 0.9 maximum_bitcast_fusion
  1.6 1.0 %broadcast_in_dim.96 = bf16[8,4,2,3200]{3,2,1,0:T(2,128)(2,1)} broadcast(bf16[8,2,3200]{2,1,0:T(2,128)(2,1)S(1)} %copy.19), dimensions={0,2,3} | broadcast | bytes 512000 | tf_op jit(solution)/shard_map/broadcast_in_dim | solution.py:78
  2.6 12.1 %all-to-all-start = ((bf16[32,2,3200]{2,1,0:T(2,128)(2,1)}), bf16[32,2,3200]{2,1,0:T(2,128)(2,1)S(1)}, u32[]{:S(2)}, u32[]{:S(2)}) async-start(bf16[32,2,3200]{2,1,0:T(2,128)(2,1)} %bitcast.3), calls=%async_computation | async-start | bytes 819200 | tf_op jit(solution)/shard_map/all_to_all | solution.py:79
  14.8 3.3 %collective-permute-start.1 = (bf16[2,129,128]{2,1,0:T(8,128)(2,1)S(1)}, bf16[2,129,128]{2,1,0:T(8,128)(2,1)S(1)}, u32[]{:S(2)}, u32[]{:S(2)}) collective-permute-start(bf16[2,129,128]{2,1,0:T(8,128)(2,1)S(1)} %pad_maximum_fusion.2), channel_id=1, source_target_pairs={{64,0},{128,64},{192,128},{256,192},{320,256},{384,320},{448,384},... | collective-permute-start | bytes 198152 | tf_op jit(solution)/shard_map/ppermute | solution.py:16
  18.1 15.0 %all-to-all-done = bf16[32,2,3200]{2,1,0:T(2,128)(2,1)S(1)} async-done(((bf16[32,2,3200]{2,1,0:T(2,128)(2,1)}), bf16[32,2,3200]{2,1,0:T(2,128)(2,1)S(1)}, u32[]{:S(2)}, u32[]{:S(2)}) %all-to-all-start) | async-done | bytes 409632 | tf_op jit(solution)/shard_map/all_to_all | solution.py:79
  33.1 1.9 %collective-permute-start = (bf16[2,32,3200]{2,0,1:T(2,128)(2,1)S(1)}, bf16[2,32,3200]{2,0,1:T(2,128)(2,1)S(1)}, u32[]{:S(2)}, u32[]{:S(2)}) collective-permute-start(bf16[2,32,3200]{2,0,1:T(2,128)(2,1)S(1)} %bitcast.171), channel_id=1, source_target_pairs={{0,1},{1,0},{2,3},{3,2},{4,5},{5,4},{6,7},{7,6},{8,9},{9,8},{10,11... | collective-permute-start | bytes 1228808 | tf_op jit(solution)/shard_map/ppermute | solution.py:20
  35.1 1.7 %collective-permute-done = bf16[2,32,3200]{2,0,1:T(2,128)(2,1)S(1)} collective-permute-done((bf16[2,32,3200]{2,0,1:T(2,128)(2,1)S(1)}, bf16[2,32,3200]{2,0,1:T(2,128)(2,1)S(1)}, u32[]{:S(2)}, u32[]{:S(2)}) %collective-permute-start) | collective-permute-done | bytes 409632 | tf_op jit(solution)/shard_map/ppermute | solution.py:20
  36.8 1.1 %pad_maximum_fusion = bf16[2,64,3200]{2,0,1:T(2,128)(2,1)S(1)} fusion(bf16[2,32,3200]{2,0,1:T(2,128)(2,1)S(1)} %collective-permute-done, bf16[2,32,3200]{2,0,1:T(2,128)(2,1)S(1)} %bitcast.172), kind=kLoop, calls=%fused_computation.43 | loop fusion | flops 409600 | bytes 1638400 | tf_op jit(solution)/shard_map/concatenate | solution.py:81
  37.9 0.4 reshape.168
  38.4 0.2 copy.22
  38.8 0.4 fusion.86
  39.1 0.2 fusion.34
  39.4 0.3 fusion.36
  39.7 6.5 %collective-permute-start.2 = (f32[130,128]{1,0:T(8,128)S(1)}, f32[130,128]{1,0:T(8,128)S(1)}, u32[]{:S(2)}, u32[]{:S(2)}) collective-permute-start(f32[130,128]{1,0:T(8,128)S(1)} %pad_maximum_fusion.3), channel_id=1, source_target_pairs={{0,64},{64,128},{128,192},{192,256},{256,320},{320,384},{384,448},... | collective-permute-start | bytes 199688 | tf_op jit(solution)/shard_map/ppermute | solution.py:16
  46.2 0.4 fusion.85
  46.7 0.5 fusion.24
  47.2 0.3 fusion.22
  47.5 0.7 collective-permute-done.2
  48.2 0.3 multiply_reduce_fusion.2
  48.5 1.9 %collective-permute-start.3 = (f32[130,128]{1,0:T(8,128)S(1)}, f32[130,128]{1,0:T(8,128)S(1)}, u32[]{:S(2)}, u32[]{:S(2)}) collective-permute-start(f32[130,128]{1,0:T(8,128)S(1)} %pad_maximum_fusion.4), channel_id=1, source_target_pairs={{64,0},{128,64},{192,128},{256,192},{320,256},{384,320},{448,384},... | collective-permute-start | bytes 199688 | tf_op jit(solution)/shard_map/ppermute | solution.py:16
  50.4 0.3 fusion.44
  50.7 0.4 fusion.10
  51.1 0.2 fusion.75
  51.3 0.4 fusion.9
  51.7 0.3 fusion.15
  52.0 0.2 fusion.13
  52.2 4.9 %collective-permute-done.3 = f32[130,128]{1,0:T(8,128)S(1)} collective-permute-done((f32[130,128]{1,0:T(8,128)S(1)}, f32[130,128]{1,0:T(8,128)S(1)}, u32[]{:S(2)}, u32[]{:S(2)}) %collective-permute-start.3) | collective-permute-done | bytes 66592 | tf_op jit(solution)/shard_map/ppermute | solution.py:16
  57.2 0.2 multiply_reduce_fusion
  57.4 0.4 fusion.11
  57.8 0.3 fusion.18
  58.0 0.2 fusion.21
  58.3 0.3 fusion.41
  58.6 1.9 %collective-permute-start.5 = (bf16[2,25,8,4,128]{4,3,2,1,0:T(4,128)(2,1)S(1)}, bf16[2,25,8,4,128]{4,3,2,1,0:T(4,128)(2,1)S(1)}, u32[]{:S(2)}, u32[]{:S(2)}) collective-permute-start(bf16[2,25,8,4,128]{4,3,2,1,0:T(4,128)(2,1)S(1)} %fusion.41), channel_id=1, source_target_pairs={{0,1},{1,0},{2,3},{3,2},{4,5},{5,4},{6,7},{7,6},{8,9},{9,8},{10,11... | collective-permute-start | bytes 1228808 | tf_op jit(solution)/shard_map/ppermute | solution.py:20
  60.5 1.7 %collective-permute-done.5 = bf16[2,25,8,4,128]{4,3,2,1,0:T(4,128)(2,1)S(1)} collective-permute-done((bf16[2,25,8,4,128]{4,3,2,1,0:T(4,128)(2,1)S(1)}, bf16[2,25,8,4,128]{4,3,2,1,0:T(4,128)(2,1)S(1)}, u32[]{:S(2)}, u32[]{:S(2)}) %collective-permute-start.5) | collective-permute-done | bytes 409632 | tf_op jit(solution)/shard_map/ppermute | solution.py:20
  62.2 0.3 fusion.38
  62.5 1.1 %copy.24 = bf16[8,4,2,25,128]{4,2,3,1,0:T(2,128)(2,1)} copy(bf16[8,4,2,25,128]{4,1,0,3,2:T(4,128)(2,1)S(1)} %fusion.38) | data formatting | bytes 819200 | tf_op jit(solution)/shard_map/transpose | solution.py:219
  63.6 4.6 %all-to-all-start.1 = ((bf16[32,2,25,128]{3,1,2,0:T(2,128)(2,1)}), bf16[32,2,25,128]{3,1,2,0:T(2,128)(2,1)S(1)}, u32[]{:S(2)}, u32[]{:S(2)}) async-start(bf16[32,2,25,128]{3,1,2,0:T(2,128)(2,1)} %bitcast.34), calls=%async_computation.1 | async-start | bytes 819200 | tf_op jit(solution)/shard_map/all_to_all | solution.py:221
  68.2 0.3 fusion.87
  68.5 0.3 fusion.88
  68.9 0.3 fusion.89
  69.2 3.9 %collective-permute-start.4 = (f32[128,128]{1,0:T(8,128)S(1)}, f32[128,128]{1,0:T(8,128)S(1)}, u32[]{:S(2)}, u32[]{:S(2)}) collective-permute-start(f32[128,128]{1,0:T(8,128)S(1)} %fusion.89), channel_id=1, source_target_pairs={{0,64},{64,128},{128,192},{192,256},{256,320},{320,384},{384,448},... | collective-permute-start | bytes 196616 | tf_op jit(solution)/shard_map/ppermute | solution.py:16
  73.1 0.6 pad_maximum_fusion.5
  73.8 2.5 %collective-permute-done.4 = f32[128,128]{1,0:T(8,128)S(1)} collective-permute-done((f32[128,128]{1,0:T(8,128)S(1)}, f32[128,128]{1,0:T(8,128)S(1)}, u32[]{:S(2)}, u32[]{:S(2)}) %collective-permute-start.4) | collective-permute-done | bytes 65568 | tf_op jit(solution)/shard_map/ppermute | solution.py:16
  76.3 0.6 fusion.49
  76.9 7.6 %all-to-all-done.1 = bf16[32,2,25,128]{3,1,2,0:T(2,128)(2,1)S(1)} async-done(((bf16[32,2,25,128]{3,1,2,0:T(2,128)(2,1)}), bf16[32,2,25,128]{3,1,2,0:T(2,128)(2,1)S(1)}, u32[]{:S(2)}, u32[]{:S(2)}) %all-to-all-start.1) | async-done | bytes 409632 | tf_op jit(solution)/shard_map/all_to_all | solution.py:221
  84.5 0.4 bitcast_reduce_fusion
  85.0 0.6 copy.27
  85.6 0.6 copy.26
  (29 shorter events, 0.6 us)
Async XLA Ops:
  0.6 14.0 %copy-start.2 = (s32[256,2]{0,1:T(2,128)S(1)}, s32[256,2]{0,1:T(2,128)}, u32[]{:S(2)}) copy-start(s32[256,2]{0,1:T(2,128)} %param.9) | copy-start | bytes 6148
  0.6 14.1 %slice-start = ((bf16[256,128]{1,0:T(8,128)(2,1)}), bf16[128,128]{1,0:T(8,128)(2,1)S(1)}, s32[]{:S(2)}) async-start(bf16[256,128]{1,0:T(8,128)(2,1)} %param.5), calls=%async_computation.2 | async-start | bytes 65536 | tf_op jit(solution)/shard_map/slice | solution.py:66
  0.7 14.1 %slice-start.1 = ((bf16[256,128]{1,0:T(8,128)(2,1)}), bf16[128,128]{1,0:T(8,128)(2,1)S(1)}, s32[]{:S(2)}) async-start(bf16[256,128]{1,0:T(8,128)(2,1)} %param.8), calls=%async_computation.3 | async-start | bytes 65536 | tf_op jit(solution)/shard_map/slice | solution.py:67
  2.6 30.5 %all-to-all-start = ((bf16[32,2,3200]{2,1,0:T(2,128)(2,1)}), bf16[32,2,3200]{2,1,0:T(2,128)(2,1)S(1)}, u32[]{:S(2)}, u32[]{:S(2)}) async-start(bf16[32,2,3200]{2,1,0:T(2,128)(2,1)} %bitcast.3), calls=%async_computation | async-start | bytes 819200 | tf_op jit(solution)/shard_map/all_to_all | solution.py:79
  14.8 20.3 %collective-permute-start.1 = (bf16[2,129,128]{2,1,0:T(8,128)(2,1)S(1)}, bf16[2,129,128]{2,1,0:T(8,128)(2,1)S(1)}, u32[]{:S(2)}, u32[]{:S(2)}) collective-permute-start(bf16[2,129,128]{2,1,0:T(8,128)(2,1)S(1)} %pad_maximum_fusion.2), channel_id=1, source_target_pairs={{64,0},{128,64},{192,128},{256,192},{320,256},{384,320},{448,384},... | collective-permute-start | bytes 198152 | tf_op jit(solution)/shard_map/ppermute | solution.py:16
  33.1 3.6 %collective-permute-start = (bf16[2,32,3200]{2,0,1:T(2,128)(2,1)S(1)}, bf16[2,32,3200]{2,0,1:T(2,128)(2,1)S(1)}, u32[]{:S(2)}, u32[]{:S(2)}) collective-permute-start(bf16[2,32,3200]{2,0,1:T(2,128)(2,1)S(1)} %bitcast.171), channel_id=1, source_target_pairs={{0,1},{1,0},{2,3},{3,2},{4,5},{5,4},{6,7},{7,6},{8,9},{9,8},{10,11... | collective-permute-start | bytes 1228808 | tf_op jit(solution)/shard_map/ppermute | solution.py:20
  38.7 7.5 %copy-start = (bf16[256,128]{1,0:T(8,128)(2,1)S(1)}, bf16[256,128]{1,0:T(8,128)(2,1)}, u32[]{:S(2)}) copy-start(bf16[256,128]{1,0:T(8,128)(2,1)} %param.5) | copy-start | bytes 196612
  39.7 8.4 %collective-permute-start.2 = (f32[130,128]{1,0:T(8,128)S(1)}, f32[130,128]{1,0:T(8,128)S(1)}, u32[]{:S(2)}, u32[]{:S(2)}) collective-permute-start(f32[130,128]{1,0:T(8,128)S(1)} %pad_maximum_fusion.3), channel_id=1, source_target_pairs={{0,64},{64,128},{128,192},{192,256},{256,320},{320,384},{384,448},... | collective-permute-start | bytes 199688 | tf_op jit(solution)/shard_map/ppermute | solution.py:16
  46.7 1.5 %copy-start.1 = (bf16[256,128]{1,0:T(8,128)(2,1)S(1)}, bf16[256,128]{1,0:T(8,128)(2,1)}, u32[]{:S(2)}) copy-start(bf16[256,128]{1,0:T(8,128)(2,1)} %param.8) | copy-start | bytes 196612
  48.5 8.7 %collective-permute-start.3 = (f32[130,128]{1,0:T(8,128)S(1)}, f32[130,128]{1,0:T(8,128)S(1)}, u32[]{:S(2)}, u32[]{:S(2)}) collective-permute-start(f32[130,128]{1,0:T(8,128)S(1)} %pad_maximum_fusion.4), channel_id=1, source_target_pairs={{64,0},{128,64},{192,128},{256,192},{320,256},{384,320},{448,384},... | collective-permute-start | bytes 199688 | tf_op jit(solution)/shard_map/ppermute | solution.py:16
  58.6 3.6 %collective-permute-start.5 = (bf16[2,25,8,4,128]{4,3,2,1,0:T(4,128)(2,1)S(1)}, bf16[2,25,8,4,128]{4,3,2,1,0:T(4,128)(2,1)S(1)}, u32[]{:S(2)}, u32[]{:S(2)}) collective-permute-start(bf16[2,25,8,4,128]{4,3,2,1,0:T(4,128)(2,1)S(1)} %fusion.41), channel_id=1, source_target_pairs={{0,1},{1,0},{2,3},{3,2},{4,5},{5,4},{6,7},{7,6},{8,9},{9,8},{10,11... | collective-permute-start | bytes 1228808 | tf_op jit(solution)/shard_map/ppermute | solution.py:20
  63.6 20.9 %all-to-all-start.1 = ((bf16[32,2,25,128]{3,1,2,0:T(2,128)(2,1)}), bf16[32,2,25,128]{3,1,2,0:T(2,128)(2,1)S(1)}, u32[]{:S(2)}, u32[]{:S(2)}) async-start(bf16[32,2,25,128]{3,1,2,0:T(2,128)(2,1)} %bitcast.34), calls=%async_computation.1 | async-start | bytes 819200 | tf_op jit(solution)/shard_map/all_to_all | solution.py:221
  69.2 7.1 %collective-permute-start.4 = (f32[128,128]{1,0:T(8,128)S(1)}, f32[128,128]{1,0:T(8,128)S(1)}, u32[]{:S(2)}, u32[]{:S(2)}) collective-permute-start(f32[128,128]{1,0:T(8,128)S(1)} %fusion.89), channel_id=1, source_target_pairs={{0,64},{64,128},{128,192},{192,256},{256,320},{320,384},{384,448},... | collective-permute-start | bytes 196616 | tf_op jit(solution)/shard_map/ppermute | solution.py:16

commit v13 on v12

--- a/solution.py
+++ b/solution.py
@@ -8,6 +8,18 @@
 KVH = 8
 
 NEGATIVE = -1e30
+
+
+def pieces(x):
+    hi = x.astype(jnp.bfloat16)
+    rest = x - hi.astype(jnp.float32)
+    mid = rest.astype(jnp.bfloat16)
+    lo = (rest - mid.astype(jnp.float32)).astype(jnp.bfloat16)
+    return [hi, mid, lo]
+
+
+def joined(parts):
+    return sum(p.astype(jnp.float32) for p in parts)
 
 
 def passed_along(value, axis, by):
@@ -100,13 +112,16 @@
         value_own,
         preferred_element_type=jnp.float32,
     )
+    step = half // HD
     stats = jnp.concatenate(
-        [partial_next, peak_next.reshape(-1, HD), total_next.reshape(-1, HD)]
+        [partial_next.astype(jnp.bfloat16)]
+        + [p.reshape(-1, HD) for p in pieces(peak_next) + pieces(total_next)]
     )
     stats = passed_along(stats, "seq", 1)
     seen = keep_prev[:half] > 0
-    got_peak = stats[half : half + half // HD].reshape(half)
-    got_total = stats[half + half // HD :].reshape(half)
+    got = [stats[half + i * step : half + (i + 1) * step].reshape(half) for i in range(6)]
+    got_peak = joined(got[:3])
+    got_total = joined(got[3:])
     rest = tokens - half
     peak_prev = jnp.concatenate(
         [jnp.where(seen, got_peak, NEGATIVE), jnp.full((rest,), NEGATIVE, jnp.float32)]
@@ -115,7 +130,10 @@
         [jnp.where(seen, got_total, 0.0), jnp.zeros((rest,), jnp.float32)]
     )
     partial_prev = jnp.concatenate(
-        [jnp.where(seen[:, None], stats[:half], 0.0), jnp.zeros((rest, HD), jnp.float32)]
+        [
+            jnp.where(seen[:, None], stats[:half].astype(jnp.float32), 0.0),
+            jnp.zeros((rest, HD), jnp.float32),
+        ]
     )
 
     highest = jnp.maximum(peak_own[:half], peak_prev[:half])
@@ -153,13 +171,15 @@
     attended = jnp.concatenate([attended_head, attended_tail])
 
     mine = jnp.concatenate(
-        [partial_own[:half], peak_own[:half].reshape(-1, HD), total_own[:half].reshape(-1, HD)]
+        [partial_own[:half].astype(jnp.bfloat16)]
+        + [p.reshape(-1, HD) for p in pieces(peak_own[:half]) + pieces(total_own[:half])]
     )
     mine = passed_along(mine, "seq", -1)
+    got_next = [mine[half + i * step : half + (i + 1) * step].reshape(half) for i in range(6)]
     seen_next = keep_prev_next > 0
     live_next = (keep_own_next + keep_prev_next > 0).astype(jnp.float32)
-    peak_own_next = mine[half : half + half // HD].reshape(half)
-    total_own_next = mine[half + half // HD :].reshape(half)
+    peak_own_next = joined(got_next[:3])
+    total_own_next = joined(got_next[3:])
     peak_prev_next = jnp.where(seen_next, peak_next, NEGATIVE)
     highest_next = jnp.maximum(peak_own_next, peak_prev_next)
     scale_own_next = jnp.exp(peak_own_next - highest_next)
@@ -171,7 +191,7 @@
     attended_next = (
         live_next[:, None]
         * (
-            scale_own_next[:, None] * mine[:half]
+            scale_own_next[:, None] * mine[:half].astype(jnp.float32)
             + scale_prev_next[:, None] * jnp.where(seen_next[:, None], partial_next, 0.0)
         )
         / totals_next[:, None]

time: 86.8 us -> 97.1 us (1.12)
  the two profiles are of different devices: /device:TPU:402 before, /device:TPU:400 now
where the time goes in v13:
time: 97.1 us; the launch traced here: 96.3 us
  starting transfers between devices  35.9 us (37%)
  waiting for transfers between devices  32.2 us (33%)
  other arithmetic  10.3 us (11%)
  local copies, waits for them, and re-layouts  9.22 us (9%)
  matrix products  7.65 us (8%)
  between operations  1.11 us (1%)
    all_to_all x1, waiting for transfers between devices, per_device(): lax.all_to_all(own_kv, ('y', 'xh'), split_axis=0, concat_axis=0, tiled=True)  15.1 us
    ppermute x4, starting transfers between devices, passed_along(): return lax.ppermute(value, axis, pairs)  13.9 us
    all_to_all x1, starting transfers between devices, per_device(): lax.all_to_all(own_kv, ('y', 'xh'), split_axis=0, concat_axis=0, tiled=True)  13 us
    all_to_all x1, waiting for transfers between devices, per_device(): lax.all_to_all(summed, ('y', 'xh'), split_axis=0, concat_axis=0, tiled=True)  8.49 us
    ppermute x4, waiting for transfers between devices, passed_along(): return lax.ppermute(value, axis, pairs)  6.34 us
    all_to_all x1, starting transfers between devices, per_device(): lax.all_to_all(summed, ('y', 'xh'), split_axis=0, concat_axis=0, tiled=True)  5.18 us
    ppermute x2, starting transfers between devices, partner(): return lax.ppermute(value, 'c', [(0, 1), (1, 0)])  3.83 us
    unnamed x45, local copies, waits for them, and re-layouts  3.56 us
  transfers between devices with their start and end apart: 8, of which 7 were waited for; matrix products, arithmetic and copies ran while one was open for 7% of the time, Pallas kernels for 0%

profile of v13, /device:TPU:400, one launch (start us, length us, event | category | flops | bytes accessed | tf_op | source)
XLA Modules:
  0.0 96.3 jit_solution(14320319390092238804)
XLA Ops:
  0.7 0.9 maximum_bitcast_fusion
  1.6 1.0 %broadcast_in_dim.96 = bf16[8,4,2,3200]{3,2,1,0:T(2,128)(2,1)} broadcast(bf16[8,2,3200]{2,1,0:T(2,128)(2,1)S(1)} %copy.19), dimensions={0,2,3} | broadcast | bytes 512000 | tf_op jit(solution)/shard_map/broadcast_in_dim | solution.py:90
  2.6 13.0 %all-to-all-start = ((bf16[32,2,3200]{2,1,0:T(2,128)(2,1)}), bf16[32,2,3200]{2,1,0:T(2,128)(2,1)S(1)}, u32[]{:S(2)}, u32[]{:S(2)}) async-start(bf16[32,2,3200]{2,1,0:T(2,128)(2,1)} %bitcast.3), calls=%async_computation | async-start | bytes 819200 | tf_op jit(solution)/shard_map/all_to_all | solution.py:91
  15.6 1.9 %collective-permute-start.1 = (bf16[2,129,128]{2,1,0:T(8,128)(2,1)S(1)}, bf16[2,129,128]{2,1,0:T(8,128)(2,1)S(1)}, u32[]{:S(2)}, u32[]{:S(2)}) collective-permute-start(bf16[2,129,128]{2,1,0:T(8,128)(2,1)S(1)} %pad_maximum_fusion.2), channel_id=1, source_target_pairs={{64,0},{128,64},{192,128},{256,192},{320,256},{384,320},{448,384},... | collective-permute-start | bytes 198152 | tf_op jit(solution)/shard_map/ppermute | solution.py:28
  17.6 0.5 compare_bitcast_fusion.1
  18.1 15.1 %all-to-all-done = bf16[32,2,3200]{2,1,0:T(2,128)(2,1)S(1)} async-done(((bf16[32,2,3200]{2,1,0:T(2,128)(2,1)}), bf16[32,2,3200]{2,1,0:T(2,128)(2,1)S(1)}, u32[]{:S(2)}, u32[]{:S(2)}) %all-to-all-start) | async-done | bytes 409632 | tf_op jit(solution)/shard_map/all_to_all | solution.py:91
  33.2 1.9 %collective-permute-start = (bf16[2,32,3200]{2,0,1:T(2,128)(2,1)S(1)}, bf16[2,32,3200]{2,0,1:T(2,128)(2,1)S(1)}, u32[]{:S(2)}, u32[]{:S(2)}) collective-permute-start(bf16[2,32,3200]{2,0,1:T(2,128)(2,1)S(1)} %bitcast.189), channel_id=1, source_target_pairs={{0,1},{1,0},{2,3},{3,2},{4,5},{5,4},{6,7},{7,6},{8,9},{9,8},{10,11... | collective-permute-start | bytes 1228808 | tf_op jit(solution)/shard_map/ppermute | solution.py:32
  35.2 0.6 slice_bitcast_fusion.6
  35.7 0.6 compare_bitcast_fusion
  36.3 0.6 collective-permute-done
  36.9 1.1 %pad_maximum_fusion = bf16[2,64,3200]{2,0,1:T(2,128)(2,1)S(1)} fusion(bf16[2,32,3200]{2,0,1:T(2,128)(2,1)S(1)} %collective-permute-done, bf16[2,32,3200]{2,0,1:T(2,128)(2,1)S(1)} %bitcast.190), kind=kLoop, calls=%fused_computation.43 | loop fusion | flops 409600 | bytes 1638400 | tf_op jit(solution)/shard_map/concatenate | solution.py:93
  38.0 0.4 reshape.305
  38.7 0.6 copy-done.6
  39.3 0.4 fusion.89
  40.0 0.5 convert_bitcast_fusion.2
  40.5 0.6 convert_bitcast_fusion
  41.3 0.4 fusion.88
  41.7 0.6 subtract_convert_fusion.1
  42.3 0.7 fusion.34
  43.0 0.5 fusion.24
  43.5 0.7 concatenate.32
  44.3 1.9 %collective-permute-start.3 = (bf16[134,128]{1,0:T(8,128)(2,1)S(1)}, bf16[134,128]{1,0:T(8,128)(2,1)S(1)}, u32[]{:S(2)}, u32[]{:S(2)}) collective-permute-start(bf16[134,128]{1,0:T(8,128)(2,1)S(1)} %concatenate.32), channel_id=1, source_target_pairs={{64,0},{128,64},{192,128},{256,192},{320,256},{384,320},{448,384},... | collective-permute-start | bytes 102920 | tf_op jit(solution)/shard_map/ppermute | solution.py:28
  46.2 1.2 %subtract_convert_fusion = (bf16[1,128]{1,0:T(2,128)(2,1)}, bf16[1,128]{1,0:T(2,128)(2,1)}) fusion(f32[128]{0:T(128)} %fusion.34), kind=kLoop, calls=%fused_computation.147 | loop fusion | flops 896 | bytes 1024 | tf_op jit(solution)/shard_map/convert_element_type | solution.py:17
  47.4 2.7 %collective-permute-done.3 = bf16[134,128]{1,0:T(8,128)(2,1)S(1)} collective-permute-done((bf16[134,128]{1,0:T(8,128)(2,1)S(1)}, bf16[134,128]{1,0:T(8,128)(2,1)S(1)}, u32[]{:S(2)}, u32[]{:S(2)}) %collective-permute-start.3) | collective-permute-done | bytes 34336 | tf_op jit(solution)/shard_map/ppermute | solution.py:28
  50.1 1.2 %compare_select_fusion = (f32[128]{0:T(128)S(1)}, f32[128]{0:T(128)S(1)}, f32[128]{0:T(128)S(1)}, f32[128]{0:T(128)}, f32[128]{0:T(128)S(1)}, /*index=5*/bf16[1,128]{1,0:T(2,128)(2,1)}, bf16[1,128]{1,0:T(2,128)(2,1)}) fusion(f32[128]{0:T(128)} %fusion.34, bf16[134,128]{1,0:T(8,128)(2,1)S(1)} %collective-permute-done.3, bf16[2,129,128]{2,1,0:T(8,128)(2,1)} %copy-done.8, ...), kind=kLoop, calls=%fused_computation.89 | loop fusion | flops 3584 | bytes 6144 | tf_op jit(solution)/shard_map/jit(_where)/select_n | solution.py:190
  51.3 1.7 %multiply_reduce_fusion = (f32[128]{0:T(128)}, bf16[128,128]{1,0:T(8,128)(2,1)S(1)}) fusion(f32[128]{0:T(128)S(1)} %get-tuple-element.10, pred[128]{0:T(512)(128)(4,1)} %compare_bitcast_fusion, f32[128]{0:T(128)S(1)} %get-tuple-element.12, bf16[134,128]{1,0:T(8,128)(2,1)S(1)} %collective-permute-done.3, f32[128]{0:T(128)S(1)} %get-tuple-element.11, ...), kind=kOutput, calls=%fused_computation.74 | convolution fusion | flops 53051264 | bytes 1330304 | tf_op jit(solution)/shard_map/dot_general | solution.py:110
  53.0 0.7 concatenate.29
  53.8 5.8 %collective-permute-start.2 = (bf16[134,128]{1,0:T(8,128)(2,1)S(1)}, bf16[134,128]{1,0:T(8,128)(2,1)S(1)}, u32[]{:S(2)}, u32[]{:S(2)}) collective-permute-start(bf16[134,128]{1,0:T(8,128)(2,1)S(1)} %concatenate.29), channel_id=1, source_target_pairs={{0,64},{64,128},{128,192},{192,256},{256,320},{320,384},{384,448},... | collective-permute-start | bytes 102920 | tf_op jit(solution)/shard_map/ppermute | solution.py:28
  59.7 1.4 %fusion.11 = bf16[128,1600]{0,1:T(8,128)(2,1)S(1)} fusion(bf16[1600,128]{1,0:T(8,128)(2,1)} %bitcast.186, f32[128]{0:T(128)} %get-tuple-element.25, f32[128]{0:T(128)} %copy-done.17, f32[128,1600]{0,1:T(8,128)S(1)} %get-tuple-element.46, f32[128]{0:T(128)} %get-tuple-element.13, pred[128]{0:T(512)(128)(4,1)} %compare_bitcast_fusion, ...), kind=kOutput, calls=%fused_computation.18 | convolution fusion | flops 53862400 | bytes 1673216 | tf_op jit(solution)/shard_map/rd,kd->rk/dot_general | solution.py:52
  62.3 0.4 fusion.10
  63.0 0.4 fusion.9
  63.7 0.4 copy-done.4
  64.4 0.6 copy-done.9
  65.9 1.9 %collective-permute-start.5 = (bf16[2,25,8,4,128]{4,3,2,1,0:T(4,128)(2,1)S(1)}, bf16[2,25,8,4,128]{4,3,2,1,0:T(4,128)(2,1)S(1)}, u32[]{:S(2)}, u32[]{:S(2)}) collective-permute-start(bf16[2,25,8,4,128]{4,3,2,1,0:T(4,128)(2,1)S(1)} %fusion.41), channel_id=1, source_target_pairs={{0,1},{1,0},{2,3},{3,2},{4,5},{5,4},{6,7},{7,6},{8,9},{9,8},{10,11... | collective-permute-start | bytes 1228808 | tf_op jit(solution)/shard_map/ppermute | solution.py:32
  67.8 1.7 %collective-permute-done.5 = bf16[2,25,8,4,128]{4,3,2,1,0:T(4,128)(2,1)S(1)} collective-permute-done((bf16[2,25,8,4,128]{4,3,2,1,0:T(4,128)(2,1)S(1)}, bf16[2,25,8,4,128]{4,3,2,1,0:T(4,128)(2,1)S(1)}, u32[]{:S(2)}, u32[]{:S(2)}) %collective-permute-start.5) | collective-permute-done | bytes 409632 | tf_op jit(solution)/shard_map/ppermute | solution.py:32
  69.8 1.1 %copy.24 = bf16[8,4,2,25,128]{4,2,3,1,0:T(2,128)(2,1)} copy(bf16[8,4,2,25,128]{4,1,0,3,2:T(4,128)(2,1)S(1)} %fusion.38) | data formatting | bytes 819200 | tf_op jit(solution)/shard_map/transpose | solution.py:239
  70.9 5.2 %all-to-all-start.1 = ((bf16[32,2,25,128]{3,1,2,0:T(2,128)(2,1)}), bf16[32,2,25,128]{3,1,2,0:T(2,128)(2,1)S(1)}, u32[]{:S(2)}, u32[]{:S(2)}) async-start(bf16[32,2,25,128]{3,1,2,0:T(2,128)(2,1)} %bitcast.38), calls=%async_computation.1 | async-start | bytes 819200 | tf_op jit(solution)/shard_map/all_to_all | solution.py:241
  76.1 0.3 fusion.92
  76.4 4.2 %collective-permute-start.4 = (f32[128,128]{1,0:T(8,128)S(1)}, f32[128,128]{1,0:T(8,128)S(1)}, u32[]{:S(2)}, u32[]{:S(2)}) collective-permute-start(f32[128,128]{1,0:T(8,128)S(1)} %fusion.92), channel_id=1, source_target_pairs={{0,64},{64,128},{128,192},{192,256},{256,320},{320,384},{384,448},... | collective-permute-start | bytes 196616 | tf_op jit(solution)/shard_map/ppermute | solution.py:28
  80.7 0.3 fusion.90
  81.0 0.3 fusion.91
  81.3 0.6 pad_maximum_fusion.3
  82.0 3.5 %collective-permute-done.4 = f32[128,128]{1,0:T(8,128)S(1)} collective-permute-done((f32[128,128]{1,0:T(8,128)S(1)}, f32[128,128]{1,0:T(8,128)S(1)}, u32[]{:S(2)}, u32[]{:S(2)}) %collective-permute-start.4) | collective-permute-done | bytes 65568 | tf_op jit(solution)/shard_map/ppermute | solution.py:28
  85.5 0.6 fusion.49
  86.1 8.5 %all-to-all-done.1 = bf16[32,2,25,128]{3,1,2,0:T(2,128)(2,1)S(1)} async-done(((bf16[32,2,25,128]{3,1,2,0:T(2,128)(2,1)}), bf16[32,2,25,128]{3,1,2,0:T(2,128)(2,1)S(1)}, u32[]{:S(2)}, u32[]{:S(2)}) %all-to-all-start.1) | async-done | bytes 409632 | tf_op jit(solution)/shard_map/all_to_all | solution.py:241
  94.6 0.4 bitcast_reduce_fusion
  95.1 0.6 copy.27
  95.7 0.6 copy.26
  (69 shorter events, 4.2 us)
Async XLA Ops:
  0.6 14.9 %copy-start.10 = (s32[256,2]{0,1:T(2,128)S(1)}, s32[256,2]{0,1:T(2,128)}, u32[]{:S(2)}) copy-start(s32[256,2]{0,1:T(2,128)} %param.9) | copy-start | bytes 6148
  0.6 14.9 %slice-start = ((bf16[256,128]{1,0:T(8,128)(2,1)}), bf16[128,128]{1,0:T(8,128)(2,1)S(1)}, s32[]{:S(2)}) async-start(bf16[256,128]{1,0:T(8,128)(2,1)} %param.5), calls=%async_computation.2 | async-start | bytes 65536 | tf_op jit(solution)/shard_map/slice | solution.py:78
  0.7 14.9 %slice-start.1 = ((bf16[256,128]{1,0:T(8,128)(2,1)}), bf16[128,128]{1,0:T(8,128)(2,1)S(1)}, s32[]{:S(2)}) async-start(bf16[256,128]{1,0:T(8,128)(2,1)} %param.8), calls=%async_computation.3 | async-start | bytes 65536 | tf_op jit(solution)/shard_map/slice | solution.py:79
  2.6 30.7 %all-to-all-start = ((bf16[32,2,3200]{2,1,0:T(2,128)(2,1)}), bf16[32,2,3200]{2,1,0:T(2,128)(2,1)S(1)}, u32[]{:S(2)}, u32[]{:S(2)}) async-start(bf16[32,2,3200]{2,1,0:T(2,128)(2,1)} %bitcast.3), calls=%async_computation | async-start | bytes 819200 | tf_op jit(solution)/shard_map/all_to_all | solution.py:91
  15.6 20.1 %collective-permute-start.1 = (bf16[2,129,128]{2,1,0:T(8,128)(2,1)S(1)}, bf16[2,129,128]{2,1,0:T(8,128)(2,1)S(1)}, u32[]{:S(2)}, u32[]{:S(2)}) collective-permute-start(bf16[2,129,128]{2,1,0:T(8,128)(2,1)S(1)} %pad_maximum_fusion.2), channel_id=1, source_target_pairs={{64,0},{128,64},{192,128},{256,192},{320,256},{384,320},{448,384},... | collective-permute-start | bytes 198152 | tf_op jit(solution)/shard_map/ppermute | solution.py:28
  33.2 3.6 %collective-permute-start = (bf16[2,32,3200]{2,0,1:T(2,128)(2,1)S(1)}, bf16[2,32,3200]{2,0,1:T(2,128)(2,1)S(1)}, u32[]{:S(2)}, u32[]{:S(2)}) collective-permute-start(bf16[2,32,3200]{2,0,1:T(2,128)(2,1)S(1)} %bitcast.189), channel_id=1, source_target_pairs={{0,1},{1,0},{2,3},{3,2},{4,5},{5,4},{6,7},{7,6},{8,9},{9,8},{10,11... | collective-permute-start | bytes 1228808 | tf_op jit(solution)/shard_map/ppermute | solution.py:32
  35.7 5.6 %copy-start.8 = (bf16[2,129,128]{2,1,0:T(8,128)(2,1)}, bf16[2,129,128]{2,1,0:T(8,128)(2,1)S(1)}, u32[]{:S(2)}) copy-start(bf16[2,129,128]{2,1,0:T(8,128)(2,1)S(1)} %collective-permute-done.1) | copy-start | bytes 198148
  38.4 0.8 copy-start.6
  41.3 10.0 %copy-start.2 = (bf16[1,25,64,128]{3,2,1,0:T(8,128)(2,1)}, bf16[1,25,64,128]{3,2,1,0:T(8,128)(2,1)S(1)}, u32[]{:S(2)}) copy-start(bf16[1,25,64,128]{3,2,1,0:T(8,128)(2,1)S(1)} %copy.22) | copy-start | bytes 1228804
  41.7 1.3 %copy-start.11 = (f32[128]{0:T(128)}, f32[128]{0:T(128)S(1)}, u32[]{:S(2)}) copy-start(f32[128]{0:T(128)S(1)} %get-tuple-element.45) | copy-start | bytes 1540
  44.3 5.8 %collective-permute-start.3 = (bf16[134,128]{1,0:T(8,128)(2,1)S(1)}, bf16[134,128]{1,0:T(8,128)(2,1)S(1)}, u32[]{:S(2)}, u32[]{:S(2)}) collective-permute-start(bf16[134,128]{1,0:T(8,128)(2,1)S(1)} %concatenate.32), channel_id=1, source_target_pairs={{64,0},{128,64},{192,128},{256,192},{320,256},{384,320},{448,384},... | collective-permute-start | bytes 102920 | tf_op jit(solution)/shard_map/ppermute | solution.py:28
  51.3 1.7 %copy-start.17 = (f32[128]{0:T(128)}, f32[128]{0:T(128)S(1)}, u32[]{:S(2)}) copy-start(f32[128]{0:T(128)S(1)} %get-tuple-element.10) | copy-start | bytes 1540
  53.8 7.4 %collective-permute-start.2 = (bf16[134,128]{1,0:T(8,128)(2,1)S(1)}, bf16[134,128]{1,0:T(8,128)(2,1)S(1)}, u32[]{:S(2)}, u32[]{:S(2)}) collective-permute-start(bf16[134,128]{1,0:T(8,128)(2,1)S(1)} %concatenate.29), channel_id=1, source_target_pairs={{0,64},{64,128},{128,192},{192,256},{256,320},{320,384},{384,448},... | collective-permute-start | bytes 102920 | tf_op jit(solution)/shard_map/ppermute | solution.py:28
  59.6 1.6 %copy-start.7 = (bf16[256,128]{1,0:T(8,128)(2,1)S(1)}, bf16[256,128]{1,0:T(8,128)(2,1)}, u32[]{:S(2)}) copy-start(bf16[256,128]{1,0:T(8,128)(2,1)} %param.8) | copy-start | bytes 196612
  59.6 1.6 %copy-start.14 = (f32[128]{0:T(128)S(1)}, f32[128]{0:T(128)}, u32[]{:S(2)}) copy-start(f32[128]{0:T(128)} %get-tuple-element.36) | copy-start | bytes 1540
  61.3 0.6 copy-start.12
  61.3 0.7 copy-start.13
  61.3 0.7 copy-start.15
  61.3 1.0 %copy-start.3 = (bf16[1,25,64,128]{3,2,1,0:T(8,128)(2,1)S(1)}, bf16[1,25,64,128]{3,2,1,0:T(8,128)(2,1)}, u32[]{:S(2)}) copy-start(bf16[1,25,64,128]{3,2,1,0:T(8,128)(2,1)} %copy-done.2) | copy-start | bytes 1228804
  62.3 0.7 copy-start.16
  62.7 0.8 copy-start
  63.4 0.7 copy-start.4
  64.2 0.9 copy-start.9
  64.2 0.9 copy-start.18
  64.2 0.9 copy-start.19
  64.2 0.9 copy-start.20
  65.9 3.6 %collective-permute-start.5 = (bf16[2,25,8,4,128]{4,3,2,1,0:T(4,128)(2,1)S(1)}, bf16[2,25,8,4,128]{4,3,2,1,0:T(4,128)(2,1)S(1)}, u32[]{:S(2)}, u32[]{:S(2)}) collective-permute-start(bf16[2,25,8,4,128]{4,3,2,1,0:T(4,128)(2,1)S(1)} %fusion.41), channel_id=1, source_target_pairs={{0,1},{1,0},{2,3},{3,2},{4,5},{5,4},{6,7},{7,6},{8,9},{9,8},{10,11... | collective-permute-start | bytes 1228808 | tf_op jit(solution)/shard_map/ppermute | solution.py:32
  69.8 10.9 %copy-start.1 = (bf16[128,1600]{0,1:T(8,128)(2,1)S(1)}, bf16[128,1600]{0,1:T(8,128)(2,1)}, u32[]{:S(2)}) copy-start(bf16[128,1600]{0,1:T(8,128)(2,1)} %copy-done) | copy-start | bytes 1228804
  69.8 11.2 %copy-start.5 = (bf16[128,1600]{0,1:T(8,128)(2,1)S(1)}, bf16[128,1600]{0,1:T(8,128)(2,1)}, u32[]{:S(2)}) copy-start(bf16[128,1600]{0,1:T(8,128)(2,1)} %copy-done.4) | copy-start | bytes 1228804
  70.9 23.7 %all-to-all-start.1 = ((bf16[32,2,25,128]{3,1,2,0:T(2,128)(2,1)}), bf16[32,2,25,128]{3,1,2,0:T(2,128)(2,1)S(1)}, u32[]{:S(2)}, u32[]{:S(2)}) async-start(bf16[32,2,25,128]{3,1,2,0:T(2,128)(2,1)} %bitcast.38), calls=%async_computation.1 | async-start | bytes 819200 | tf_op jit(solution)/shard_map/all_to_all | solution.py:241
  76.4 9.0 %collective-permute-start.4 = (f32[128,128]{1,0:T(8,128)S(1)}, f32[128,128]{1,0:T(8,128)S(1)}, u32[]{:S(2)}, u32[]{:S(2)}) collective-permute-start(f32[128,128]{1,0:T(8,128)S(1)} %fusion.92), channel_id=1, source_target_pairs={{0,64},{64,128},{128,192},{192,256},{256,320},{320,384},{384,448},... | collective-permute-start | bytes 196616 | tf_op jit(solution)/shard_map/ppermute | solution.py:28

commit v14 on v12

--- a/solution.py
+++ b/solution.py
@@ -86,8 +86,12 @@
     keep_own = mask[:, 0]
     keep_prev = mask[:, 1]
     live_rows = (keep_own + keep_prev > 0).astype(jnp.float32)
-    score_own, peak_own, total_own, partial_own = block_forward(
-        queries, key_own, value_own, keep_own
+    own = [
+        block_forward(queries[:half], key_own, value_own, keep_own[:half]),
+        block_forward(queries[half:], key_own, value_own, keep_own[half:]),
+    ]
+    score_own, peak_own, total_own, partial_own = (
+        jnp.concatenate([own[0][i], own[1][i]]) for i in range(4)
     )
 
     score_next = jnp.einsum(

time: 86.8 us -> 89.2 us (1.028)
  the two profiles are of different devices: /device:TPU:402 before, /device:TPU:400 now
where the time goes in v14:
time: 89.2 us; the launch traced here: 88.6 us
  starting transfers between devices  35.7 us (40%)
  waiting for transfers between devices  35.2 us (39%)
  matrix products  5.99 us (7%)
  local copies, waits for them, and re-layouts  5.74 us (6%)
  other arithmetic  4.96 us (6%)
  between operations  1 us (1%)
    all_to_all x1, waiting for transfers between devices, per_device(): lax.all_to_all(own_kv, ('y', 'xh'), split_axis=0, concat_axis=0, tiled=True)  14.9 us
    ppermute x4, starting transfers between devices, passed_along(): return lax.ppermute(value, axis, pairs)  14.1 us
    all_to_all x1, starting transfers between devices, per_device(): lax.all_to_all(own_kv, ('y', 'xh'), split_axis=0, concat_axis=0, tiled=True)  13.1 us
    ppermute x4, waiting for transfers between devices, passed_along(): return lax.ppermute(value, axis, pairs)  8.94 us
    all_to_all x1, waiting for transfers between devices, per_device(): lax.all_to_all(summed, ('y', 'xh'), split_axis=0, concat_axis=0, tiled=True)  7.98 us
    all_to_all x1, starting transfers between devices, per_device(): lax.all_to_all(summed, ('y', 'xh'), split_axis=0, concat_axis=0, tiled=True)  4.59 us
    ppermute x2, starting transfers between devices, partner(): return lax.ppermute(value, 'c', [(0, 1), (1, 0)])  3.83 us
    ppermute x2, waiting for transfers between devices, partner(): return lax.ppermute(value, 'c', [(0, 1), (1, 0)])  3.39 us
  transfers between devices with their start and end apart: 8, of which 7 were waited for; matrix products, arithmetic and copies ran while one was open for 4% of the time, Pallas kernels for 0%

profile of v14, /device:TPU:400, one launch (start us, length us, event | category | flops | bytes accessed | tf_op | source)
XLA Modules:
  0.0 88.6 jit_solution(17899151357404375280)
XLA Ops:
  0.6 0.8 maximum_bitcast_fusion
  1.6 1.0 %broadcast_in_dim.109 = bf16[8,4,2,3200]{3,2,1,0:T(2,128)(2,1)} broadcast(bf16[8,2,3200]{2,1,0:T(2,128)(2,1)S(1)} %copy.19), dimensions={0,2,3} | broadcast | bytes 512000 | tf_op jit(solution)/shard_map/broadcast_in_dim | solution.py:78
  2.5 13.1 %all-to-all-start = ((bf16[32,2,3200]{2,1,0:T(2,128)(2,1)}), bf16[32,2,3200]{2,1,0:T(2,128)(2,1)S(1)}, u32[]{:S(2)}, u32[]{:S(2)}) async-start(bf16[32,2,3200]{2,1,0:T(2,128)(2,1)} %bitcast.4), calls=%async_computation | async-start | bytes 819200 | tf_op jit(solution)/shard_map/all_to_all | solution.py:79
  15.7 0.7 slice-done
  16.5 1.9 %collective-permute-start.1 = (bf16[2,129,128]{2,1,0:T(8,128)(2,1)S(1)}, bf16[2,129,128]{2,1,0:T(8,128)(2,1)S(1)}, u32[]{:S(2)}, u32[]{:S(2)}) collective-permute-start(bf16[2,129,128]{2,1,0:T(8,128)(2,1)S(1)} %pad_maximum_fusion.2), channel_id=1, source_target_pairs={{64,0},{128,64},{192,128},{256,192},{320,256},{384,320},{448,384},... | collective-permute-start | bytes 198152 | tf_op jit(solution)/shard_map/ppermute | solution.py:16
  18.4 14.9 %all-to-all-done = bf16[32,2,3200]{2,1,0:T(2,128)(2,1)S(1)} async-done(((bf16[32,2,3200]{2,1,0:T(2,128)(2,1)}), bf16[32,2,3200]{2,1,0:T(2,128)(2,1)S(1)}, u32[]{:S(2)}, u32[]{:S(2)}) %all-to-all-start) | async-done | bytes 409632 | tf_op jit(solution)/shard_map/all_to_all | solution.py:79
  33.3 1.9 %collective-permute-start = (bf16[2,32,3200]{2,0,1:T(2,128)(2,1)S(1)}, bf16[2,32,3200]{2,0,1:T(2,128)(2,1)S(1)}, u32[]{:S(2)}, u32[]{:S(2)}) collective-permute-start(bf16[2,32,3200]{2,0,1:T(2,128)(2,1)S(1)} %bitcast.179), channel_id=1, source_target_pairs={{0,1},{1,0},{2,3},{3,2},{4,5},{5,4},{6,7},{7,6},{8,9},{9,8},{10,11... | collective-permute-start | bytes 1228808 | tf_op jit(solution)/shard_map/ppermute | solution.py:20
  35.3 1.7 %collective-permute-done = bf16[2,32,3200]{2,0,1:T(2,128)(2,1)S(1)} collective-permute-done((bf16[2,32,3200]{2,0,1:T(2,128)(2,1)S(1)}, bf16[2,32,3200]{2,0,1:T(2,128)(2,1)S(1)}, u32[]{:S(2)}, u32[]{:S(2)}) %collective-permute-start) | collective-permute-done | bytes 409632 | tf_op jit(solution)/shard_map/ppermute | solution.py:20
  37.0 1.1 %pad_maximum_fusion = bf16[2,64,3200]{2,0,1:T(2,128)(2,1)S(1)} fusion(bf16[2,32,3200]{2,0,1:T(2,128)(2,1)S(1)} %collective-permute-done, bf16[2,32,3200]{2,0,1:T(2,128)(2,1)S(1)} %bitcast.180), kind=kLoop, calls=%fused_computation.34 | loop fusion | flops 409600 | bytes 1638400 | tf_op jit(solution)/shard_map/concatenate | solution.py:81
  38.1 0.4 reshape.180
  39.0 0.7 copy-done
  39.6 0.4 fusion.86
  40.0 0.4 fusion.87
  40.4 0.2 fusion.26
  40.6 0.3 fusion.31
  41.0 1.9 %collective-permute-start.3 = (f32[130,128]{1,0:T(8,128)S(1)}, f32[130,128]{1,0:T(8,128)S(1)}, u32[]{:S(2)}, u32[]{:S(2)}) collective-permute-start(f32[130,128]{1,0:T(8,128)S(1)} %pad_maximum_fusion.4), channel_id=1, source_target_pairs={{64,0},{128,64},{192,128},{256,192},{320,256},{384,320},{448,384},... | collective-permute-start | bytes 199688 | tf_op jit(solution)/shard_map/ppermute | solution.py:16
  43.2 0.4 fusion.88
  43.5 0.2 fusion.24
  43.8 3.4 %collective-permute-done.3 = f32[130,128]{1,0:T(8,128)S(1)} collective-permute-done((f32[130,128]{1,0:T(8,128)S(1)}, f32[130,128]{1,0:T(8,128)S(1)}, u32[]{:S(2)}, u32[]{:S(2)}) %collective-permute-start.3) | collective-permute-done | bytes 66592 | tf_op jit(solution)/shard_map/ppermute | solution.py:16
  47.2 0.4 multiply_reduce_fusion
  47.7 6.0 %collective-permute-start.2 = (f32[130,128]{1,0:T(8,128)S(1)}, f32[130,128]{1,0:T(8,128)S(1)}, u32[]{:S(2)}, u32[]{:S(2)}) collective-permute-start(f32[130,128]{1,0:T(8,128)S(1)} %pad_maximum_fusion.3), channel_id=1, source_target_pairs={{0,64},{64,128},{128,192},{192,256},{256,320},{320,384},{384,448},... | collective-permute-start | bytes 199688 | tf_op jit(solution)/shard_map/ppermute | solution.py:16
  53.7 0.4 fusion.10
  54.1 1.5 %collective-permute-done.2 = f32[130,128]{1,0:T(8,128)S(1)} collective-permute-done((f32[130,128]{1,0:T(8,128)S(1)}, f32[130,128]{1,0:T(8,128)S(1)}, u32[]{:S(2)}, u32[]{:S(2)}) %collective-permute-start.2) | collective-permute-done | bytes 66592 | tf_op jit(solution)/shard_map/ppermute | solution.py:16
  55.6 0.3 fusion.40
  55.9 0.4 multiply_reduce_fusion.2
  56.4 0.4 fusion.8
  56.7 0.3 fusion.14
  57.0 0.4 fusion.9
  57.7 0.2 fusion.12
  57.9 0.3 fusion.17
  58.2 0.2 fusion.20
  58.4 0.3 fusion.38
  58.7 1.9 %collective-permute-start.5 = (bf16[2,25,8,4,128]{4,3,2,1,0:T(4,128)(2,1)S(1)}, bf16[2,25,8,4,128]{4,3,2,1,0:T(4,128)(2,1)S(1)}, u32[]{:S(2)}, u32[]{:S(2)}) collective-permute-start(bf16[2,25,8,4,128]{4,3,2,1,0:T(4,128)(2,1)S(1)} %fusion.38), channel_id=1, source_target_pairs={{0,1},{1,0},{2,3},{3,2},{4,5},{5,4},{6,7},{7,6},{8,9},{9,8},{10,11... | collective-permute-start | bytes 1228808 | tf_op jit(solution)/shard_map/ppermute | solution.py:20
  60.7 1.7 %collective-permute-done.5 = bf16[2,25,8,4,128]{4,3,2,1,0:T(4,128)(2,1)S(1)} collective-permute-done((bf16[2,25,8,4,128]{4,3,2,1,0:T(4,128)(2,1)S(1)}, bf16[2,25,8,4,128]{4,3,2,1,0:T(4,128)(2,1)S(1)}, u32[]{:S(2)}, u32[]{:S(2)}) %collective-permute-start.5) | collective-permute-done | bytes 409632 | tf_op jit(solution)/shard_map/ppermute | solution.py:20
  62.4 0.3 fusion.35
  62.7 1.1 %copy.24 = bf16[8,4,2,25,128]{4,2,3,1,0:T(2,128)(2,1)} copy(bf16[8,4,2,25,128]{4,1,0,3,2:T(4,128)(2,1)S(1)} %fusion.35) | data formatting | bytes 819200 | tf_op jit(solution)/shard_map/transpose | solution.py:223
  63.7 4.6 %all-to-all-start.1 = ((bf16[32,2,25,128]{3,1,2,0:T(2,128)(2,1)}), bf16[32,2,25,128]{3,1,2,0:T(2,128)(2,1)S(1)}, u32[]{:S(2)}, u32[]{:S(2)}) async-start(bf16[32,2,25,128]{3,1,2,0:T(2,128)(2,1)} %bitcast.39), calls=%async_computation.1 | async-start | bytes 819200 | tf_op jit(solution)/shard_map/all_to_all | solution.py:225
  68.3 0.3 fusion.91
  68.7 4.3 %collective-permute-start.4 = (f32[128,128]{1,0:T(8,128)S(1)}, f32[128,128]{1,0:T(8,128)S(1)}, u32[]{:S(2)}, u32[]{:S(2)}) collective-permute-start(f32[128,128]{1,0:T(8,128)S(1)} %fusion.91), channel_id=1, source_target_pairs={{0,64},{64,128},{128,192},{192,256},{256,320},{320,384},{384,448},... | collective-permute-start | bytes 196616 | tf_op jit(solution)/shard_map/ppermute | solution.py:16
  73.0 0.3 fusion.90
  73.3 0.3 fusion.89
  73.6 0.6 pad_maximum_fusion.5
  74.2 4.0 %collective-permute-done.4 = f32[128,128]{1,0:T(8,128)S(1)} collective-permute-done((f32[128,128]{1,0:T(8,128)S(1)}, f32[128,128]{1,0:T(8,128)S(1)}, u32[]{:S(2)}, u32[]{:S(2)}) %collective-permute-start.4) | collective-permute-done | bytes 65568 | tf_op jit(solution)/shard_map/ppermute | solution.py:16
  78.2 0.6 fusion.46
  78.9 8.0 %all-to-all-done.1 = bf16[32,2,25,128]{3,1,2,0:T(2,128)(2,1)S(1)} async-done(((bf16[32,2,25,128]{3,1,2,0:T(2,128)(2,1)}), bf16[32,2,25,128]{3,1,2,0:T(2,128)(2,1)S(1)}, u32[]{:S(2)}, u32[]{:S(2)}) %all-to-all-start.1) | async-done | bytes 409632 | tf_op jit(solution)/shard_map/all_to_all | solution.py:225
  86.8 0.4 bitcast_reduce_fusion
  87.3 0.6 copy.27
  87.9 0.6 copy.26
  (30 shorter events, 1.2 us)
Async XLA Ops:
  2.5 13.1 %copy-start.2 = (s32[256,2]{0,1:T(2,128)S(1)}, s32[256,2]{0,1:T(2,128)}, u32[]{:S(2)}) copy-start(s32[256,2]{0,1:T(2,128)} %param.9) | copy-start | bytes 6148
  2.5 30.8 %all-to-all-start = ((bf16[32,2,3200]{2,1,0:T(2,128)(2,1)}), bf16[32,2,3200]{2,1,0:T(2,128)(2,1)S(1)}, u32[]{:S(2)}, u32[]{:S(2)}) async-start(bf16[32,2,3200]{2,1,0:T(2,128)(2,1)} %bitcast.4), calls=%async_computation | async-start | bytes 819200 | tf_op jit(solution)/shard_map/all_to_all | solution.py:79
  15.7 0.8 slice-start
  15.7 0.8 slice-start.1
  16.5 18.8 %collective-permute-start.1 = (bf16[2,129,128]{2,1,0:T(8,128)(2,1)S(1)}, bf16[2,129,128]{2,1,0:T(8,128)(2,1)S(1)}, u32[]{:S(2)}, u32[]{:S(2)}) collective-permute-start(bf16[2,129,128]{2,1,0:T(8,128)(2,1)S(1)} %pad_maximum_fusion.2), channel_id=1, source_target_pairs={{64,0},{128,64},{192,128},{256,192},{320,256},{384,320},{448,384},... | collective-permute-start | bytes 198152 | tf_op jit(solution)/shard_map/ppermute | solution.py:16
  33.3 3.6 %collective-permute-start = (bf16[2,32,3200]{2,0,1:T(2,128)(2,1)S(1)}, bf16[2,32,3200]{2,0,1:T(2,128)(2,1)S(1)}, u32[]{:S(2)}, u32[]{:S(2)}) collective-permute-start(bf16[2,32,3200]{2,0,1:T(2,128)(2,1)S(1)} %bitcast.179), channel_id=1, source_target_pairs={{0,1},{1,0},{2,3},{3,2},{4,5},{5,4},{6,7},{7,6},{8,9},{9,8},{10,11... | collective-permute-start | bytes 1228808 | tf_op jit(solution)/shard_map/ppermute | solution.py:20
  38.8 0.8 copy-start
  41.0 6.2 %collective-permute-start.3 = (f32[130,128]{1,0:T(8,128)S(1)}, f32[130,128]{1,0:T(8,128)S(1)}, u32[]{:S(2)}, u32[]{:S(2)}) collective-permute-start(f32[130,128]{1,0:T(8,128)S(1)} %pad_maximum_fusion.4), channel_id=1, source_target_pairs={{64,0},{128,64},{192,128},{256,192},{320,256},{384,320},{448,384},... | collective-permute-start | bytes 199688 | tf_op jit(solution)/shard_map/ppermute | solution.py:16
  47.7 8.0 %collective-permute-start.2 = (f32[130,128]{1,0:T(8,128)S(1)}, f32[130,128]{1,0:T(8,128)S(1)}, u32[]{:S(2)}, u32[]{:S(2)}) collective-permute-start(f32[130,128]{1,0:T(8,128)S(1)} %pad_maximum_fusion.3), channel_id=1, source_target_pairs={{0,64},{64,128},{128,192},{192,256},{256,320},{320,384},{384,448},... | collective-permute-start | bytes 199688 | tf_op jit(solution)/shard_map/ppermute | solution.py:16
  53.7 1.9 %copy-start.1 = (bf16[256,128]{1,0:T(8,128)(2,1)S(1)}, bf16[256,128]{1,0:T(8,128)(2,1)}, u32[]{:S(2)}) copy-start(bf16[256,128]{1,0:T(8,128)(2,1)} %param.8) | copy-start | bytes 196612
  58.7 3.6 %collective-permute-start.5 = (bf16[2,25,8,4,128]{4,3,2,1,0:T(4,128)(2,1)S(1)}, bf16[2,25,8,4,128]{4,3,2,1,0:T(4,128)(2,1)S(1)}, u32[]{:S(2)}, u32[]{:S(2)}) collective-permute-start(bf16[2,25,8,4,128]{4,3,2,1,0:T(4,128)(2,1)S(1)} %fusion.38), channel_id=1, source_target_pairs={{0,1},{1,0},{2,3},{3,2},{4,5},{5,4},{6,7},{7,6},{8,9},{9,8},{10,11... | collective-permute-start | bytes 1228808 | tf_op jit(solution)/shard_map/ppermute | solution.py:20
  63.7 23.1 %all-to-all-start.1 = ((bf16[32,2,25,128]{3,1,2,0:T(2,128)(2,1)}), bf16[32,2,25,128]{3,1,2,0:T(2,128)(2,1)S(1)}, u32[]{:S(2)}, u32[]{:S(2)}) async-start(bf16[32,2,25,128]{3,1,2,0:T(2,128)(2,1)} %bitcast.39), calls=%async_computation.1 | async-start | bytes 819200 | tf_op jit(solution)/shard_map/all_to_all | solution.py:225
  68.7 9.6 %collective-permute-start.4 = (f32[128,128]{1,0:T(8,128)S(1)}, f32[128,128]{1,0:T(8,128)S(1)}, u32[]{:S(2)}, u32[]{:S(2)}) collective-permute-start(f32[128,128]{1,0:T(8,128)S(1)} %fusion.91), channel_id=1, source_target_pairs={{0,64},{64,128},{128,192},{192,256},{256,320},{320,384},{384,448},... | collective-permute-start | bytes 196616 | tf_op jit(solution)/shard_map/ppermute | solution.py:16

commit v15 on v12

--- a/solution.py
+++ b/solution.py
@@ -203,7 +203,7 @@
     gq_next, gk_next, gv_next = finish_backward(
         weights_next, grad_next, delta_next, query_next, key_own, value_own
     )
-    gq_prev = passed_along(gq_next, "seq", 1)
+    gq_prev = passed_along(gq_next.astype(jnp.bfloat16), "seq", 1).astype(jnp.float32)
     grad_query = (
         gq_own + jnp.concatenate([gq_prev, jnp.zeros((rest, HD), jnp.float32)])
     ).astype(jnp.bfloat16)

time: 86.8 us -> 86.7 us (level)
  the two profiles are of different devices: /device:TPU:402 before, /device:TPU:386 now
where the time goes in v15:
time: 86.7 us; the launch traced here: 86.2 us
  starting transfers between devices  36.5 us (42%)
  waiting for transfers between devices  33.8 us (39%)
  other arithmetic  5.32 us (6%)
  matrix products  5.24 us (6%)
  local copies, waits for them, and re-layouts  4.38 us (5%)
  between operations  1.04 us (1%)
    ppermute x4, starting transfers between devices, passed_along(): return lax.ppermute(value, axis, pairs)  16.2 us
    all_to_all x1, waiting for transfers between devices, per_device(): lax.all_to_all(own_kv, ('y', 'xh'), split_axis=0, concat_axis=0, tiled=True)  14.6 us
    all_to_all x1, starting transfers between devices, per_device(): lax.all_to_all(own_kv, ('y', 'xh'), split_axis=0, concat_axis=0, tiled=True)  12 us
    all_to_all x1, waiting for transfers between devices, per_device(): lax.all_to_all(summed, ('y', 'xh'), split_axis=0, concat_axis=0, tiled=True)  8.72 us
    ppermute x4, waiting for transfers between devices, passed_along(): return lax.ppermute(value, axis, pairs)  7.08 us
    all_to_all x1, starting transfers between devices, per_device(): lax.all_to_all(summed, ('y', 'xh'), split_axis=0, concat_axis=0, tiled=True)  4.5 us
    ppermute x2, starting transfers between devices, partner(): return lax.ppermute(value, 'c', [(0, 1), (1, 0)])  3.83 us
    ppermute x2, waiting for transfers between devices, partner(): return lax.ppermute(value, 'c', [(0, 1), (1, 0)])  3.39 us
  transfers between devices with their start and end apart: 8, of which 7 were waited for; matrix products, arithmetic and copies ran while one was open for 6% of the time, Pallas kernels for 0%

profile of v15, /device:TPU:386, one launch (start us, length us, event | category | flops | bytes accessed | tf_op | source)
XLA Modules:
  0.0 86.2 jit_solution(2155606081949379505)
XLA Ops:
  0.7 0.9 maximum_bitcast_fusion
  1.6 1.0 %broadcast_in_dim.96 = bf16[8,4,2,3200]{3,2,1,0:T(2,128)(2,1)} broadcast(bf16[8,2,3200]{2,1,0:T(2,128)(2,1)S(1)} %copy.19), dimensions={0,2,3} | broadcast | bytes 512000 | tf_op jit(solution)/shard_map/broadcast_in_dim | solution.py:78
  2.6 12.0 %all-to-all-start = ((bf16[32,2,3200]{2,1,0:T(2,128)(2,1)}), bf16[32,2,3200]{2,1,0:T(2,128)(2,1)S(1)}, u32[]{:S(2)}, u32[]{:S(2)}) async-start(bf16[32,2,3200]{2,1,0:T(2,128)(2,1)} %bitcast.3), calls=%async_computation | async-start | bytes 819200 | tf_op jit(solution)/shard_map/all_to_all | solution.py:79
  14.7 3.3 %collective-permute-start.1 = (bf16[2,129,128]{2,1,0:T(8,128)(2,1)S(1)}, bf16[2,129,128]{2,1,0:T(8,128)(2,1)S(1)}, u32[]{:S(2)}, u32[]{:S(2)}) collective-permute-start(bf16[2,129,128]{2,1,0:T(8,128)(2,1)S(1)} %pad_maximum_fusion.2), channel_id=1, source_target_pairs={{64,0},{128,64},{192,128},{256,192},{320,256},{384,320},{448,384},... | collective-permute-start | bytes 198152 | tf_op jit(solution)/shard_map/ppermute | solution.py:16
  18.0 14.6 %all-to-all-done = bf16[32,2,3200]{2,1,0:T(2,128)(2,1)S(1)} async-done(((bf16[32,2,3200]{2,1,0:T(2,128)(2,1)}), bf16[32,2,3200]{2,1,0:T(2,128)(2,1)S(1)}, u32[]{:S(2)}, u32[]{:S(2)}) %all-to-all-start) | async-done | bytes 409632 | tf_op jit(solution)/shard_map/all_to_all | solution.py:79
  32.6 1.9 %collective-permute-start = (bf16[2,32,3200]{2,0,1:T(2,128)(2,1)S(1)}, bf16[2,32,3200]{2,0,1:T(2,128)(2,1)S(1)}, u32[]{:S(2)}, u32[]{:S(2)}) collective-permute-start(bf16[2,32,3200]{2,0,1:T(2,128)(2,1)S(1)} %bitcast.171), channel_id=1, source_target_pairs={{0,1},{1,0},{2,3},{3,2},{4,5},{5,4},{6,7},{7,6},{8,9},{9,8},{10,11... | collective-permute-start | bytes 1228808 | tf_op jit(solution)/shard_map/ppermute | solution.py:20
  34.6 1.7 %collective-permute-done = bf16[2,32,3200]{2,0,1:T(2,128)(2,1)S(1)} collective-permute-done((bf16[2,32,3200]{2,0,1:T(2,128)(2,1)S(1)}, bf16[2,32,3200]{2,0,1:T(2,128)(2,1)S(1)}, u32[]{:S(2)}, u32[]{:S(2)}) %collective-permute-start) | collective-permute-done | bytes 409632 | tf_op jit(solution)/shard_map/ppermute | solution.py:20
  36.3 1.1 %pad_maximum_fusion = bf16[2,64,3200]{2,0,1:T(2,128)(2,1)S(1)} fusion(bf16[2,32,3200]{2,0,1:T(2,128)(2,1)S(1)} %collective-permute-done, bf16[2,32,3200]{2,0,1:T(2,128)(2,1)S(1)} %bitcast.172), kind=kLoop, calls=%fused_computation.44 | loop fusion | flops 409600 | bytes 1638400 | tf_op jit(solution)/shard_map/concatenate | solution.py:81
  37.4 0.4 reshape.168
  37.9 0.2 copy.22
  38.3 0.4 fusion.86
  38.6 0.2 fusion.34
  38.9 0.3 fusion.36
  39.2 7.0 %collective-permute-start.2 = (f32[130,128]{1,0:T(8,128)S(1)}, f32[130,128]{1,0:T(8,128)S(1)}, u32[]{:S(2)}, u32[]{:S(2)}) collective-permute-start(f32[130,128]{1,0:T(8,128)S(1)} %pad_maximum_fusion.3), channel_id=1, source_target_pairs={{0,64},{64,128},{128,192},{192,256},{256,320},{320,384},{384,448},... | collective-permute-start | bytes 199688 | tf_op jit(solution)/shard_map/ppermute | solution.py:16
  46.2 0.4 fusion.85
  46.7 0.5 fusion.24
  47.2 0.3 fusion.22
  47.5 0.7 collective-permute-done.2
  48.2 0.3 multiply_reduce_fusion.2
  48.5 1.9 %collective-permute-start.3 = (f32[130,128]{1,0:T(8,128)S(1)}, f32[130,128]{1,0:T(8,128)S(1)}, u32[]{:S(2)}, u32[]{:S(2)}) collective-permute-start(f32[130,128]{1,0:T(8,128)S(1)} %pad_maximum_fusion.4), channel_id=1, source_target_pairs={{64,0},{128,64},{192,128},{256,192},{320,256},{384,320},{448,384},... | collective-permute-start | bytes 199688 | tf_op jit(solution)/shard_map/ppermute | solution.py:16
  50.4 0.3 fusion.44
  50.7 0.4 fusion.10
  51.1 0.2 fusion.75
  51.3 0.4 fusion.9
  51.7 0.3 fusion.15
  52.0 0.2 fusion.13
  52.2 4.9 %collective-permute-done.3 = f32[130,128]{1,0:T(8,128)S(1)} collective-permute-done((f32[130,128]{1,0:T(8,128)S(1)}, f32[130,128]{1,0:T(8,128)S(1)}, u32[]{:S(2)}, u32[]{:S(2)}) %collective-permute-start.3) | collective-permute-done | bytes 66592 | tf_op jit(solution)/shard_map/ppermute | solution.py:16
  57.1 0.2 multiply_reduce_fusion
  57.4 0.4 fusion.11
  57.8 0.3 fusion.18
  58.0 0.3 fusion.21
  58.3 0.3 fusion.41
  58.6 1.9 %collective-permute-start.5 = (bf16[2,25,8,4,128]{4,3,2,1,0:T(4,128)(2,1)S(1)}, bf16[2,25,8,4,128]{4,3,2,1,0:T(4,128)(2,1)S(1)}, u32[]{:S(2)}, u32[]{:S(2)}) collective-permute-start(bf16[2,25,8,4,128]{4,3,2,1,0:T(4,128)(2,1)S(1)} %fusion.41), channel_id=1, source_target_pairs={{0,1},{1,0},{2,3},{3,2},{4,5},{5,4},{6,7},{7,6},{8,9},{9,8},{10,11... | collective-permute-start | bytes 1228808 | tf_op jit(solution)/shard_map/ppermute | solution.py:20
  60.5 1.7 %collective-permute-done.5 = bf16[2,25,8,4,128]{4,3,2,1,0:T(4,128)(2,1)S(1)} collective-permute-done((bf16[2,25,8,4,128]{4,3,2,1,0:T(4,128)(2,1)S(1)}, bf16[2,25,8,4,128]{4,3,2,1,0:T(4,128)(2,1)S(1)}, u32[]{:S(2)}, u32[]{:S(2)}) %collective-permute-start.5) | collective-permute-done | bytes 409632 | tf_op jit(solution)/shard_map/ppermute | solution.py:20
  62.2 0.3 fusion.38
  62.5 1.1 %copy.24 = bf16[8,4,2,25,128]{4,2,3,1,0:T(2,128)(2,1)} copy(bf16[8,4,2,25,128]{4,1,0,3,2:T(4,128)(2,1)S(1)} %fusion.38) | data formatting | bytes 819200 | tf_op jit(solution)/shard_map/transpose | solution.py:219
  63.6 4.5 %all-to-all-start.1 = ((bf16[32,2,25,128]{3,1,2,0:T(2,128)(2,1)}), bf16[32,2,25,128]{3,1,2,0:T(2,128)(2,1)S(1)}, u32[]{:S(2)}, u32[]{:S(2)}) async-start(bf16[32,2,25,128]{3,1,2,0:T(2,128)(2,1)} %bitcast.34), calls=%async_computation.1 | async-start | bytes 819200 | tf_op jit(solution)/shard_map/all_to_all | solution.py:221
  68.1 0.3 fusion.87
  68.4 0.3 fusion.88
  68.8 0.3 convolution_convert_fusion.2
  69.1 3.9 %collective-permute-start.4 = (bf16[128,128]{1,0:T(8,128)(2,1)S(1)}, bf16[128,128]{1,0:T(8,128)(2,1)S(1)}, u32[]{:S(2)}, u32[]{:S(2)}) collective-permute-start(bf16[128,128]{1,0:T(8,128)(2,1)S(1)} %convolution_convert_fusion.2), channel_id=1, source_target_pairs={{0,64},{64,128},{128,192},{192,256},{256,320},{320,384},{384,448},... | collective-permute-start | bytes 98312 | tf_op jit(solution)/shard_map/ppermute | solution.py:16
  73.0 0.6 pad_maximum_fusion.5
  73.7 1.5 %collective-permute-done.4 = bf16[128,128]{1,0:T(8,128)(2,1)S(1)} collective-permute-done((bf16[128,128]{1,0:T(8,128)(2,1)S(1)}, bf16[128,128]{1,0:T(8,128)(2,1)S(1)}, u32[]{:S(2)}, u32[]{:S(2)}) %collective-permute-start.4) | collective-permute-done | bytes 32800 | tf_op jit(solution)/shard_map/ppermute | solution.py:16
  75.1 0.6 fusion.49
  75.8 8.7 %all-to-all-done.1 = bf16[32,2,25,128]{3,1,2,0:T(2,128)(2,1)S(1)} async-done(((bf16[32,2,25,128]{3,1,2,0:T(2,128)(2,1)}), bf16[32,2,25,128]{3,1,2,0:T(2,128)(2,1)S(1)}, u32[]{:S(2)}, u32[]{:S(2)}) %all-to-all-start.1) | async-done | bytes 409632 | tf_op jit(solution)/shard_map/all_to_all | solution.py:221
  84.5 0.4 bitcast_reduce_fusion
  85.0 0.6 copy.27
  85.6 0.6 copy.26
  (29 shorter events, 0.6 us)
Async XLA Ops:
  0.6 13.9 %copy-start.2 = (s32[256,2]{0,1:T(2,128)S(1)}, s32[256,2]{0,1:T(2,128)}, u32[]{:S(2)}) copy-start(s32[256,2]{0,1:T(2,128)} %param.9) | copy-start | bytes 6148
  0.6 14.0 %slice-start = ((bf16[256,128]{1,0:T(8,128)(2,1)}), bf16[128,128]{1,0:T(8,128)(2,1)S(1)}, s32[]{:S(2)}) async-start(bf16[256,128]{1,0:T(8,128)(2,1)} %param.5), calls=%async_computation.2 | async-start | bytes 65536 | tf_op jit(solution)/shard_map/slice | solution.py:66
  0.7 14.0 %slice-start.1 = ((bf16[256,128]{1,0:T(8,128)(2,1)}), bf16[128,128]{1,0:T(8,128)(2,1)S(1)}, s32[]{:S(2)}) async-start(bf16[256,128]{1,0:T(8,128)(2,1)} %param.8), calls=%async_computation.3 | async-start | bytes 65536 | tf_op jit(solution)/shard_map/slice | solution.py:67
  2.6 30.1 %all-to-all-start = ((bf16[32,2,3200]{2,1,0:T(2,128)(2,1)}), bf16[32,2,3200]{2,1,0:T(2,128)(2,1)S(1)}, u32[]{:S(2)}, u32[]{:S(2)}) async-start(bf16[32,2,3200]{2,1,0:T(2,128)(2,1)} %bitcast.3), calls=%async_computation | async-start | bytes 819200 | tf_op jit(solution)/shard_map/all_to_all | solution.py:79
  14.7 19.9 %collective-permute-start.1 = (bf16[2,129,128]{2,1,0:T(8,128)(2,1)S(1)}, bf16[2,129,128]{2,1,0:T(8,128)(2,1)S(1)}, u32[]{:S(2)}, u32[]{:S(2)}) collective-permute-start(bf16[2,129,128]{2,1,0:T(8,128)(2,1)S(1)} %pad_maximum_fusion.2), channel_id=1, source_target_pairs={{64,0},{128,64},{192,128},{256,192},{320,256},{384,320},{448,384},... | collective-permute-start | bytes 198152 | tf_op jit(solution)/shard_map/ppermute | solution.py:16
  32.6 3.6 %collective-permute-start = (bf16[2,32,3200]{2,0,1:T(2,128)(2,1)S(1)}, bf16[2,32,3200]{2,0,1:T(2,128)(2,1)S(1)}, u32[]{:S(2)}, u32[]{:S(2)}) collective-permute-start(bf16[2,32,3200]{2,0,1:T(2,128)(2,1)S(1)} %bitcast.171), channel_id=1, source_target_pairs={{0,1},{1,0},{2,3},{3,2},{4,5},{5,4},{6,7},{7,6},{8,9},{9,8},{10,11... | collective-permute-start | bytes 1228808 | tf_op jit(solution)/shard_map/ppermute | solution.py:20
  38.3 8.0 %copy-start = (bf16[256,128]{1,0:T(8,128)(2,1)S(1)}, bf16[256,128]{1,0:T(8,128)(2,1)}, u32[]{:S(2)}) copy-start(bf16[256,128]{1,0:T(8,128)(2,1)} %param.5) | copy-start | bytes 196612
  39.2 8.9 %collective-permute-start.2 = (f32[130,128]{1,0:T(8,128)S(1)}, f32[130,128]{1,0:T(8,128)S(1)}, u32[]{:S(2)}, u32[]{:S(2)}) collective-permute-start(f32[130,128]{1,0:T(8,128)S(1)} %pad_maximum_fusion.3), channel_id=1, source_target_pairs={{0,64},{64,128},{128,192},{192,256},{256,320},{320,384},{384,448},... | collective-permute-start | bytes 199688 | tf_op jit(solution)/shard_map/ppermute | solution.py:16
  46.7 1.5 %copy-start.1 = (bf16[256,128]{1,0:T(8,128)(2,1)S(1)}, bf16[256,128]{1,0:T(8,128)(2,1)}, u32[]{:S(2)}) copy-start(bf16[256,128]{1,0:T(8,128)(2,1)} %param.8) | copy-start | bytes 196612
  48.5 8.7 %collective-permute-start.3 = (f32[130,128]{1,0:T(8,128)S(1)}, f32[130,128]{1,0:T(8,128)S(1)}, u32[]{:S(2)}, u32[]{:S(2)}) collective-permute-start(f32[130,128]{1,0:T(8,128)S(1)} %pad_maximum_fusion.4), channel_id=1, source_target_pairs={{64,0},{128,64},{192,128},{256,192},{320,256},{384,320},{448,384},... | collective-permute-start | bytes 199688 | tf_op jit(solution)/shard_map/ppermute | solution.py:16
  58.6 3.6 %collective-permute-start.5 = (bf16[2,25,8,4,128]{4,3,2,1,0:T(4,128)(2,1)S(1)}, bf16[2,25,8,4,128]{4,3,2,1,0:T(4,128)(2,1)S(1)}, u32[]{:S(2)}, u32[]{:S(2)}) collective-permute-start(bf16[2,25,8,4,128]{4,3,2,1,0:T(4,128)(2,1)S(1)} %fusion.41), channel_id=1, source_target_pairs={{0,1},{1,0},{2,3},{3,2},{4,5},{5,4},{6,7},{7,6},{8,9},{9,8},{10,11... | collective-permute-start | bytes 1228808 | tf_op jit(solution)/shard_map/ppermute | solution.py:20
  63.6 20.9 %all-to-all-start.1 = ((bf16[32,2,25,128]{3,1,2,0:T(2,128)(2,1)}), bf16[32,2,25,128]{3,1,2,0:T(2,128)(2,1)S(1)}, u32[]{:S(2)}, u32[]{:S(2)}) async-start(bf16[32,2,25,128]{3,1,2,0:T(2,128)(2,1)} %bitcast.34), calls=%async_computation.1 | async-start | bytes 819200 | tf_op jit(solution)/shard_map/all_to_all | solution.py:221
  69.1 6.1 %collective-permute-start.4 = (bf16[128,128]{1,0:T(8,128)(2,1)S(1)}, bf16[128,128]{1,0:T(8,128)(2,1)S(1)}, u32[]{:S(2)}, u32[]{:S(2)}) collective-permute-start(bf16[128,128]{1,0:T(8,128)(2,1)S(1)} %convolution_convert_fusion.2), channel_id=1, source_target_pairs={{0,64},{64,128},{128,192},{192,256},{256,320},{320,384},{384,448},... | collective-permute-start | bytes 98312 | tf_op jit(solution)/shard_map/ppermute | solution.py:16
